TPU v7x, 32 devices: a whole 2x2x4 slice. The times are simulated.
32 devices in a mesh: dp: 16 (over z, y, x), lat: 2 (over core).
Axes of the slice: x: 2, y: 2, z: 4, core: 2. Of those that a mesh axis runs over, the one named last changes fastest.
Arguments:
- acts: bfloat16 [2048, 8192], P('dp', 'lat'), may hold values from -6 to 6
- owner_ids: int32 [2048, 4], P('dp'), may hold values from 0 to 31, all different within a row; in each aligned block of 128 rows (0 to 127, 128 to 255, ...) at most 32 rows name the same one
- block_codes: int32 [2048, 4], P('dp'), may hold values from 1 to 3
- weights: bfloat16 [4096, 8192], P(('dp', 'lat')), may hold values from -0.25 to 0.25
- enc_bias: float32 [4096], P(('dp', 'lat')), may hold values from -3 to 3
- dec_bias: float32 [8192], P('lat'), may hold values from -3 to 3
Outputs:
- recon: bfloat16 [2048, 8192], P('dp', 'lat')
- grad_weights: bfloat16 [4096, 8192], P(('dp', 'lat'))
- grad_enc_bias: float32 [4096], P(('dp', 'lat'))
- grad_dec_bias: float32 [8192], P('lat')
Inputs may be any that keep to these rules, and one draw needn't show every extreme that they name: `owner_ids`: each row names 4 different devices; in each aligned block of 128 rows (the rows of one index of dp) no device is named by more than 32 rows, and some device is named by exactly 32. `block_codes`: bit j (j < 2) of an entry says whether block j of that device's 2 blocks is active for the token.
All inputs are finite; a program needn't handle non-finite values.
Results may differ from a plain program's by a relative error of at most 0.0056.
Values may be sent and summed in bfloat16 or wider, within the bound.
No kernel may reach another device: no remote copies, remote signals or barrier semaphores. Data moves between devices by JAX's collectives and lax.ppermute only.
A program may use at most 192 MiB of HBM per device.

v0:
```python
import jax
import jax.numpy as jnp
from jax import lax
from jax.sharding import PartitionSpec as P

BLK_DEV = 2


def owner_work(rows, gate, weights, enc_bias, block_width):
    pre = (
        lax.dot_general(rows, weights, (((1,), (1,)), ((), ())), preferred_element_type=jnp.float32)
        + enc_bias[None, :]
    )
    gate_lat = jnp.repeat(gate.astype(jnp.float32), block_width, axis=1)
    codes = (jnp.maximum(pre, 0.0) * gate_lat).astype(jnp.bfloat16)
    parts = jnp.dot(codes, weights, preferred_element_type=jnp.float32).astype(jnp.bfloat16)
    return (pre, gate_lat, codes, parts)


def owner_grads(rows, errors, weights, pre, gate_lat, codes):
    gcodes = lax.dot_general(
        errors, weights, (((1,), (1,)), ((), ())), preferred_element_type=jnp.float32
    )
    gpre = gcodes * gate_lat * (pre > 0.0).astype(jnp.float32)
    grad_w = lax.dot_general(
        codes, errors, (((0,), (0,)), ((), ())), preferred_element_type=jnp.float32
    )
    grad_w = grad_w + lax.dot_general(
        gpre.astype(jnp.bfloat16),
        rows,
        (((0,), (0,)), ((), ())),
        preferred_element_type=jnp.float32,
    )
    return (grad_w.astype(jnp.bfloat16), jnp.sum(gpre, axis=0))


def slot_tables(owner_ids, block_codes, owner_total, slot_cap, blk_count):
    tok_rows, own_count = owner_ids.shape
    onehot = (
        owner_ids[:, :, None] == jnp.arange(owner_total, dtype=jnp.int32)[None, None, :]
    ).astype(jnp.float32)
    present = jnp.sum(onehot, axis=1)
    lower = (jnp.arange(tok_rows)[None, :] < jnp.arange(tok_rows)[:, None]).astype(jnp.float32)
    before = jnp.dot(lower, present, precision=lax.Precision.HIGHEST)
    slot_of = jnp.sum(onehot * before[:, None, :], axis=2)
    slot_hit = (
        slot_of[:, :, None] == jnp.arange(slot_cap, dtype=jnp.float32)[None, None, :]
    ).astype(jnp.float32)
    select = (onehot[:, :, :, None] * slot_hit[:, :, None, :]).reshape(
        tok_rows, own_count, owner_total * slot_cap
    )
    place = jnp.sum(select, axis=1)
    bits = jnp.stack([block_codes // 2**j % 2 for j in range(blk_count)], axis=-1).astype(
        jnp.float32
    )
    gates = jnp.einsum("tks,tkj->sj", select, bits)
    return (place, gates)


def local(acts, owner_ids, block_codes, weights, enc_bias, dec_bias):
    dp_count = lax.axis_size("dp")
    lat_count = lax.axis_size("lat")
    owner_total = dp_count * lat_count
    tok_rows, own_count = owner_ids.shape
    full_width = weights.shape[1]
    blk_count = BLK_DEV
    block_width = weights.shape[0] // blk_count
    slot_cap = max(2, 2 * tok_rows * own_count // owner_total)
    place, gates = slot_tables(owner_ids, block_codes, owner_total, slot_cap, blk_count)
    lat_hit = (jnp.arange(lat_count, dtype=jnp.int32) == lax.axis_index("lat")).astype(jnp.float32)
    mine = jnp.einsum(
        "tdlc,l->tdc", place.reshape(tok_rows, dp_count, lat_count, slot_cap), lat_hit
    )
    mine_b = mine.reshape(tok_rows, dp_count * slot_cap).astype(jnp.bfloat16)
    mine_gate = jnp.einsum(
        "dlcj,l->dcj", gates.reshape(dp_count, lat_count, slot_cap, blk_count), lat_hit
    )
    whole = lax.all_gather(acts, "lat", axis=1, tiled=True)
    sent = lax.dot_general(
        mine_b, whole, (((0,), (0,)), ((), ())), preferred_element_type=jnp.float32
    )
    sent = sent.astype(jnp.bfloat16).reshape(dp_count, slot_cap, full_width)
    got_rows, got_gate = (
        lax.all_to_all(sent, "dp", split_axis=0, concat_axis=0, tiled=True),
        lax.all_to_all(
            mine_gate.astype(jnp.bfloat16), "dp", split_axis=0, concat_axis=0, tiled=True
        ),
    )
    rows = got_rows.reshape(dp_count * slot_cap, full_width)
    gate = got_gate.reshape(dp_count * slot_cap, blk_count)
    pre, gate_lat, codes, parts = owner_work(rows, gate, weights, enc_bias, block_width)
    back = lax.all_to_all(
        parts.reshape(dp_count, slot_cap, full_width), "dp", split_axis=0, concat_axis=0, tiled=True
    )
    partial_value = jnp.dot(
        mine_b, back.reshape(dp_count * slot_cap, full_width), preferred_element_type=jnp.float32
    )
    summed = lax.psum_scatter(partial_value, "lat", scatter_dimension=1, tiled=True)
    full = dec_bias[None, :] + summed
    err = full - acts.astype(jnp.float32)
    gerr = err.astype(jnp.bfloat16)
    err_whole = lax.all_gather(gerr, "lat", axis=1, tiled=True)
    err_sent = lax.dot_general(
        mine_b, err_whole, (((0,), (0,)), ((), ())), preferred_element_type=jnp.float32
    )
    err_sent = err_sent.astype(jnp.bfloat16).reshape(dp_count, slot_cap, full_width)
    got_err = lax.all_to_all(err_sent, "dp", split_axis=0, concat_axis=0, tiled=True)
    errors = got_err.reshape(dp_count * slot_cap, full_width)
    recon = full.astype(jnp.bfloat16)
    grad_weights, grad_enc_bias = owner_grads(rows, errors, weights, pre, gate_lat, codes)
    grad_dec_bias = lax.psum(jnp.sum(err, axis=0), "dp")
    return (recon, grad_weights, grad_enc_bias, grad_dec_bias)


def solution(mesh):
    in_specs = (
        P("dp", "lat"),
        P("dp", None),
        P("dp", None),
        P(("dp", "lat"), None),
        P(("dp", "lat")),
        P("lat"),
    )
    out_specs = (P("dp", "lat"), P(("dp", "lat"), None), P(("dp", "lat")), P("lat"))
    return jax.shard_map(local, mesh=mesh, in_specs=in_specs, out_specs=out_specs, check_vma=False)
```

profile of v0, /device:TPU:0, one launch (start us, length us, event | category | flops | bytes accessed | tf_op | source)
XLA Modules:
  0.0 737.8 jit_solution(16515403187644802783)
XLA Ops:
  7.2 0.0 copy-start
  7.2 0.0 all-gather.3.cloned.1.call-start
  7.2 0.7 all-gather.3.cloned.1.call-update
  7.9 0.7 fusion.37
  8.6 0.7 add_select_fusion.2
  9.3 0.1 fusion.19
  9.4 0.8 fusion.16
  10.2 0.7 fusion.12
  10.9 0.2 broadcast_multiply_fusion
  11.1 0.8 fusion.6
  11.9 0.2 fusion.35
  12.1 0.6 convert_element_type.64
  12.7 8.3 %all-to-all-start.1 = ((bf16[16,32,2]{1,2,0:T(2,128)(2,1)}), bf16[16,32,2]{1,2,0:T(2,128)(2,1)S(1)}, u32[]{:S(2)}, u32[]{:S(2)}) async-start(bf16[16,32,2]{1,2,0:T(2,128)(2,1)} %convert_element_type.64), calls=%async_computation.1 | async-start | bytes 16384 | tf_op jit(solution)/shard_map/all_to_all | solution.py:85
  21.0 0.2 fusion.9
  21.2 0.2 copy.34
  21.4 0.4 fusion.45
  21.8 0.0 copy-start.2
  21.8 1.1 all-gather.3.cloned.1.call-done
  22.9 7.2 convolution_convert_fusion.2
  30.1 0.0 all-to-all-done.1
  30.1 0.0 copy-start.4
  30.1 7.0 all-to-all-start
  37.0 0.0 reduce-scatter.2.cloned.1.call-start
  37.1 0.1 reshape.66
  37.2 0.1 copy.32
  37.3 158.9 %all-to-all-done = bf16[16,32,8192]{2,1,0:T(8,128)(2,1)} async-done(((bf16[16,32,8192]{2,1,0:T(8,128)(2,1)}), bf16[16,32,8192]{2,1,0:T(8,128)(2,1)}, u32[]{:S(2)}, u32[]{:S(2)}) %all-to-all-start) | async-done | bytes 8388640 | tf_op jit(solution)/shard_map/all_to_all | solution.py:84
  196.3 0.0 copy-done
  196.3 0.0 copy-done.4
  196.3 6.5 multiply_convert_fusion
  202.7 2.3 convolution_convert_fusion.1
  205.1 220.9 %all_to_all.20 = bf16[16,32,8192]{2,1,0:T(8,128)(2,1)S(1)} all-to-all(bf16[16,32,8192]{2,1,0:T(8,128)(2,1)S(1)} %bitcast.62), channel_id=1, replica_groups=mesh['dp'=16,'lat'=2] {'dp'}, dimensions={0} | all-to-all | bytes 16777216 | tf_op jit(solution)/shard_map/all_to_all | solution.py:92
  426.0 0.0 copy-done.2
  426.0 3.2 fusion.63
  429.2 0.0 reduce-scatter.2.cloned.1.call-update
  429.2 0.2 all-gather.5.cloned.1.call-start
  429.5 10.7 %reduce-scatter.2.cloned.1.call-done = f32[128,4096]{1,0:T(8,128)} async-done(((f32[128,8192]{1,0:T(8,128)}), f32[128,4096]{1,0:T(8,128)}) %reduce-scatter.2.cloned.1.call-update) | async-done | bytes 2097168 | tf_op jit(solution)/shard_map/reduce_scatter | solution.py:98
  440.1 0.0 copy-done.1
  440.2 3.3 fusion.3
  443.5 0.0 all-gather.5.cloned.1.call-update
  443.5 12.0 %all-gather.5.cloned.1.call-done = bf16[128,8192]{1,0:T(8,128)(2,1)} async-done(((bf16[128,4096]{1,0:T(8,128)(2,1)}), bf16[128,8192]{1,0:T(8,128)(2,1)}) %all-gather.5.cloned.1.call-update) | async-done | bytes 2097168 | tf_op jit(solution)/shard_map/all_gather | solution.py:102
  455.5 7.3 convolution_convert_fusion
  462.8 6.8 all-to-all-start.3
  469.7 244.3 %psum.7 = f32[4096]{0:T(1024)} all-reduce(f32[4096]{0:T(1024)S(1)} %get-tuple-element.4), channel_id=1, replica_groups=mesh['dp'=16,'lat'=2] {'dp'}, use_global_device_ids=true, to_apply=%region_6.7 | all-reduce | flops 4096 | bytes 32768 | tf_op jit(solution)/shard_map/psum | solution.py:111
  713.9 0.0 all-to-all-done.3
  713.9 4.8 fusion.65
  718.8 0.0 copy-done.3
  718.8 6.2 fusion.64
  725.0 6.3 fusion
  (5 shorter events, 0.0 us)
Async XLA Ops:
  7.2 189.1 %copy-start = (bf16[128,8192]{1,0:T(8,128)(2,1)S(1)}, bf16[128,8192]{1,0:T(8,128)(2,1)}, u32[]{:S(2)}) copy-start(bf16[128,8192]{1,0:T(8,128)(2,1)} %param.9) | copy-start | bytes 6291460
  7.2 15.7 %all-gather.3.cloned.1.call-start = ((), (), s32[]{:S(2)}) async-start(), calls=%async_computation.5 | async-start | bytes 3145728 | tf_op jit(solution)/shard_map/all_gather | solution.py:78
  12.7 17.4 %all-to-all-start.1 = ((bf16[16,32,2]{1,2,0:T(2,128)(2,1)}), bf16[16,32,2]{1,2,0:T(2,128)(2,1)S(1)}, u32[]{:S(2)}, u32[]{:S(2)}) async-start(bf16[16,32,2]{1,2,0:T(2,128)(2,1)} %convert_element_type.64), calls=%async_computation.1 | async-start | bytes 16384 | tf_op jit(solution)/shard_map/all_to_all | solution.py:85
  21.8 404.2 %copy-start.2 = (bf16[1,128,512]{2,0,1:T(2,128)(2,1)}, bf16[1,128,512]{2,0,1:T(2,128)(2,1)S(1)}, u32[]{:S(2)}) copy-start(bf16[1,128,512]{2,0,1:T(2,128)(2,1)S(1)} %fusion.45) | copy-start | bytes 393220
  30.1 166.2 %copy-start.4 = (f32[128]{0:T(128)S(1)}, f32[128]{0:T(128)}, u32[]{:S(2)}) copy-start(f32[128]{0:T(128)} %param.10) | copy-start | bytes 1540
  30.1 166.2 %all-to-all-start = ((bf16[16,32,8192]{2,1,0:T(8,128)(2,1)}), bf16[16,32,8192]{2,1,0:T(8,128)(2,1)}, u32[]{:S(2)}, u32[]{:S(2)}) async-start(bf16[16,32,8192]{2,1,0:T(8,128)(2,1)} %bitcast.59), calls=%async_computation | async-start | bytes 16777216 | tf_op jit(solution)/shard_map/all_to_all | solution.py:84
  37.0 403.1 %reduce-scatter.2.cloned.1.call-start = ((), (), s32[]{:S(2)}) async-start(), calls=%async_computation.6 | async-start | bytes 6291456 | tf_op jit(solution)/shard_map/reduce_scatter | solution.py:98
  429.2 10.9 %copy-start.1 = (bf16[128,4096]{1,0:T(8,128)(2,1)S(1)}, bf16[128,4096]{1,0:T(8,128)(2,1)}, u32[]{:S(2)}) copy-start(bf16[128,4096]{1,0:T(8,128)(2,1)} %param.6) | copy-start | bytes 3145732
  429.2 26.3 %all-gather.5.cloned.1.call-start = ((), (), s32[]{:S(2)}) async-start(), calls=%async_computation.7 | async-start | bytes 3145728 | tf_op jit(solution)/shard_map/all_gather | solution.py:102
  462.8 251.1 %all-to-all-start.3 = ((bf16[16,32,8192]{2,1,0:T(8,128)(2,1)}), bf16[16,32,8192]{2,1,0:T(8,128)(2,1)}, u32[]{:S(2)}, u32[]{:S(2)}) async-start(bf16[16,32,8192]{2,1,0:T(8,128)(2,1)} %bitcast.60), calls=%async_computation.4 | async-start | bytes 16777216 | tf_op jit(solution)/shard_map/all_to_all | solution.py:107
  713.9 4.8 copy-start.3
Sparse Core Ops, SparseCore 0:
  9.6 13.2 all-gather.2
  429.4 10.7 reduce-scatter.1
  443.6 11.8 all-gather.4
where the time goes:
time: 739 us; the launch traced here: 738 us
  blocking collectives  465 us (63%)
  waiting for transfers between devices  183 us (25%)
  matrix products  45.3 us (6%)
  starting transfers between devices  22.4 us (3%)
  between operations  13.9 us (2%)
    psum x1, blocking collectives, local(): grad_dec_bias = lax.psum(jnp.sum(err, axis=0), 'dp')  244 us
    all_to_all x1, blocking collectives, local(): lax.all_to_all(parts.reshape(dp_count, slot_cap, full_width), 'dp', split...  221 us
    all_to_all x1, waiting for transfers between devices, local(): lax.all_to_all(sent, 'dp', split_axis=0, concat_axis=0, tiled=True)  159 us
  transfers between devices with their start and end apart: 6, of which 4 were waited for; matrix products, arithmetic and copies ran while one was open for 2% of the time, Pallas kernels for 0%

commit v1 on v0

v1 whole, which is shorter than its diff:
```python
import jax
import jax.numpy as jnp
from jax import lax
from jax.sharding import PartitionSpec as P

BLK_DEV = 2
ALL = ("dp", "lat")


def slot_tables(ids, owner_total, block_rows, slot_cap):
    tokens, own_count = ids.shape
    blocks = tokens // block_rows
    per_owner = blocks * slot_cap
    onehot = (ids[:, :, None] == jnp.arange(owner_total, dtype=jnp.int32)[None, None, :]).astype(
        jnp.int32
    )
    present = jnp.sum(onehot, axis=1).reshape(blocks, block_rows, owner_total)
    before = (jnp.cumsum(present, axis=1) - present).reshape(tokens, owner_total)
    rank = jnp.take_along_axis(before, ids, axis=1)
    block = (jnp.arange(tokens, dtype=jnp.int32) // block_rows)[:, None]
    slot = ids * per_owner + block * slot_cap + rank
    slot_flat = slot.reshape(-1)
    pair_index = jnp.arange(tokens * own_count, dtype=jnp.int32)
    total = owner_total * per_owner
    pair_at = jnp.zeros((total,), jnp.int32).at[slot_flat].set(pair_index, unique_indices=True)
    valid = jnp.zeros((total,), jnp.bool_).at[slot_flat].set(True, unique_indices=True)
    return slot_flat, pair_at, valid, per_owner


def local(acts, owner_ids, block_codes, weights, enc_bias, dec_bias):
    dp_count = lax.axis_size("dp")
    lat_count = lax.axis_size("lat")
    dp_idx = lax.axis_index("dp")
    lat_idx = lax.axis_index("lat")
    owner_total = dp_count * lat_count
    tok_rows, own_count = owner_ids.shape
    half = acts.shape[1]
    full_width = weights.shape[1]
    lat_own = weights.shape[0]
    block_width = lat_own // BLK_DEV
    fs = half // dp_count
    mine_rows = tok_rows // lat_count
    tokens = tok_rows * dp_count
    slot_cap = max(2, 2 * tok_rows * own_count // owner_total)

    acts_fs = lax.all_to_all(
        acts.reshape(tok_rows, dp_count, fs).transpose(1, 0, 2), "dp", 0, 0, tiled=True
    ).reshape(tokens, fs)
    w_send = (
        weights.reshape(lat_own, lat_count, dp_count, fs)
        .transpose(2, 1, 0, 3)
        .reshape(owner_total, lat_own, fs)
    )
    w_fs = lax.all_to_all(w_send, ALL, 0, 0, tiled=True)

    ids_all = lax.all_gather(owner_ids, "dp", axis=0, tiled=True)
    slot_flat, pair_at, valid, per_owner = slot_tables(ids_all, owner_total, tok_rows, slot_cap)
    tok_at = pair_at // own_count
    valid_col = valid[:, None]

    def to_slots(x_fs):
        return jnp.where(valid_col, jnp.take(x_fs, tok_at, axis=0, mode="clip"), 0).reshape(
            owner_total, per_owner, fs
        )

    def slots_to_pairs(v):
        return jnp.take(v.reshape(owner_total * per_owner, -1), slot_flat, axis=0, mode="clip").reshape(
            tokens, own_count, -1
        )

    def pairs_to_slots(x):
        flat = x.reshape(tokens * own_count, -1)
        return jnp.where(valid_col, jnp.take(flat, pair_at, axis=0, mode="clip"), 0).reshape(
            owner_total, per_owner, -1
        )

    acts_slots = to_slots(acts_fs)
    pre_part = jnp.einsum("ocf,olf->ocl", acts_slots, w_fs, preferred_element_type=jnp.float32)
    pre_sum = lax.psum_scatter(slots_to_pairs(pre_part), ALL, scatter_dimension=0, tiled=True)

    start = lat_idx * mine_rows
    my_ids = lax.dynamic_slice_in_dim(owner_ids, start, mine_rows, 0)
    my_codes = lax.dynamic_slice_in_dim(block_codes, start, mine_rows, 0)
    enc_all = lax.all_gather(enc_bias, ALL, axis=0, tiled=True).reshape(owner_total, lat_own)
    pre = pre_sum + jnp.take(enc_all, my_ids, axis=0, mode="clip")
    lat_block = jnp.arange(lat_own, dtype=jnp.int32) // block_width
    gate = ((my_codes[:, :, None] // (2 ** lat_block)[None, None, :]) % 2).astype(jnp.float32)
    codes = (jnp.maximum(pre, 0.0) * gate).astype(jnp.bfloat16)

    codes_all = lax.all_gather(codes, ALL, axis=0, tiled=True)
    codes_slots = pairs_to_slots(codes_all)
    contrib = jnp.einsum("ocl,olf->ocf", codes_slots, w_fs, preferred_element_type=jnp.float32)
    summed = jnp.sum(slots_to_pairs(contrib), axis=1)
    bias_fs = lax.dynamic_slice_in_dim(dec_bias, dp_idx * fs, fs, 0)
    full = summed + bias_fs[None, :]
    err = full - acts_fs.astype(jnp.float32)
    gerr = err.astype(jnp.bfloat16)
    recon_fs = full.astype(jnp.bfloat16)
    recon = (
        lax.all_to_all(recon_fs.reshape(dp_count, tok_rows, fs), "dp", 0, 0, tiled=True)
        .transpose(1, 0, 2)
        .reshape(tok_rows, half)
    )
    grad_dec_bias = lax.all_gather(jnp.sum(err, axis=0), "dp", axis=0, tiled=True)

    gerr_slots = to_slots(gerr)
    gc_part = jnp.einsum("ocf,olf->ocl", gerr_slots, w_fs, preferred_element_type=jnp.float32)
    gcodes = lax.psum_scatter(slots_to_pairs(gc_part), ALL, scatter_dimension=0, tiled=True)
    gpre = gcodes * gate * (pre > 0.0).astype(jnp.float32)
    own_hit = (
        my_ids[:, :, None] == jnp.arange(owner_total, dtype=jnp.int32)[None, None, :]
    ).astype(jnp.float32)
    genc_part = jnp.sum(own_hit[:, :, :, None] * gpre[:, :, None, :], axis=(0, 1))
    grad_enc_bias = lax.psum_scatter(genc_part.reshape(-1), ALL, scatter_dimension=0, tiled=True)

    gpre_all = lax.all_gather(gpre.astype(jnp.bfloat16), ALL, axis=0, tiled=True)
    gpre_slots = pairs_to_slots(gpre_all)
    gw = jnp.einsum("ocl,ocf->olf", codes_slots, gerr_slots, preferred_element_type=jnp.float32)
    gw = gw + jnp.einsum(
        "ocl,ocf->olf", gpre_slots, acts_slots, preferred_element_type=jnp.float32
    )
    gw_back = lax.all_to_all(gw.astype(jnp.bfloat16), ALL, 0, 0, tiled=True)
    grad_weights = (
        gw_back.reshape(dp_count, lat_count, lat_own, fs)
        .transpose(2, 1, 0, 3)
        .reshape(lat_own, full_width)
    )
    return (recon, grad_weights, grad_enc_bias, grad_dec_bias)


def solution(mesh):
    in_specs = (
        P("dp", "lat"),
        P("dp", None),
        P("dp", None),
        P(("dp", "lat"), None),
        P(("dp", "lat")),
        P("lat"),
    )
    out_specs = (P("dp", "lat"), P(("dp", "lat"), None), P(("dp", "lat")), P("lat"))
    return jax.shard_map(local, mesh=mesh, in_specs=in_specs, out_specs=out_specs, check_vma=False)
```

time: 739 us -> 1200 us (1.62)
  local copies, waits for them, and re-layouts: 0.46 us -> 523 us
  blocking collectives: 465 us -> 212 us
  waiting for transfers between devices: 183 us -> 347 us
  other arithmetic: 7.18 us -> 32.1 us
    gather x0 -> x13, local copies, waits for them, and re-layouts: none -> 426 us  [the longest x2 130 us: to_slots(): jnp.take(x_fs, tok_at, axis=0, mode='clip')]
    psum x1 -> x0, blocking collectives: 244 us -> none  [local(): grad_dec_bias = lax.psum(jnp.sum(err, axis=0), 'dp')]
    unnamed x3 -> x6, waiting for transfers between devices: 0.71 us -> 240 us
    all_to_all x1 -> x0, blocking collectives: 221 us -> none  [local(): lax.all_to_all(parts.reshape(dp_count, slot_cap, full_width), 'dp', split...]
    all_gather x0 -> x3, blocking collectives: none -> 169 us  [the longest x1 68.7 us: local(): lax.all_gather(jnp.sum(err, axis=0), 'dp', axis=0, tiled=True)]
    all_to_all x3 -> x4, waiting for transfers between devices: 159 us -> 0.01 us  [the longest x1 0.01 us: local(): lax.all_to_all(acts.reshape(tok_rows, dp_count, fs).transpose(1, 0, 2), '...]
    all_gather x2, waiting for transfers between devices: 13.1 us -> 107 us  [the longest x1 54.6 us: local(): codes_all = lax.all_gather(codes, ALL, axis=0, tiled=True)]
    scatter x0 -> x2, local copies, waits for them, and re-layouts: none -> 65.1 us  [the longest x1 34.6 us: slot_tables(): jnp.zeros((total,), jnp.bool_).at[slot_flat].set(True, unique_indices=True)]
  transfers between devices with their start and end apart: 6 -> 8, of which waited for: 4 -> 4; matrix products, arithmetic and copies ran while one was open for 2% -> 25% of each run, Pallas kernels for 0% -> 0%
where the time goes in v1:
time: 1200 us; the launch traced here: 1190 us
  local copies, waits for them, and re-layouts  523 us (44%)
  waiting for transfers between devices  347 us (29%)
  blocking collectives  212 us (18%)
  matrix products  42.1 us (4%)
  other arithmetic  32.1 us (3%)
  starting transfers between devices  21.8 us (2%)
  between operations  14.5 us (1%)
    unnamed x6, waiting for transfers between devices  240 us
    gather x2, local copies, waits for them, and re-layouts, to_slots(): jnp.take(x_fs, tok_at, axis=0, mode='clip')  130 us
    gather x4, local copies, waits for them, and re-layouts, pairs_to_slots(): jnp.take(flat, pair_at, axis=0, mode='clip')  127 us
    gather x3, local copies, waits for them, and re-layouts, slots_to_pairs(): jnp.take(v.reshape(owner_total * per_owner, -1), slot_flat, axis=0, mode=...  99.6 us
    all_gather x1, blocking collectives, local(): lax.all_gather(jnp.sum(err, axis=0), 'dp', axis=0, tiled=True)  68.7 us
    gather x3, local copies, waits for them, and re-layouts, slot_tables(): rank = jnp.take_along_axis(before, ids, axis=1)  68.3 us
    all_gather x1, blocking collectives, local(): ids_all = lax.all_gather(owner_ids, 'dp', axis=0, tiled=True)  58.4 us
    all_gather x1, waiting for transfers between devices, local(): codes_all = lax.all_gather(codes, ALL, axis=0, tiled=True)  54.6 us
  transfers between devices with their start and end apart: 8, of which 4 were waited for; matrix products, arithmetic and copies ran while one was open for 25% of the time, Pallas kernels for 0%

profile of v1, /device:TPU:0, one launch (start us, length us, event | category | flops | bytes accessed | tf_op | source)
XLA Modules:
  0.0 1192.7 jit_solution(9231432582393051338)
XLA Ops:
  7.2 2.3 copy.112
  9.5 8.3 all-to-all-start
  17.9 58.4 %all_gather.15 = s32[2048,4]{1,0:T(8,128)S(1)} all-gather(s32[128,4]{1,0:T(8,128)S(1)} %copy.88), channel_id=1, replica_groups=mesh['dp'=16,'lat'=2] {'dp'}, dimensions={0}, use_global_device_ids=true | all-gather | bytes 34816 | tf_op jit(solution)/shard_map/all_gather | solution.py:56
  77.5 1.5 copy.90
  79.0 1.1 fusion.39
  80.1 2.4 copy.91
  82.5 2.2 copy.108
  84.7 2.5 copy.93
  87.2 5.0 all-to-all-start.1
  93.4 1.0 bitcast_subtract_fusion
  94.5 65.5 %gather_fusion.8 = s32[8192]{0:T(1024)S(1)} fusion(s32[2048,32]{0,1:T(8,128)S(1)} %bitcast_subtract_fusion, s32[8192]{0:T(1024)S(1)} %reshape.297), kind=kCustom, calls=%fused_computation.8 | custom fusion | bytes 131072 | tf_op jit(solution)/shard_map/jit(take_along_axis)/gather | solution.py:19
  160.0 2.1 reshape.300
  162.1 1.5 select_add_fusion
  165.1 34.6 %scatter_custom_fusion = pred[16384]{0:T(1024)(128)(4,1)S(1)} fusion(s32[8192]{0:T(1024)S(1)} %bitcast.93, pred[8192]{0:T(1024)(128)(4,1)S(1)} %broadcast.354, pred[]{:T(512)} %constant.107.clone.1), kind=kCustom, calls=%fused_computation.66 | custom fusion | bytes 16385 | tf_op jit(solution)/shard_map/scatter | solution.py:26
  199.8 30.5 %scatter_custom_fusion.1 = s32[16384]{0:T(1024)S(1)} fusion(s32[8192]{0:T(1024)S(1)} %bitcast.94, s32[8192]{0:T(1024)S(1)} %iota.27, s32[]{:T(128)} %constant.111.clone.1), kind=kCustom, calls=%fused_computation.64 | custom fusion | bytes 65540 | tf_op jit(solution)/shard_map/scatter | solution.py:25
  230.4 65.2 %gather_fusion = bf16[16384,256]{1,0:T(8,128)(2,1)} fusion(bf16[2048,256]{1,0:T(8,128)(2,1)S(1)} %bitcast.62, s32[16384]{0:T(1024)S(1)} %get-tuple-element.9), kind=kCustom, calls=%fused_computation | custom fusion | bytes 16842752 | tf_op jit(solution)/shard_map/jit(_take)/gather | solution.py:62
  295.6 8.5 fusion.1
  304.1 31.2 %gather_fusion.1 = f32[8192,128]{1,0:T(8,128)} fusion(f32[16384,128]{1,0:T(8,128)} %bitcast.67, s32[8192]{0:T(1024)S(1)} %broadcast_clamp_fusion.1), kind=kCustom, calls=%fused_computation.1 | custom fusion | bytes 8421376 | tf_op jit(solution)/shard_map/jit(_take)/gather | solution.py:67
  336.8 41.7 %all-gather = f32[32,1,128]{2,1,0:T(1,128)S(1)} all-gather(f32[1,1,128]{2,1,0:T(1,128)S(1)} %bitcast.96), channel_id=1, replica_groups=mesh['dp'=16,'lat'=2] {'dp','lat'}, dimensions={0}, use_global_device_ids=true | all-gather | bytes 16896 | tf_op jit(solution)/shard_map/all_gather | solution.py:84
  379.3 99.2 %all-reduce.6.cloned.1.call-done = f32[2048,4,128]{2,1,0:T(4,128)} async-done(((f32[2048,4,128]{2,1,0:T(4,128)}), f32[2048,4,128]{2,1,0:T(4,128)}) %all-reduce.6.cloned.1.call-update) | async-done | bytes 4194320
  478.4 4.3 multiply_convert_fusion
  483.6 54.6 %all-gather.5.cloned.1.call-done = bf16[2048,4,128]{2,1,0:T(4,128)(2,1)} async-done(((bf16[64,4,128]{2,1,0:T(4,128)(2,1)}), bf16[2048,4,128]{2,1,0:T(4,128)(2,1)}) %all-gather.5.cloned.1.call-update) | async-done | bytes 2097168 | tf_op jit(solution)/shard_map/all_gather | solution.py:90
  538.2 57.2 %gather_fusion.3 = bf16[16384,128]{1,0:T(8,128)(2,1)} fusion(bf16[8192,128]{1,0:T(8,128)(2,1)} %bitcast.63, s32[16384]{0:T(1024)S(1)} %get-tuple-element.8), kind=kCustom, calls=%fused_computation.3 | custom fusion | bytes 8454144 | tf_op jit(solution)/shard_map/jit(_take)/gather | solution.py:73
  595.4 6.5 copy.97
  601.9 11.0 fusion.10
  612.9 37.2 %gather_fusion.4 = f32[8192,256]{1,0:T(8,128)} fusion(f32[16384,256]{1,0:T(8,128)} %bitcast.65, s32[8192]{0:T(1024)S(1)} %broadcast_clamp_fusion.1), kind=kCustom, calls=%fused_computation.4 | custom fusion | bytes 16809984 | tf_op jit(solution)/shard_map/jit(_take)/gather | solution.py:67
  650.1 9.8 reshape.225
  659.9 13.8 %reduce_sum.39 = f32[2048,256]{1,0:T(8,128)} reduce(f32[2048,4,256]{2,1,0:T(4,128)} %reshape.225, f32[]{:T(128)} %constant.125.clone.1), dimensions={1}, to_apply=%region_5.6 | reduce | flops 1572864 | bytes 10485764 | tf_op jit(solution)/shard_map/reduce_sum | solution.py:93
  673.6 1.8 subtract_convert_fusion
  675.5 65.2 %gather_fusion.5 = bf16[16384,256]{1,0:T(8,128)(2,1)} fusion(bf16[2048,256]{1,0:T(8,128)(2,1)S(1)} %subtract_convert_fusion, s32[16384]{0:T(1024)S(1)} %get-tuple-element.9), kind=kCustom, calls=%fused_computation.5 | custom fusion | bytes 16842752 | tf_op jit(solution)/shard_map/jit(_take)/gather | solution.py:62
  740.6 8.5 fusion.2
  749.1 31.2 %gather_fusion.6 = f32[8192,128]{1,0:T(8,128)} fusion(f32[16384,128]{1,0:T(8,128)} %bitcast.66, s32[8192]{0:T(1024)S(1)} %broadcast_clamp_fusion.1), kind=kCustom, calls=%fused_computation.6 | custom fusion | bytes 8421376 | tf_op jit(solution)/shard_map/jit(_take)/gather | solution.py:67
  780.6 140.4 %all-reduce.8.cloned.1.call-done = f32[2048,4,128]{2,1,0:T(4,128)} async-done(((f32[2048,4,128]{2,1,0:T(4,128)}), f32[2048,4,128]{2,1,0:T(4,128)}) %all-reduce.8.cloned.1.call-update) | async-done | bytes 4194320
  921.1 4.4 fusion.36
  925.5 2.0 subtract_reduce_fusion
  927.6 4.5 all-to-all-start.2
  932.1 52.9 %all-gather.7.cloned.1.call-done = bf16[2048,4,128]{2,1,0:T(4,128)(2,1)} async-done(((bf16[64,4,128]{2,1,0:T(4,128)(2,1)}), bf16[2048,4,128]{2,1,0:T(4,128)(2,1)}) %all-gather.7.cloned.1.call-update) | async-done | bytes 2097168 | tf_op jit(solution)/shard_map/all_gather | solution.py:116
  984.9 57.2 %gather_fusion.7 = bf16[16384,128]{1,0:T(8,128)(2,1)} fusion(bf16[8192,128]{1,0:T(8,128)(2,1)} %bitcast.64, s32[16384]{0:T(1024)S(1)} %get-tuple-element.8), kind=kCustom, calls=%fused_computation.7 | custom fusion | bytes 8454144 | tf_op jit(solution)/shard_map/jit(_take)/gather | solution.py:73
  1042.1 6.5 copy.100
  1048.6 7.1 fusion
  1055.7 7.0 add_convert_fusion
  1062.7 3.5 all-to-all-start.3
  1066.3 68.7 %all-gather.1 = f32[16,1,256]{2,1,0:T(1,128)S(1)} all-gather(f32[1,1,256]{2,1,0:T(1,128)S(1)} %bitcast.95), channel_id=1, replica_groups=mesh['dp'=16,'lat'=2] {'dp'}, dimensions={0}, use_global_device_ids=true | all-gather | bytes 17408 | tf_op jit(solution)/shard_map/all_gather | solution.py:104
  1135.1 1.1 copy.105
  1136.1 1.3 multiply_reduce_fusion
  1137.5 43.1 %all-reduce.2 = f32[4096]{0:T(1024)S(1)} all-reduce(f32[4096]{0:T(1024)S(1)} %bitcast.91), channel_id=4, replica_groups=mesh['dp'=16,'lat'=2] {'dp','lat'}, use_global_device_ids=true, to_apply=%region_8.9.clone | all-reduce | flops 4096 | bytes 32768
  1181.2 1.2 copy.101
  1182.4 2.7 copy.109
  (70 shorter events, 8.8 us)
Async XLA Ops:
  7.2 10.6 copy-start.9
  9.5 77.7 %all-to-all-start = ((bf16[16,128,256]{2,1,0:T(8,128)(2,1)}), bf16[16,128,256]{2,1,0:T(8,128)(2,1)S(1)}, u32[]{:S(2)}, u32[]{:S(2)}) async-start(bf16[16,128,256]{2,1,0:T(8,128)(2,1)} %bitcast.61), calls=%async_computation | async-start | bytes 2097152 | tf_op jit(solution)/shard_map/all_to_all | solution.py:46
  76.3 16.1 %copy-start.4 = (s32[2048,4]{1,0:T(8,128)}, s32[2048,4]{1,0:T(8,128)S(1)}, u32[]{:S(2)}) copy-start(s32[2048,4]{1,0:T(8,128)S(1)} %all_gather.15) | copy-start | bytes 98308
  87.2 6.2 copy-start
  87.2 208.4 %all-to-all-start.1 = ((bf16[32,128,256]{2,1,0:T(8,128)(2,1)}), bf16[32,128,256]{2,1,0:T(8,128)(2,1)}, u32[]{:S(2)}, u32[]{:S(2)}) async-start(bf16[32,128,256]{2,1,0:T(8,128)(2,1)} %bitcast.73), calls=%async_computation.1 | async-start | bytes 4194304 | tf_op jit(solution)/shard_map/all_to_all | solution.py:54
  92.2 386.2 %all-reduce.6.cloned.1.call-start = ((), (), s32[]{:S(2)}) async-start(), calls=%async_computation.6 | async-start | bytes 8388608
  94.5 67.7 %copy-start.5 = (s32[2048,4]{1,0:T(8,128)S(1)}, s32[2048,4]{1,0:T(8,128)}, u32[]{:S(2)}) copy-start(s32[2048,4]{1,0:T(8,128)} %copy-done.4) | copy-start | bytes 98308
  160.0 70.3 %copy-start.1 = (bf16[16,128,256]{2,1,0:T(8,128)(2,1)S(1)}, bf16[16,128,256]{2,1,0:T(8,128)(2,1)}, u32[]{:S(2)}) copy-start(bf16[16,128,256]{2,1,0:T(8,128)(2,1)} %copy-done) | copy-start | bytes 3145732
  335.3 0.7 copy-start.10
  335.3 1.0 copy-start.11
  335.3 1.5 copy-start.14
  335.3 202.9 %all-gather.5.cloned.1.call-start = ((), (), s32[]{:S(2)}) async-start(), calls=%async_computation.4 | async-start | bytes 2162688 | tf_op jit(solution)/shard_map/all_gather | solution.py:90
  336.2 0.6 copy-start.6
  379.3 103.6 %copy-start.12 = (s32[128]{0:T(128)}, s32[128]{0:T(128)S(1)}, u32[]{:S(2)}) copy-start(s32[128]{0:T(128)S(1)} %get-tuple-element.12) | copy-start | bytes 1540
  379.3 216.1 %copy-start.13 = (s32[128]{0:T(128)}, s32[128]{0:T(128)S(1)}, u32[]{:S(2)}) copy-start(s32[128]{0:T(128)S(1)} %get-tuple-element.13) | copy-start | bytes 1540
  482.8 438.3 %all-reduce.8.cloned.1.call-start = ((), (), s32[]{:S(2)}) async-start(), calls=%async_computation.7 | async-start | bytes 8388608
  483.6 190.0 %copy-start.8 = (f32[256]{0:T(256)}, f32[256]{0:T(256)S(1)}, u32[]{:S(2)}) copy-start(f32[256]{0:T(256)S(1)} %dynamic_slice.11) | copy-start | bytes 3076
  780.3 145.2 %copy-start.2 = (f32[2048,256]{1,0:T(8,128)S(1)}, f32[2048,256]{1,0:T(8,128)}, u32[]{:S(2)}) copy-start(f32[2048,256]{1,0:T(8,128)} %reduce_sum.39) | copy-start | bytes 6291460
  780.3 204.6 %all-gather.7.cloned.1.call-start = ((), (), s32[]{:S(2)}) async-start(), calls=%async_computation.5 | async-start | bytes 2162688 | tf_op jit(solution)/shard_map/all_gather | solution.py:116
  927.6 135.2 %all-to-all-start.2 = ((bf16[16,128,256]{2,1,0:T(8,128)(2,1)}), bf16[16,128,256]{2,1,0:T(8,128)(2,1)S(1)}, u32[]{:S(2)}, u32[]{:S(2)}) async-start(bf16[16,128,256]{2,1,0:T(8,128)(2,1)} %get-tuple-element.11), calls=%async_computation.2 | async-start | bytes 2097152 | tf_op jit(solution)/shard_map/all_to_all | solution.py:100
  1048.6 7.1 copy-start.3
  1062.7 3.5 copy-start.7
  1062.7 118.5 %all-to-all-start.3 = ((bf16[32,128,256]{2,1,0:T(8,128)(2,1)}), bf16[32,128,256]{2,1,0:T(8,128)(2,1)S(1)}, u32[]{:S(2)}, u32[]{:S(2)}) async-start(bf16[32,128,256]{2,1,0:T(8,128)(2,1)} %add_convert_fusion), calls=%async_computation.3 | async-start | bytes 4194304 | tf_op jit(solution)/shard_map/all_to_all | solution.py:122
Sparse Core Ops, SparseCore 0:
  335.5 142.9 all-reduce.5
  482.9 55.2 all-gather.4
  780.5 140.5 all-reduce.7
  925.6 59.2 all-gather.6

commit v2 on v1

v2 whole, which is shorter than its diff:
```python
import jax
import jax.numpy as jnp
from jax import lax
from jax.sharding import PartitionSpec as P

BLK_DEV = 2
ALL = ("dp", "lat")
F32 = jnp.float32
BF16 = jnp.bfloat16


def slot_tables(ids, owner_total, block_rows, slot_cap):
    tokens, own_count = ids.shape
    blocks = tokens // block_rows
    onehot = (ids[:, :, None] == jnp.arange(owner_total, dtype=jnp.int32)[None, None, :]).astype(
        jnp.int32
    )
    present = jnp.sum(onehot, axis=1).reshape(blocks, block_rows, owner_total)
    before = (jnp.cumsum(present, axis=1) - present).reshape(tokens, owner_total)
    rank = jnp.take_along_axis(before, ids, axis=1)
    slot = ids * slot_cap + rank
    slots = owner_total * slot_cap
    sel = (slot[:, :, None] == jnp.arange(slots, dtype=jnp.int32)[None, None, :]).astype(BF16)
    sel = sel.reshape(blocks, block_rows, own_count, slots)
    place = jnp.sum(sel, axis=2)
    return sel, place


def split_hi_lo(x):
    hi = lax.reduce_precision(x, exponent_bits=8, mantissa_bits=7)
    return hi.astype(BF16), (x - hi).astype(BF16)


def local(acts, owner_ids, block_codes, weights, enc_bias, dec_bias):
    dp_count = lax.axis_size("dp")
    lat_count = lax.axis_size("lat")
    dp_idx = lax.axis_index("dp")
    lat_idx = lax.axis_index("lat")
    me = dp_idx * lat_count + lat_idx
    owner_total = dp_count * lat_count
    tok_rows, own_count = owner_ids.shape
    half = acts.shape[1]
    full_width = weights.shape[1]
    lat_own = weights.shape[0]
    block_width = lat_own // BLK_DEV
    fs = half // dp_count
    mine_rows = tok_rows // lat_count
    tokens = tok_rows * dp_count
    blocks = dp_count
    slot_cap = max(2, 2 * tok_rows * own_count // owner_total)

    def rs_tokens(x):
        tail = x.shape[1:]
        y = x.reshape((dp_count, lat_count, mine_rows) + tail).swapaxes(0, 1)
        y = lax.psum_scatter(y, "lat", scatter_dimension=0, tiled=True)[0]
        return lax.psum_scatter(y, "dp", scatter_dimension=0, tiled=True)[0]

    def ag_tokens(x):
        y = lax.all_gather(x, "dp", axis=0, tiled=False)
        y = lax.all_gather(y, "lat", axis=1, tiled=False)
        return y.reshape((tokens,) + x.shape[1:])

    acts_fs = lax.all_to_all(
        acts.reshape(tok_rows, dp_count, fs).transpose(1, 0, 2), "dp", 0, 0, tiled=True
    )
    w_send = (
        weights.reshape(lat_own, lat_count, dp_count, fs)
        .transpose(2, 1, 0, 3)
        .reshape(owner_total, lat_own, fs)
    )
    w_fs = lax.all_to_all(w_send, ALL, 0, 0, tiled=True)

    ids_all = lax.all_gather(owner_ids, "dp", axis=0, tiled=True)
    sel, place = slot_tables(ids_all, owner_total, tok_rows, slot_cap)

    def rows_to_slots(x_fs):
        y = jnp.einsum("btq,btf->bqf", place, x_fs, preferred_element_type=F32).astype(BF16)
        return y.reshape(blocks, owner_total, slot_cap, fs)

    def slots_to_pairs(v):
        v = v.reshape(blocks, owner_total * slot_cap, -1)
        width = v.shape[-1]
        both = jnp.concatenate(split_hi_lo(v), axis=-1)
        out = jnp.einsum("btkq,bql->btkl", sel, both, preferred_element_type=F32)
        out = out[..., :width] + out[..., width:]
        return out.reshape(tokens, own_count, width)

    def pairs_to_slots(x):
        x = x.reshape(blocks, tok_rows, own_count, -1)
        y = jnp.einsum("btkq,btkl->bql", sel, x, preferred_element_type=F32).astype(BF16)
        return y.reshape(blocks, owner_total, slot_cap, -1)

    acts_slots = rows_to_slots(acts_fs)
    pre_part = jnp.einsum("borf,olf->borl", acts_slots, w_fs, preferred_element_type=F32)
    own_bias = jnp.where(
        (jnp.arange(owner_total) == me)[:, None], enc_bias[None, :], 0.0
    )
    pre_part = pre_part + own_bias[None, :, None, :]
    pre = rs_tokens(slots_to_pairs(pre_part))

    start = lat_idx * mine_rows
    my_ids = lax.dynamic_slice_in_dim(owner_ids, start, mine_rows, 0)
    my_codes = lax.dynamic_slice_in_dim(block_codes, start, mine_rows, 0)
    lat_block = jnp.arange(lat_own, dtype=jnp.int32) // block_width
    gate = ((my_codes[:, :, None] // (2**lat_block)[None, None, :]) % 2).astype(F32)
    codes = (jnp.maximum(pre, 0.0) * gate).astype(BF16)

    codes_slots = pairs_to_slots(ag_tokens(codes))
    contrib = jnp.einsum("borl,olf->borf", codes_slots, w_fs, preferred_element_type=F32)
    contrib = contrib.astype(BF16).reshape(blocks, owner_total * slot_cap, fs)
    summed = jnp.einsum("btq,bqf->btf", place, contrib, preferred_element_type=F32)
    bias_fs = lax.dynamic_slice_in_dim(dec_bias, dp_idx * fs, fs, 0)
    full = summed + bias_fs[None, None, :]
    err = full - acts_fs.astype(F32)
    gerr = err.astype(BF16)
    recon = (
        lax.all_to_all(full.astype(BF16), "dp", 0, 0, tiled=True)
        .transpose(1, 0, 2)
        .reshape(tok_rows, half)
    )
    grad_dec_bias = lax.all_gather(jnp.sum(err, axis=(0, 1)), "dp", axis=0, tiled=True)

    gerr_slots = rows_to_slots(gerr)
    gc_part = jnp.einsum("borf,olf->borl", gerr_slots, w_fs, preferred_element_type=F32)
    gcodes = rs_tokens(slots_to_pairs(gc_part))
    gpre = gcodes * gate * (pre > 0.0).astype(F32)
    own_hit = (
        my_ids[:, :, None] == jnp.arange(owner_total, dtype=jnp.int32)[None, None, :]
    ).astype(F32)
    genc_part = jnp.sum(own_hit[:, :, :, None] * gpre[:, :, None, :], axis=(0, 1))
    grad_enc_bias = lax.psum_scatter(genc_part.reshape(-1), ALL, scatter_dimension=0, tiled=True)

    gpre_slots = pairs_to_slots(ag_tokens(gpre.astype(BF16)))
    gw = jnp.einsum("borl,borf->olf", codes_slots, gerr_slots, preferred_element_type=F32)
    gw = gw + jnp.einsum("borl,borf->olf", gpre_slots, acts_slots, preferred_element_type=F32)
    gw_back = lax.all_to_all(gw.astype(BF16), ALL, 0, 0, tiled=True)
    grad_weights = (
        gw_back.reshape(dp_count, lat_count, lat_own, fs)
        .transpose(2, 1, 0, 3)
        .reshape(lat_own, full_width)
    )
    return (recon, grad_weights, grad_enc_bias, grad_dec_bias)


def solution(mesh):
    in_specs = (
        P("dp", "lat"),
        P("dp", None),
        P("dp", None),
        P(("dp", "lat"), None),
        P(("dp", "lat")),
        P("lat"),
    )
    out_specs = (P("dp", "lat"), P(("dp", "lat"), None), P(("dp", "lat")), P("lat"))
    return jax.shard_map(local, mesh=mesh, in_specs=in_specs, out_specs=out_specs, check_vma=False)
```

time: 1200 us -> 873 us (0.73)
  local copies, waits for them, and re-layouts: 523 us -> 119 us
  matrix products: 42.1 us -> 104 us
  other arithmetic: 32.1 us -> 66 us
  blocking collectives: 212 us -> 189 us
    gather x10 -> x0, local copies, waits for them, and re-layouts: 358 us -> none  [the longest x2 130 us: to_slots(): jnp.take(x_fs, tok_at, axis=0, mode='clip')]
    unnamed x6 -> x9, waiting for transfers between devices: 240 us -> 28.6 us
    reduce_scatter x0 -> x3, waiting for transfers between devices: none -> 179 us  [the longest x2 165 us: rs_tokens(): return lax.psum_scatter(y, 'dp', scatter_dimension=0, tiled=True)[0]]
    scatter x2 -> x0, local copies, waits for them, and re-layouts: 65.1 us -> none  [the longest x1 34.6 us: slot_tables(): jnp.zeros((total,), jnp.bool_).at[slot_flat].set(True, unique_indices=True)]
    dot_general x5 -> x12, matrix products: 42.1 us -> 104 us  [the longest x2 31.4 us: slots_to_pairs(): out = jnp.einsum('btkq,bql->btkl', sel, both, preferred_element_type=F32)]
    all_gather x2 -> x1, blocking collectives: 110 us -> 68.6 us  [local(): lax.all_gather(jnp.sum(err, axis=(0, 1)), 'dp', axis=0, tiled=True)]
    another operation x1, other arithmetic: 1.11 us -> 23.3 us  [slot_tables(): jnp.cumsum(present, axis=1) - present]
    all_to_all x1, waiting for transfers between devices: 0.01 us -> 21.3 us  [local(): lax.all_to_all(acts.reshape(tok_rows, dp_count, fs).transpose(1, 0, 2), '...]
  transfers between devices with their start and end apart: 8 -> 12, of which waited for: 4 -> 9; matrix products, arithmetic and copies ran while one was open for 25% -> 16% of each run, Pallas kernels for 0% -> 0%
where the time goes in v2:
time: 873 us; the launch traced here: 861 us
  waiting for transfers between devices  345 us (40%)
  blocking collectives  189 us (22%)
  local copies, waits for them, and re-layouts  119 us (14%)
  matrix products  104 us (12%)
  other arithmetic  66 us (8%)
  starting transfers between devices  24 us (3%)
  between operations  14.7 us (2%)
    reduce_scatter x2, waiting for transfers between devices, rs_tokens(): return lax.psum_scatter(y, 'dp', scatter_dimension=0, tiled=True)[0]  165 us
    all_gather x2, waiting for transfers between devices, ag_tokens(): y = lax.all_gather(x, 'dp', axis=0, tiled=False)  106 us
    all_gather x1, blocking collectives, local(): ids_all = lax.all_gather(owner_ids, 'dp', axis=0, tiled=True)  77.2 us
    all_gather x1, blocking collectives, local(): lax.all_gather(jnp.sum(err, axis=(0, 1)), 'dp', axis=0, tiled=True)  68.6 us
    gather x3, local copies, waits for them, and re-layouts, slot_tables(): rank = jnp.take_along_axis(before, ids, axis=1)  67.4 us
    unnamed x1, blocking collectives  43.3 us
    dot_general x2, matrix products, slots_to_pairs(): out = jnp.einsum('btkq,bql->btkl', sel, both, preferred_element_type=F32)  31.4 us
    unnamed x9, waiting for transfers between devices  28.6 us
  transfers between devices with their start and end apart: 12, of which 9 were waited for; matrix products, arithmetic and copies ran while one was open for 16% of the time, Pallas kernels for 0%

profile of v2, /device:TPU:0, one launch (start us, length us, event | category | flops | bytes accessed | tf_op | source)
XLA Modules:
  0.0 861.4 jit_solution(8032556234913147094)
XLA Ops:
  7.2 1.8 copy.158
  10.3 8.3 all-to-all-start
  19.2 2.5 copy.160
  21.7 21.3 %all-to-all-done = bf16[16,128,256]{2,1,0:T(8,128)(2,1)S(1)} async-done(((bf16[16,128,256]{2,1,0:T(8,128)(2,1)}), bf16[16,128,256]{2,1,0:T(8,128)(2,1)S(1)}, u32[]{:S(2)}, u32[]{:S(2)}) %all-to-all-start) | async-done | bytes 1048608 | tf_op jit(solution)/shard_map/all_to_all | solution.py:63
  43.0 4.9 all-to-all-start.1
  48.2 77.2 %all_gather.26 = s32[2048,4]{1,0:T(8,128)S(1)} all-gather(s32[128,4]{1,0:T(8,128)S(1)} %copy.153), channel_id=1, replica_groups=mesh['dp'=16,'lat'=2] {'dp'}, dimensions={0}, use_global_device_ids=true | all-gather | bytes 34816 | tf_op jit(solution)/shard_map/all_gather | solution.py:73
  126.4 23.3 %fusion.47 = s32[16,128,32]{2,0,1:T(8,128)S(1)} fusion(s32[16,128,32]{2,0,1:T(8,128)S(1)} %copy.155), kind=kOutput, calls=%fused_computation.98 | output fusion | flops 8323072 | bytes 524288 | tf_op jit(solution)/shard_map/jit(cumsum)/reduce_window_sum | solution.py:19
  152.9 65.7 %gather_fusion = s32[8192]{0:T(1024)S(1)} fusion(s32[2048,32]{0,1:T(8,128)S(1)} %bitcast_subtract_fusion, s32[8192]{0:T(1024)S(1)} %reshape.258), kind=kCustom, calls=%fused_computation | custom fusion | bytes 131072 | tf_op jit(solution)/shard_map/jit(take_along_axis)/gather | solution.py:20
  222.7 4.6 fusion.5
  227.4 2.0 copy-done.1
  229.3 5.6 convolution_convert_fusion.1
  234.9 9.5 %add_bitcast_fusion = f32[16,32,32,128]{3,2,0,1:T(8,128)} fusion(f32[32,128]{1,0:T(8,128)S(1)} %broadcast_select_fusion, bf16[16,32,32,256]{3,2,1,0:T(8,128)(2,1)} %bitcast.118, bf16[32,128,256]{2,1,0:T(8,128)(2,1)} %all-to-all-done.1), kind=kOutput, calls=%fused_computation.31 | convolution fusion | flops 1075838976 | bytes 18890752 | tf_op jit(solution)/shard_map/borf,olf->borl/dot_general | solution.py:94
  244.5 4.8 copy.162
  249.3 5.8 reduce-precision_convert_fusion.1
  255.1 15.6 %fusion.3 = f32[16,128,4,256]{3,1,2,0:T(8,128)} fusion(s32[16,128,4]{1,2,0:T(4,128)S(1)} %copy.157, bf16[16,1024,128]{2,1,0:T(8,128)(2,1)} %get-tuple-element.35, bf16[16,1024,128]{2,1,0:T(8,128)(2,1)} %get-tuple-element.34), kind=kOutput, calls=%fused_computation.5 | convolution fusion | flops 4320133120 | bytes 16809984 | tf_op jit(solution)/shard_map/btkq,bql->btkl/dot_general | solution.py:84
  270.6 4.2 slice_add_fusion.1
  274.9 2.3 copy.202
  277.2 13.4 %reduce-scatter.7.cloned.1.call-done = f32[1,16,64,4,128]{4,2,3,1,0:T(8,128)} async-done(((f32[2,16,64,4,128]{4,2,3,1,0:T(8,128)}), f32[1,16,64,4,128]{4,2,3,1,0:T(8,128)}) %reduce-scatter.7.cloned.1.call-update) | async-done | bytes 2097168 | tf_op jit(solution)/shard_map/reduce_scatter | solution.py:55
  290.8 83.9 %reduce-scatter.9.cloned.1.call-done = f32[1,64,4,128]{3,1,2,0:T(8,128)} async-done(((f32[16,64,4,128]{3,1,2,0:T(8,128)}), f32[1,64,4,128]{3,1,2,0:T(8,128)}) %reduce-scatter.9.cloned.1.call-update) | async-done | bytes 131088 | tf_op jit(solution)/shard_map/reduce_scatter | solution.py:56
  374.7 3.0 multiply_convert_fusion
  377.7 53.2 %all-gather.8.cloned.1.call-done = bf16[16,64,4,128]{3,1,2,0:T(8,128)(2,1)} async-done(((bf16[1,64,4,128]{3,1,2,0:T(8,128)(2,1)}), bf16[16,64,4,128]{3,1,2,0:T(8,128)(2,1)}) %all-gather.8.cloned.1.call-update) | async-done | bytes 1048592 | tf_op jit(solution)/shard_map/all_gather | solution.py:59
  431.8 10.0 %all-gather.12.cloned.1.call-done = bf16[16,128,4,128]{3,1,2,0:T(8,128)(2,1)} async-done(((bf16[16,64,4,128]{3,1,2,0:T(8,128)(2,1)}), bf16[16,128,4,128]{3,1,2,0:T(8,128)(2,1)}) %all-gather.12.cloned.1.call-update) | async-done | bytes 2097168 | tf_op jit(solution)/shard_map/all_gather | solution.py:60
  441.8 7.3 bitcast_convert_fusion.1
  449.1 2.1 copy-done.5
  451.2 7.2 convert_bitcast_fusion
  458.4 8.2 copy.166
  466.6 6.8 fusion.30
  473.3 3.9 convolution_convert_fusion
  477.3 8.7 %fusion.22 = f32[16,32,32,128]{3,2,0,1:T(8,128)} fusion(bf16[16,32,32,256]{3,2,1,0:T(8,128)(2,1)S(1)} %bitcast.116, bf16[32,128,256]{2,1,0:T(8,128)(2,1)} %all-to-all-done.1), kind=kOutput, calls=%fused_computation.41 | convolution fusion | flops 1073741824 | bytes 18874368 | tf_op jit(solution)/shard_map/borf,olf->borl/dot_general | solution.py:124
  486.1 8.1 copy.170
  494.1 8.7 %reduce-precision_convert_fusion = (bf16[16,1024,128]{2,1,0:T(8,128)(2,1)}, bf16[16,1024,128]{2,1,0:T(8,128)(2,1)}) fusion(f32[16,32,32,128]{3,2,1,0:T(8,128)} %copy.170), kind=kLoop, calls=%fused_computation.13 | loop fusion | flops 8388608 | bytes 16777216 | tf_op jit(solution)/shard_map/convert_element_type | solution.py:31
  502.9 15.8 %fusion.1 = f32[16,128,4,256]{3,1,2,0:T(8,128)} fusion(s32[16,128,4]{1,2,0:T(4,128)S(1)} %copy.157, bf16[16,1024,128]{2,1,0:T(8,128)(2,1)} %get-tuple-element.33, bf16[16,1024,128]{2,1,0:T(8,128)(2,1)} %get-tuple-element.32), kind=kOutput, calls=%fused_computation.3 | convolution fusion | flops 4320133120 | bytes 16809984 | tf_op jit(solution)/shard_map/btkq,bql->btkl/dot_general | solution.py:84
  518.7 6.5 slice_add_fusion
  526.4 28.5 %all-reduce.4.cloned.1.call-done = f32[2,16,64,4,128]{4,2,0,3,1:T(8,128)} async-done(((f32[2,16,64,4,128]{4,2,0,3,1:T(8,128)}), f32[2,16,64,4,128]{4,2,0,3,1:T(8,128)}) %all-reduce.4.cloned.1.call-update) | async-done | bytes 4194320
  555.0 3.8 dynamic-slice_bitcast_fusion
  559.2 81.6 %reduce-scatter.11.cloned.1.call-done = f32[1,64,4,128]{3,1,2,0:T(8,128)} async-done(((f32[16,64,4,128]{3,1,2,0:T(8,128)}), f32[1,64,4,128]{3,1,2,0:T(8,128)}) %reduce-scatter.11.cloned.1.call-update) | async-done | bytes 131088 | tf_op jit(solution)/shard_map/reduce_scatter | solution.py:56
  640.8 2.4 fusion.39
  643.2 3.0 select_convert_fusion
  646.3 52.4 %all-gather.10.cloned.1.call-done = bf16[16,64,4,128]{3,1,2,0:T(8,128)(2,1)} async-done(((bf16[1,64,4,128]{3,1,2,0:T(8,128)(2,1)}), bf16[16,64,4,128]{3,1,2,0:T(8,128)(2,1)}) %all-gather.10.cloned.1.call-update) | async-done | bytes 1048592 | tf_op jit(solution)/shard_map/all_gather | solution.py:59
  698.6 4.4 all-to-all-start.2
  703.1 9.2 %fusion.48 = f32[32,128,256,1]{2,1,0,3:T(8,128)} fusion(bf16[16,32,32,128]{3,2,1,0:T(8,128)(2,1)} %bitcast.124, bf16[16,32,32,256]{3,2,1,0:T(8,128)(2,1)} %bitcast.117), kind=kOutput, calls=%fused_computation.99 | convolution fusion | flops 1073741824 | bytes 16777216 | tf_op jit(solution)/shard_map/borl,borf->olf/dot_general | solution.py:134
  712.3 7.3 bitcast_convert_fusion
  719.6 6.6 fusion.20
  726.4 5.6 all-to-all-start.3
  732.4 68.6 %all-gather.2 = f32[16,1,256]{2,1,0:T(1,128)S(1)} all-gather(f32[1,1,256]{2,1,0:T(1,128)S(1)} %bitcast.142), channel_id=1, replica_groups=mesh['dp'=16,'lat'=2] {'dp'}, dimensions={0}, use_global_device_ids=true | all-gather | bytes 17408 | tf_op jit(solution)/shard_map/all_gather | solution.py:121
  802.3 2.3 copy.175
  805.9 43.3 %all-reduce.1 = f32[4096]{0:T(1024)S(1)} all-reduce(f32[4096]{0:T(1024)S(1)} %bitcast.140), channel_id=8, replica_groups=mesh['dp'=16,'lat'=2] {'dp','lat'}, use_global_device_ids=true, to_apply=%region_8.9.clone | all-reduce | flops 4096 | bytes 32768
  851.0 2.7 copy.189
  (80 shorter events, 18.8 us)
Async XLA Ops:
  7.2 11.4 %copy-start.9 = (bf16[128,8192]{1,0:T(8,128)(2,1)S(1)}, bf16[128,8192]{1,0:T(8,128)(2,1)}, u32[]{:S(2)}) copy-start(bf16[128,8192]{1,0:T(8,128)(2,1)} %param.9) | copy-start | bytes 6291460
  10.3 32.8 %all-to-all-start = ((bf16[16,128,256]{2,1,0:T(8,128)(2,1)}), bf16[16,128,256]{2,1,0:T(8,128)(2,1)S(1)}, u32[]{:S(2)}, u32[]{:S(2)}) async-start(bf16[16,128,256]{2,1,0:T(8,128)(2,1)} %bitcast.3), calls=%async_computation | async-start | bytes 2097152 | tf_op jit(solution)/shard_map/all_to_all | solution.py:63
  19.2 28.8 %copy-start.11 = (s32[128,4]{0,1:T(4,128)S(1)}, s32[128,4]{0,1:T(4,128)}, u32[]{:S(2)}) copy-start(s32[128,4]{0,1:T(4,128)} %param.7) | copy-start | bytes 6148
  43.0 5.0 copy-start.6
  43.0 191.9 %all-to-all-start.1 = ((bf16[32,128,256]{2,1,0:T(8,128)(2,1)}), bf16[32,128,256]{2,1,0:T(8,128)(2,1)}, u32[]{:S(2)}, u32[]{:S(2)}) async-start(bf16[32,128,256]{2,1,0:T(8,128)(2,1)} %bitcast.6), calls=%async_computation.1 | async-start | bytes 4194304 | tf_op jit(solution)/shard_map/all_to_all | solution.py:71
  48.0 242.6 %reduce-scatter.7.cloned.1.call-start = ((), (), s32[]{:S(2)}) async-start(), calls=%async_computation.7 | async-start | bytes 6291456 | tf_op jit(solution)/shard_map/reduce_scatter | solution.py:55
  125.3 25.6 %copy-start.3 = (s32[2048,4]{1,0:T(8,128)}, s32[2048,4]{1,0:T(8,128)S(1)}, u32[]{:S(2)}) copy-start(s32[2048,4]{1,0:T(8,128)S(1)} %all_gather.26) | copy-start | bytes 98308
  152.9 66.8 %copy-start.4 = (s32[2048,4]{1,0:T(8,128)S(1)}, s32[2048,4]{1,0:T(8,128)}, u32[]{:S(2)}) copy-start(s32[2048,4]{1,0:T(8,128)} %copy-done.3) | copy-start | bytes 98308
  218.7 4.0 copy-start.14
  219.8 9.6 %copy-start.7 = (bf16[16,128,256]{2,1,0:T(8,128)(2,1)S(1)}, bf16[16,128,256]{2,1,0:T(8,128)(2,1)}, u32[]{:S(2)}) copy-start(bf16[16,128,256]{2,1,0:T(8,128)(2,1)} %copy-done.6) | copy-start | bytes 3145732
  227.3 2.0 copy-start.1
  277.1 13.5 %copy-start.13 = (s32[128,4]{0,1:T(4,128)S(1)}, s32[128,4]{0,1:T(4,128)}, u32[]{:S(2)}) copy-start(s32[128,4]{0,1:T(4,128)} %param.8) | copy-start | bytes 6148
  277.2 97.5 %reduce-scatter.9.cloned.1.call-start = ((), (), s32[]{:S(2)}) async-start(), calls=%async_computation.8 | async-start | bytes 2228224 | tf_op jit(solution)/shard_map/reduce_scatter | solution.py:56
  290.6 140.3 %all-gather.8.cloned.1.call-start = ((), (), s32[]{:S(2)}) async-start(), calls=%async_computation.9 | async-start | bytes 1114112 | tf_op jit(solution)/shard_map/all_gather | solution.py:59
  377.7 64.1 %all-gather.12.cloned.1.call-start = ((), (), s32[]{:S(2)}) async-start(), calls=%async_computation.12 | async-start | bytes 3145728 | tf_op jit(solution)/shard_map/all_gather | solution.py:60
  431.0 124.0 %all-reduce.4.cloned.1.call-start = ((), (), s32[]{:S(2)}) async-start(), calls=%async_computation.14 | async-start | bytes 8388608
  449.1 2.1 copy-start.5
  458.4 8.2 copy-start.2
  477.3 8.8 %copy-start = (bf16[16,1024,256]{2,1,0:T(8,128)(2,1)}, bf16[16,1024,256]{2,1,0:T(8,128)(2,1)S(1)}, u32[]{:S(2)}) copy-start(bf16[16,1024,256]{2,1,0:T(8,128)(2,1)S(1)} %convolution_convert_fusion) | copy-start | bytes 25165828
  525.2 0.7 copy-start.15
  525.2 115.6 %copy-start.10 = (f32[1,64,4,128]{3,1,2,0:T(8,128)S(1)}, f32[1,64,4,128]{3,1,2,0:T(8,128)}, u32[]{:S(2)}) copy-start(f32[1,64,4,128]{3,1,2,0:T(8,128)} %reduce-scatter.9.cloned.1.call-done) | copy-start | bytes 393220
  525.2 115.6 %reduce-scatter.11.cloned.1.call-start = ((), (), s32[]{:S(2)}) async-start(), calls=%async_computation.10 | async-start | bytes 2228224 | tf_op jit(solution)/shard_map/reduce_scatter | solution.py:56
  558.8 139.8 %all-gather.10.cloned.1.call-start = ((), (), s32[]{:S(2)}) async-start(), calls=%async_computation.11 | async-start | bytes 1114112 | tf_op jit(solution)/shard_map/all_gather | solution.py:59
  646.2 66.1 %all-gather.14.cloned.1.call-start = ((), (), s32[]{:S(2)}) async-start(), calls=%async_computation.13 | async-start | bytes 3145728 | tf_op jit(solution)/shard_map/all_gather | solution.py:60
  698.6 27.8 %all-to-all-start.2 = ((bf16[16,128,256]{2,1,0:T(8,128)(2,1)}), bf16[16,128,256]{2,1,0:T(8,128)(2,1)S(1)}, u32[]{:S(2)}, u32[]{:S(2)}) async-start(bf16[16,128,256]{2,1,0:T(8,128)(2,1)} %get-tuple-element.37), calls=%async_computation.4 | async-start | bytes 2097152 | tf_op jit(solution)/shard_map/all_to_all | solution.py:117
  712.3 7.3 copy-start.8
  726.2 5.9 copy-start.12
  726.4 123.4 %all-to-all-start.3 = ((bf16[32,128,256]{2,1,0:T(8,128)(2,1)}), bf16[32,128,256]{2,1,0:T(8,128)(2,1)S(1)}, u32[]{:S(2)}, u32[]{:S(2)}) async-start(bf16[32,128,256]{2,1,0:T(8,128)(2,1)} %fusion.20), calls=%async_computation.6 | async-start | bytes 4194304 | tf_op jit(solution)/shard_map/all_to_all | solution.py:136
Sparse Core Ops, SparseCore 0:
  277.3 13.2 reduce-scatter.6
  292.9 81.6 reduce-scatter.8
  378.4 52.5 all-gather.7
  432.4 9.3 all-gather.11
  525.3 29.5 all-reduce.3
  558.9 81.8 reduce-scatter.10
  646.3 52.2 all-gather.9
  700.2 9.3 all-gather.13

commit v3 on v2

--- a/solution.py
+++ b/solution.py
@@ -17,7 +17,7 @@
     )
     present = jnp.sum(onehot, axis=1).reshape(blocks, block_rows, owner_total)
     before = (jnp.cumsum(present, axis=1) - present).reshape(tokens, owner_total)
-    rank = jnp.take_along_axis(before, ids, axis=1)
+    rank = jnp.sum(onehot * before[:, None, :], axis=2)
     slot = ids * slot_cap + rank
     slots = owner_total * slot_cap
     sel = (slot[:, :, None] == jnp.arange(slots, dtype=jnp.int32)[None, None, :]).astype(BF16)
@@ -52,11 +52,11 @@
     def rs_tokens(x):
         tail = x.shape[1:]
         y = x.reshape((dp_count, lat_count, mine_rows) + tail).swapaxes(0, 1)
-        y = lax.psum_scatter(y, "lat", scatter_dimension=0, tiled=True)[0]
-        return lax.psum_scatter(y, "dp", scatter_dimension=0, tiled=True)[0]
+        y = jnp.sum(lax.all_to_all(y, "lat", 0, 0, tiled=True), axis=0)
+        return jnp.sum(lax.all_to_all(y, "dp", 0, 0, tiled=True), axis=0)
 
     def ag_tokens(x):
-        y = lax.all_gather(x, "dp", axis=0, tiled=False)
+        y = lax.all_to_all(jnp.broadcast_to(x[None], (dp_count,) + x.shape), "dp", 0, 0, tiled=True)
         y = lax.all_gather(y, "lat", axis=1, tiled=False)
         return y.reshape((tokens,) + x.shape[1:])
 
@@ -70,7 +70,9 @@
     )
     w_fs = lax.all_to_all(w_send, ALL, 0, 0, tiled=True)
 
-    ids_all = lax.all_gather(owner_ids, "dp", axis=0, tiled=True)
+    ids_rep = jnp.broadcast_to(owner_ids.astype(F32)[None], (dp_count, tok_rows, own_count))
+    ids_all = lax.all_to_all(ids_rep, "dp", 0, 0, tiled=True).astype(jnp.int32)
+    ids_all = ids_all.reshape(tokens, own_count)
     sel, place = slot_tables(ids_all, owner_total, tok_rows, slot_cap)
 
     def rows_to_slots(x_fs):
@@ -118,7 +120,8 @@
         .transpose(1, 0, 2)
         .reshape(tok_rows, half)
     )
-    grad_dec_bias = lax.all_gather(jnp.sum(err, axis=(0, 1)), "dp", axis=0, tiled=True)
+    gdb_rep = jnp.broadcast_to(jnp.sum(err, axis=(0, 1))[None], (dp_count, fs))
+    grad_dec_bias = lax.all_to_all(gdb_rep, "dp", 0, 0, tiled=True).reshape(half)
 
     gerr_slots = rows_to_slots(gerr)
     gc_part = jnp.einsum("borf,olf->borl", gerr_slots, w_fs, preferred_element_type=F32)
@@ -128,7 +131,7 @@
         my_ids[:, :, None] == jnp.arange(owner_total, dtype=jnp.int32)[None, None, :]
     ).astype(F32)
     genc_part = jnp.sum(own_hit[:, :, :, None] * gpre[:, :, None, :], axis=(0, 1))
-    grad_enc_bias = lax.psum_scatter(genc_part.reshape(-1), ALL, scatter_dimension=0, tiled=True)
+    grad_enc_bias = jnp.sum(lax.all_to_all(genc_part, ALL, 0, 0, tiled=True), axis=0)
 
     gpre_slots = pairs_to_slots(ag_tokens(gpre.astype(BF16)))
     gw = jnp.einsum("borl,borf->olf", codes_slots, gerr_slots, preferred_element_type=F32)

time: 873 us -> 560 us (0.64)
  waiting for transfers between devices: 345 us -> 161 us
  local copies, waits for them, and re-layouts: 119 us -> 46.7 us
  blocking collectives: 189 us -> 138 us
  other arithmetic: 66 us -> 47.4 us
  starting transfers between devices: 24 us -> 40.4 us
    reduce_scatter x3 -> x0, waiting for transfers between devices: 179 us -> none  [the longest x2 165 us: rs_tokens(): return lax.psum_scatter(y, 'dp', scatter_dimension=0, tiled=True)[0]]
    all_gather x2 -> x0, blocking collectives: 146 us -> none  [the longest x1 77.2 us: local(): ids_all = lax.all_gather(owner_ids, 'dp', axis=0, tiled=True)]
    all_to_all x0 -> x5, blocking collectives: none -> 138 us  [the longest x2 65.3 us: ag_tokens(): lax.all_to_all(jnp.broadcast_to(x[None], (dp_count,) + x.shape), 'dp', 0,...]
    all_gather x2 -> x0, waiting for transfers between devices: 106 us -> none  [ag_tokens(): y = lax.all_gather(x, 'dp', axis=0, tiled=False)]
    gather x3 -> x0, local copies, waits for them, and re-layouts: 67.4 us -> none  [slot_tables(): rank = jnp.take_along_axis(before, ids, axis=1)]
    all_to_all x0 -> x4, waiting for transfers between devices: none -> 54.8 us  [the longest x1 43.2 us: rs_tokens(): return jnp.sum(lax.all_to_all(y, 'dp', 0, 0, tiled=True), axis=0)]
    all_to_all x1, waiting for transfers between devices: 0.01 us -> 44.8 us  [local(): gw_back = lax.all_to_all(gw.astype(BF16), ALL, 0, 0, tiled=True)]
    unnamed x1 -> x0, blocking collectives: 43.3 us -> none
  transfers between devices with their start and end apart: 12 -> 10, of which waited for: 9 -> 8; matrix products, arithmetic and copies ran while one was open for 16% -> 10% of each run, Pallas kernels for 0% -> 0%
where the time goes in v3:
time: 560 us; the launch traced here: 550 us
  waiting for transfers between devices  161 us (29%)
  blocking collectives  138 us (25%)
  matrix products  102 us (18%)
  other arithmetic  47.4 us (8%)
  local copies, waits for them, and re-layouts  46.7 us (8%)
  starting transfers between devices  40.4 us (7%)
  between operations  14.6 us (3%)
    all_to_all x2, blocking collectives, ag_tokens(): lax.all_to_all(jnp.broadcast_to(x[None], (dp_count,) + x.shape), 'dp', 0,...  65.3 us
    all_to_all x1, blocking collectives, rs_tokens(): return jnp.sum(lax.all_to_all(y, 'dp', 0, 0, tiled=True), axis=0)  56.2 us
    all_to_all x1, waiting for transfers between devices, local(): gw_back = lax.all_to_all(gw.astype(BF16), ALL, 0, 0, tiled=True)  44.8 us
    all_to_all x1, waiting for transfers between devices, rs_tokens(): return jnp.sum(lax.all_to_all(y, 'dp', 0, 0, tiled=True), axis=0)  43.2 us
    dot_general x2, matrix products, slots_to_pairs(): out = jnp.einsum('btkq,bql->btkl', sel, both, preferred_element_type=F32)  31.2 us
    all_to_all x1, waiting for transfers between devices, local(): w_fs = lax.all_to_all(w_send, ALL, 0, 0, tiled=True)  29.2 us
    all_to_all x1, waiting for transfers between devices, local(): lax.all_to_all(acts.reshape(tok_rows, dp_count, fs).transpose(1, 0, 2), '...  20.1 us
    all_to_all x2, blocking collectives, rs_tokens(): y = jnp.sum(lax.all_to_all(y, 'lat', 0, 0, tiled=True), axis=0)  16.3 us
  transfers between devices with their start and end apart: 10, of which 8 were waited for; matrix products, arithmetic and copies ran while one was open for 10% of the time, Pallas kernels for 0%

profile of v3, /device:TPU:0, one launch (start us, length us, event | category | flops | bytes accessed | tf_op | source)
XLA Modules:
  0.0 549.8 jit_solution(17241950959453173431)
XLA Ops:
  8.6 8.3 %all-to-all-start = ((f32[16,128,4]{1,2,0:T(4,128)}), f32[16,128,4]{1,2,0:T(4,128)S(1)}, u32[]{:S(2)}, u32[]{:S(2)}) async-start(f32[16,128,4]{1,2,0:T(4,128)} %broadcast_in_dim.32), calls=%async_computation | async-start | bytes 65536 | tf_op jit(solution)/shard_map/all_to_all | solution.py:74
  19.9 4.5 all-to-all-done
  24.4 3.7 all-to-all-start.1
  28.6 2.5 copy.83
  31.1 20.1 %all-to-all-done.1 = bf16[16,128,256]{2,1,0:T(8,128)(2,1)S(1)} async-done(((bf16[16,128,256]{2,1,0:T(8,128)(2,1)}), bf16[16,128,256]{2,1,0:T(8,128)(2,1)S(1)}, u32[]{:S(2)}, u32[]{:S(2)}) %all-to-all-start.1) | async-done | bytes 1048608 | tf_op jit(solution)/shard_map/all_to_all | solution.py:63
  52.2 5.0 all-to-all-start.2
  59.0 2.4 fusion.44
  63.3 4.6 fusion.5
  69.9 6.8 %convolution_convert_fusion.1 = bf16[16,1024,256]{2,1,0:T(8,128)(2,1)} fusion(bf16[16,128,1024]{1,2,0:T(8,128)(2,1)S(1)} %fusion.5, bf16[16,128,256]{2,1,0:T(8,128)(2,1)} %copy-done.4), kind=kOutput, calls=%fused_computation.32 | convolution fusion | flops 1077936128 | bytes 13631488 | tf_op jit(solution)/shard_map/btq,btf->bqf/dot_general | solution.py:79
  76.7 29.2 %all-to-all-done.2 = bf16[32,128,256]{2,1,0:T(8,128)(2,1)S(1)} async-done(((bf16[32,128,256]{2,1,0:T(8,128)(2,1)}), bf16[32,128,256]{2,1,0:T(8,128)(2,1)S(1)}, u32[]{:S(2)}, u32[]{:S(2)}) %all-to-all-start.2) | async-done | bytes 2097184 | tf_op jit(solution)/shard_map/all_to_all | solution.py:71
  105.9 9.0 %add_bitcast_fusion = f32[16,32,32,128]{3,2,0,1:T(8,128)} fusion(f32[32,128]{1,0:T(8,128)S(1)} %broadcast_select_fusion, bf16[16,32,32,256]{3,2,1,0:T(8,128)(2,1)} %bitcast.111, bf16[32,128,256]{2,1,0:T(8,128)(2,1)S(1)} %all-to-all-done.2), kind=kOutput, calls=%fused_computation.30 | convolution fusion | flops 1075838976 | bytes 18890752 | tf_op jit(solution)/shard_map/borf,olf->borl/dot_general | solution.py:96
  114.9 4.8 copy.85
  119.7 5.8 %reduce-precision_convert_fusion.1 = (bf16[16,1024,128]{2,1,0:T(8,128)(2,1)}, bf16[16,1024,128]{2,1,0:T(8,128)(2,1)}) fusion(f32[16,32,32,128]{3,2,1,0:T(8,128)S(1)} %copy.85), kind=kLoop, calls=%fused_computation.14 | loop fusion | flops 8388608 | bytes 16777216 | tf_op jit(solution)/shard_map/convert_element_type | solution.py:31
  125.5 15.6 %fusion.3 = f32[16,128,4,256]{3,1,2,0:T(8,128)} fusion(s32[16,128,4]{1,2,0:T(4,128)S(1)} %copy.80, bf16[16,1024,128]{2,1,0:T(8,128)(2,1)} %get-tuple-element.23, bf16[16,1024,128]{2,1,0:T(8,128)(2,1)} %get-tuple-element.22), kind=kOutput, calls=%fused_computation.4 | convolution fusion | flops 4320133120 | bytes 16809984 | tf_op jit(solution)/shard_map/btkq,bql->btkl/dot_general | solution.py:86
  141.0 4.2 slice_add_fusion.1
  145.6 8.2 %all_to_all.70 = f32[2,16,64,4,128]{4,2,3,1,0:T(8,128)} all-to-all(f32[2,16,64,4,128]{4,2,3,1,0:T(8,128)S(1)} %bitcast.118), channel_id=1, replica_groups=mesh['dp'=16,'lat'=2] {'lat'}, dimensions={0} | all-to-all | bytes 8388608 | tf_op jit(solution)/shard_map/all_to_all | solution.py:55
  153.8 4.1 reduce_sum.99
  157.9 5.1 all-to-all-start.4
  163.1 43.2 %all-to-all-done.4 = f32[16,64,4,128]{3,1,2,0:T(8,128)} async-done(((f32[16,64,4,128]{3,1,2,0:T(8,128)}), f32[16,64,4,128]{3,1,2,0:T(8,128)}, u32[]{:S(2)}, u32[]{:S(2)}) %all-to-all-start.4) | async-done | bytes 2097184 | tf_op jit(solution)/shard_map/all_to_all | solution.py:56
  209.7 35.8 %all_to_all.71 = bf16[16,64,4,128]{3,1,2,0:T(8,128)(2,1)} all-to-all(bf16[16,64,4,128]{3,1,2,0:T(8,128)(2,1)S(1)} %broadcast_in_dim.36), channel_id=1, replica_groups=mesh['dp'=16,'lat'=2] {'dp'}, dimensions={0} | all-to-all | bytes 2097152 | tf_op jit(solution)/shard_map/all_to_all | solution.py:59
  246.3 8.2 %all-gather.5.cloned.1.call-done = bf16[16,128,4,128]{3,1,2,0:T(8,128)(2,1)} async-done(((bf16[16,64,4,128]{3,1,2,0:T(8,128)(2,1)}), bf16[16,128,4,128]{3,1,2,0:T(8,128)(2,1)}) %all-gather.5.cloned.1.call-update) | async-done | bytes 2097168 | tf_op jit(solution)/shard_map/all_gather | solution.py:60
  254.5 7.3 %bitcast_convert_fusion.1 = bf16[16,1024,128]{2,1,0:T(8,128)(2,1)S(1)} fusion(bf16[16,128,4,128]{3,1,2,0:T(8,128)(2,1)} %all-gather.5.cloned.1.call-done, s32[16,128,4]{1,2,0:T(4,128)S(1)} %copy.80), kind=kOutput, calls=%fused_computation.24 | convolution fusion | flops 2157969408 | bytes 6324224 | tf_op jit(solution)/shard_map/btkq,btkl->bql/dot_general | solution.py:92
  261.9 2.0 copy-done.3
  263.9 5.6 %convert_bitcast_fusion = bf16[16,32,32,256]{3,2,0,1:T(8,128)(2,1)} fusion(bf16[16,32,32,128]{3,2,1,0:T(8,128)(2,1)S(1)} %bitcast.116, bf16[32,128,256]{2,1,0:T(8,128)(2,1)S(1)} %all-to-all-done.2), kind=kOutput, calls=%fused_computation.29 | convolution fusion | flops 1077936128 | bytes 14680064 | tf_op jit(solution)/shard_map/borl,olf->borf/dot_general | solution.py:111
  269.5 8.2 %copy.90 = bf16[16,32,32,256]{3,2,1,0:T(8,128)(2,1)} copy(bf16[16,32,32,256]{3,2,0,1:T(8,128)(2,1)} %convert_bitcast_fusion) | data formatting | bytes 16777216 | tf_op jit(solution)/shard_map/convert_element_type | solution.py:112
  277.6 7.1 %fusion.30 = (f32[256]{0:T(256)S(1)}, bf16[16,128,256]{2,1,0:T(8,128)(2,1)}, f32[16,128,256]{2,1,0:T(8,128)}) fusion(bf16[16,128,256]{2,1,0:T(8,128)(2,1)} %copy-done.4, f32[256]{0:T(256)S(1)} %dynamic_slice.10, bf16[16,128,1024]{1,2,0:T(8,128)(2,1)S(1)} %copy-done.2, bf16[16,1024,256]{2,1,0:T(8,128)(2,1)} %bitcast.113), kind=kOutput, calls=%fused_computation.47 | convolution fusion | flops 1076363008 | bytes 16779264 | tf_op jit(solution)/shard_map/btq,bqf->btf/dot_general | solution.py:113
  284.8 4.0 convolution_convert_fusion
  288.7 5.7 %fusion.22 = f32[16,32,32,128]{3,2,0,1:T(8,128)} fusion(bf16[16,32,32,256]{3,2,1,0:T(8,128)(2,1)S(1)} %bitcast.109, bf16[32,128,256]{2,1,0:T(8,128)(2,1)S(1)} %all-to-all-done.2), kind=kOutput, calls=%fused_computation.41 | convolution fusion | flops 1073741824 | bytes 18874368 | tf_op jit(solution)/shard_map/borf,olf->borl/dot_general | solution.py:127
  294.5 8.0 %copy.94 = f32[16,32,32,128]{3,2,1,0:T(8,128)} copy(f32[16,32,32,128]{3,2,0,1:T(8,128)} %fusion.22) | data formatting | bytes 16777216 | tf_op jit(solution)/shard_map/borf,olf->borl/transpose | solution.py:127
  302.5 8.9 %reduce-precision_convert_fusion = (bf16[16,1024,128]{2,1,0:T(8,128)(2,1)}, bf16[16,1024,128]{2,1,0:T(8,128)(2,1)}) fusion(f32[16,32,32,128]{3,2,1,0:T(8,128)} %copy.94), kind=kLoop, calls=%fused_computation.12 | loop fusion | flops 8388608 | bytes 16777216 | tf_op jit(solution)/shard_map/convert_element_type | solution.py:31
  311.4 15.6 %fusion.1 = f32[16,128,4,256]{3,1,2,0:T(8,128)} fusion(s32[16,128,4]{1,2,0:T(4,128)S(1)} %copy.80, bf16[16,1024,128]{2,1,0:T(8,128)(2,1)} %get-tuple-element.21, bf16[16,1024,128]{2,1,0:T(8,128)(2,1)} %get-tuple-element.20), kind=kOutput, calls=%fused_computation.2 | convolution fusion | flops 4320133120 | bytes 16809984 | tf_op jit(solution)/shard_map/btkq,bql->btkl/dot_general | solution.py:86
  327.0 4.2 slice_add_fusion
  331.5 8.2 %all_to_all.72 = f32[2,16,64,4,128]{4,2,3,1,0:T(8,128)} all-to-all(f32[2,16,64,4,128]{4,2,3,1,0:T(8,128)S(1)} %bitcast.119), channel_id=1, replica_groups=mesh['dp'=16,'lat'=2] {'lat'}, dimensions={0} | all-to-all | bytes 8388608 | tf_op jit(solution)/shard_map/all_to_all | solution.py:55
  339.7 2.8 reduce_sum.101
  342.5 56.2 %all_to_all.73 = f32[16,64,4,128]{3,1,2,0:T(8,128)} all-to-all(f32[16,64,4,128]{3,1,2,0:T(8,128)S(1)} %reduce_sum.101), channel_id=1, replica_groups=mesh['dp'=16,'lat'=2] {'dp'}, dimensions={0} | all-to-all | bytes 4194304 | tf_op jit(solution)/shard_map/all_to_all | solution.py:56
  402.1 29.5 %all_to_all.74 = bf16[16,64,4,128]{3,1,2,0:T(8,128)(2,1)} all-to-all(bf16[16,64,4,128]{3,1,2,0:T(8,128)(2,1)S(1)} %broadcast_in_dim.37), channel_id=1, replica_groups=mesh['dp'=16,'lat'=2] {'dp'}, dimensions={0} | all-to-all | bytes 2097152 | tf_op jit(solution)/shard_map/all_to_all | solution.py:59
  432.5 3.9 all-to-all-start.12
  436.5 7.2 %all-to-all-done.12 = f32[16,1,256]{2,1,0:T(1,128)S(1)} async-done(((f32[16,1,256]{2,1,0:T(1,128)}), f32[16,1,256]{2,1,0:T(1,128)S(1)}, u32[]{:S(2)}, u32[]{:S(2)}) %all-to-all-start.12) | async-done | bytes 16416 | tf_op jit(solution)/shard_map/all_to_all | solution.py:124
  443.7 3.7 all-to-all-start.6
  447.3 8.1 %fusion.45 = f32[32,128,256,1]{2,1,0,3:T(8,128)} fusion(bf16[16,32,32,128]{3,2,1,0:T(8,128)(2,1)} %bitcast.117, bf16[16,32,32,256]{3,2,1,0:T(8,128)(2,1)} %bitcast.110), kind=kOutput, calls=%fused_computation.90 | convolution fusion | flops 1073741824 | bytes 16777216 | tf_op jit(solution)/shard_map/borl,borf->olf/dot_general | solution.py:137
  457.5 8.4 %bitcast_convert_fusion = bf16[16,1024,128]{2,1,0:T(8,128)(2,1)} fusion(bf16[16,128,4,128]{3,1,2,0:T(8,128)(2,1)} %all-gather.7.cloned.1.call-done, s32[16,128,4]{1,2,0:T(4,128)S(1)} %copy.80), kind=kOutput, calls=%fused_computation.23 | convolution fusion | flops 2157969408 | bytes 6324224 | tf_op jit(solution)/shard_map/btkq,btkl->bql/dot_general | solution.py:92
  465.9 3.9 all-to-all-done.6
  469.9 4.8 all-to-all-start.11
  474.7 8.6 %fusion.20 = bf16[32,128,256]{2,1,0:T(8,128)(2,1)} fusion(f32[32,128,256,1]{2,1,0,3:T(8,128)} %fusion.45, bf16[16,32,32,128]{3,2,1,0:T(8,128)(2,1)} %bitcast.127, bf16[16,32,32,256]{3,2,1,0:T(8,128)(2,1)} %bitcast.112), kind=kOutput, calls=%fused_computation.36 | convolution fusion | flops 1075838976 | bytes 18874368 | tf_op jit(solution)/shard_map/borl,borf->olf/dot_general | solution.py:138
  483.3 6.0 %all-to-all-start.10 = ((bf16[32,128,256]{2,1,0:T(8,128)(2,1)}), bf16[32,128,256]{2,1,0:T(8,128)(2,1)S(1)}, u32[]{:S(2)}, u32[]{:S(2)}) async-start(bf16[32,128,256]{2,1,0:T(8,128)(2,1)} %fusion.20), calls=%async_computation.10 | async-start | bytes 4194304 | tf_op jit(solution)/shard_map/all_to_all | solution.py:139
  490.6 2.3 copy.102
  493.5 44.8 %all-to-all-done.10 = bf16[32,128,256]{2,1,0:T(8,128)(2,1)S(1)} async-done(((bf16[32,128,256]{2,1,0:T(8,128)(2,1)}), bf16[32,128,256]{2,1,0:T(8,128)(2,1)S(1)}, u32[]{:S(2)}, u32[]{:S(2)}) %all-to-all-start.10) | async-done | bytes 2097184 | tf_op jit(solution)/shard_map/all_to_all | solution.py:139
  539.4 2.7 copy.118
  (63 shorter events, 26.6 us)
Async XLA Ops:
  7.2 20.9 %copy-start.6 = (bf16[128,8192]{1,0:T(8,128)(2,1)S(1)}, bf16[128,8192]{1,0:T(8,128)(2,1)}, u32[]{:S(2)}) copy-start(bf16[128,8192]{1,0:T(8,128)(2,1)} %param.9) | copy-start | bytes 6291460
  8.6 15.7 %all-to-all-start = ((f32[16,128,4]{1,2,0:T(4,128)}), f32[16,128,4]{1,2,0:T(4,128)S(1)}, u32[]{:S(2)}, u32[]{:S(2)}) async-start(f32[16,128,4]{1,2,0:T(4,128)} %broadcast_in_dim.32), calls=%async_computation | async-start | bytes 65536 | tf_op jit(solution)/shard_map/all_to_all | solution.py:74
  24.4 26.9 %all-to-all-start.1 = ((bf16[16,128,256]{2,1,0:T(8,128)(2,1)}), bf16[16,128,256]{2,1,0:T(8,128)(2,1)S(1)}, u32[]{:S(2)}, u32[]{:S(2)}) async-start(bf16[16,128,256]{2,1,0:T(8,128)(2,1)} %bitcast.1), calls=%async_computation.1 | async-start | bytes 2097152 | tf_op jit(solution)/shard_map/all_to_all | solution.py:63
  28.6 28.6 %copy-start.9 = (f32[128]{0:T(128)S(1)}, f32[128]{0:T(128)}, u32[]{:S(2)}) copy-start(f32[128]{0:T(128)} %param.10) | copy-start | bytes 1540
  51.3 1.0 copy-start.4
  52.2 53.7 %all-to-all-start.2 = ((bf16[32,128,256]{2,1,0:T(8,128)(2,1)}), bf16[32,128,256]{2,1,0:T(8,128)(2,1)S(1)}, u32[]{:S(2)}, u32[]{:S(2)}) async-start(bf16[32,128,256]{2,1,0:T(8,128)(2,1)} %bitcast.120), calls=%async_computation.2 | async-start | bytes 4194304 | tf_op jit(solution)/shard_map/all_to_all | solution.py:71
  68.0 2.0 copy-start.1
  153.8 9.3 %copy-start.8 = (s32[128,4]{0,1:T(4,128)S(1)}, s32[128,4]{0,1:T(4,128)}, u32[]{:S(2)}) copy-start(s32[128,4]{0,1:T(4,128)} %param.8) | copy-start | bytes 6148
  157.9 48.4 %all-to-all-start.4 = ((f32[16,64,4,128]{3,1,2,0:T(8,128)}), f32[16,64,4,128]{3,1,2,0:T(8,128)}, u32[]{:S(2)}, u32[]{:S(2)}) async-start(f32[16,64,4,128]{3,1,2,0:T(8,128)} %reduce_sum.99), calls=%async_computation.4 | async-start | bytes 4194304 | tf_op jit(solution)/shard_map/all_to_all | solution.py:56
  163.0 91.6 %all-gather.5.cloned.1.call-start = ((), (), s32[]{:S(2)}) async-start(), calls=%async_computation.13 | async-start | bytes 3145728 | tf_op jit(solution)/shard_map/all_gather | solution.py:60
  245.5 212.0 %all-gather.7.cloned.1.call-start = ((), (), s32[]{:S(2)}) async-start(), calls=%async_computation.14 | async-start | bytes 3145728 | tf_op jit(solution)/shard_map/all_gather | solution.py:60
  261.8 2.1 copy-start.3
  269.5 8.2 %copy-start.2 = (bf16[16,128,1024]{1,2,0:T(8,128)(2,1)S(1)}, bf16[16,128,1024]{1,2,0:T(8,128)(2,1)}, u32[]{:S(2)}) copy-start(bf16[16,128,1024]{1,2,0:T(8,128)(2,1)} %copy-done.1) | copy-start | bytes 12582916
  277.6 7.1 %copy-start.5 = (bf16[16,128,256]{2,1,0:T(8,128)(2,1)S(1)}, bf16[16,128,256]{2,1,0:T(8,128)(2,1)}, u32[]{:S(2)}) copy-start(bf16[16,128,256]{2,1,0:T(8,128)(2,1)} %copy-done.4) | copy-start | bytes 3145732
  288.7 5.7 %copy-start = (bf16[16,1024,256]{2,1,0:T(8,128)(2,1)}, bf16[16,1024,256]{2,1,0:T(8,128)(2,1)S(1)}, u32[]{:S(2)}) copy-start(bf16[16,1024,256]{2,1,0:T(8,128)(2,1)S(1)} %convolution_convert_fusion) | copy-start | bytes 25165828
  398.7 33.0 %copy-start.7 = (s32[128,4]{0,1:T(4,128)S(1)}, s32[128,4]{0,1:T(4,128)}, u32[]{:S(2)}) copy-start(s32[128,4]{0,1:T(4,128)} %param.7) | copy-start | bytes 6148
  432.5 11.2 %all-to-all-start.12 = ((f32[16,1,256]{2,1,0:T(1,128)}), f32[16,1,256]{2,1,0:T(1,128)S(1)}, u32[]{:S(2)}, u32[]{:S(2)}) async-start(f32[16,1,256]{2,1,0:T(1,128)} %broadcast_in_dim.38), calls=%async_computation.12 | async-start | bytes 32768 | tf_op jit(solution)/shard_map/all_to_all | solution.py:124
  443.7 26.2 %all-to-all-start.6 = ((bf16[16,128,256]{2,1,0:T(8,128)(2,1)}), bf16[16,128,256]{2,1,0:T(8,128)(2,1)S(1)}, u32[]{:S(2)}, u32[]{:S(2)}) async-start(bf16[16,128,256]{2,1,0:T(8,128)(2,1)} %get-tuple-element.25), calls=%async_computation.6 | async-start | bytes 2097152 | tf_op jit(solution)/shard_map/all_to_all | solution.py:119
  469.9 13.4 %all-to-all-start.11 = ((f32[32,1,128]{2,1,0:T(1,128)}), f32[32,1,128]{2,1,0:T(1,128)S(1)}, u32[]{:S(2)}, u32[]{:S(2)}) async-start(f32[32,1,128]{2,1,0:T(1,128)} %bitcast.36), calls=%async_computation.11 | async-start | bytes 32768 | tf_op jit(solution)/shard_map/all_to_all | solution.py:134
  483.3 54.9 %all-to-all-start.10 = ((bf16[32,128,256]{2,1,0:T(8,128)(2,1)}), bf16[32,128,256]{2,1,0:T(8,128)(2,1)S(1)}, u32[]{:S(2)}, u32[]{:S(2)}) async-start(bf16[32,128,256]{2,1,0:T(8,128)(2,1)} %fusion.20), calls=%async_computation.10 | async-start | bytes 4194304 | tf_op jit(solution)/shard_map/all_to_all | solution.py:139
Sparse Core Ops, SparseCore 0:
  245.6 8.8 all-gather.4
  431.8 8.8 all-gather.6

commit v4 on v3

--- a/solution.py
+++ b/solution.py
@@ -60,9 +60,22 @@
         y = lax.all_gather(y, "lat", axis=1, tiled=False)
         return y.reshape((tokens,) + x.shape[1:])
 
-    acts_fs = lax.all_to_all(
-        acts.reshape(tok_rows, dp_count, fs).transpose(1, 0, 2), "dp", 0, 0, tiled=True
+    id_vals = tok_rows * own_count * 2
+    id_rows = -(-id_vals // fs)
+    id_code = jnp.concatenate([owner_ids // 16, owner_ids % 16], axis=1).astype(BF16).reshape(-1)
+    id_code = jnp.pad(id_code, (0, id_rows * fs - id_vals)).reshape(id_rows, fs)
+    acts_send = jnp.concatenate(
+        [
+            acts.reshape(tok_rows, dp_count, fs).transpose(1, 0, 2),
+            jnp.broadcast_to(id_code[None], (dp_count, id_rows, fs)),
+        ],
+        axis=1,
     )
+    acts_got = lax.all_to_all(acts_send, "dp", 0, 0, tiled=True)
+    acts_fs = acts_got[:, :tok_rows]
+    id_got = acts_got[:, tok_rows:].reshape(dp_count, id_rows * fs)[:, :id_vals]
+    id_got = id_got.astype(jnp.int32).reshape(dp_count, tok_rows, 2, own_count)
+    ids_all = (id_got[:, :, 0] * 16 + id_got[:, :, 1]).reshape(tokens, own_count)
     w_send = (
         weights.reshape(lat_own, lat_count, dp_count, fs)
         .transpose(2, 1, 0, 3)
@@ -70,9 +83,6 @@
     )
     w_fs = lax.all_to_all(w_send, ALL, 0, 0, tiled=True)
 
-    ids_rep = jnp.broadcast_to(owner_ids.astype(F32)[None], (dp_count, tok_rows, own_count))
-    ids_all = lax.all_to_all(ids_rep, "dp", 0, 0, tiled=True).astype(jnp.int32)
-    ids_all = ids_all.reshape(tokens, own_count)
     sel, place = slot_tables(ids_all, owner_total, tok_rows, slot_cap)
 
     def rows_to_slots(x_fs):
@@ -115,13 +125,14 @@
     full = summed + bias_fs[None, None, :]
     err = full - acts_fs.astype(F32)
     gerr = err.astype(BF16)
-    recon = (
-        lax.all_to_all(full.astype(BF16), "dp", 0, 0, tiled=True)
-        .transpose(1, 0, 2)
-        .reshape(tok_rows, half)
+    gdb = jnp.stack(split_hi_lo(jnp.sum(err, axis=(0, 1))))
+    recon_send = jnp.concatenate(
+        [full.astype(BF16), jnp.broadcast_to(gdb[None], (dp_count, 2, fs))], axis=1
     )
-    gdb_rep = jnp.broadcast_to(jnp.sum(err, axis=(0, 1))[None], (dp_count, fs))
-    grad_dec_bias = lax.all_to_all(gdb_rep, "dp", 0, 0, tiled=True).reshape(half)
+    recon_got = lax.all_to_all(recon_send, "dp", 0, 0, tiled=True)
+    recon = recon_got[:, :tok_rows].transpose(1, 0, 2).reshape(tok_rows, half)
+    gdb_got = recon_got[:, tok_rows:].astype(F32)
+    grad_dec_bias = (gdb_got[:, 0] + gdb_got[:, 1]).reshape(half)
 
     gerr_slots = rows_to_slots(gerr)
     gc_part = jnp.einsum("borf,olf->borl", gerr_slots, w_fs, preferred_element_type=F32)
@@ -131,12 +142,20 @@
         my_ids[:, :, None] == jnp.arange(owner_total, dtype=jnp.int32)[None, None, :]
     ).astype(F32)
     genc_part = jnp.sum(own_hit[:, :, :, None] * gpre[:, :, None, :], axis=(0, 1))
-    grad_enc_bias = jnp.sum(lax.all_to_all(genc_part, ALL, 0, 0, tiled=True), axis=0)
 
     gpre_slots = pairs_to_slots(ag_tokens(gpre.astype(BF16)))
     gw = jnp.einsum("borl,borf->olf", codes_slots, gerr_slots, preferred_element_type=F32)
     gw = gw + jnp.einsum("borl,borf->olf", gpre_slots, acts_slots, preferred_element_type=F32)
-    gw_back = lax.all_to_all(gw.astype(BF16), ALL, 0, 0, tiled=True)
+    enc_vals = 2 * lat_own
+    enc_rows = -(-enc_vals // fs)
+    genc = jnp.concatenate(split_hi_lo(genc_part), axis=1)
+    genc = jnp.pad(genc, ((0, 0), (0, enc_rows * fs - enc_vals))).reshape(owner_total, enc_rows, fs)
+    gw_got = lax.all_to_all(
+        jnp.concatenate([gw.astype(BF16), genc], axis=1), ALL, 0, 0, tiled=True
+    )
+    gw_back = gw_got[:, :lat_own]
+    genc_got = gw_got[:, lat_own:].reshape(owner_total, enc_rows * fs)[:, :enc_vals].astype(F32)
+    grad_enc_bias = jnp.sum(genc_got[:, :lat_own] + genc_got[:, lat_own:], axis=0)
     grad_weights = (
         gw_back.reshape(dp_count, lat_count, lat_own, fs)
         .transpose(2, 1, 0, 3)

time: 560 us -> 537 us (0.959)
  waiting for transfers between devices: 161 us -> 146 us
  starting transfers between devices: 40.4 us -> 27.9 us
    all_to_all x6 -> x3, waiting for transfers between devices: 80.5 us -> 67.1 us  [the longest x1 45.5 us: local(): lax.all_to_all(jnp.concatenate([gw.astype(BF16), genc], axis=1), ALL, 0,...]
    all_to_all x6 -> x3, starting transfers between devices: 30.3 us -> 17.7 us  [the longest x1 8.31 us: local(): acts_got = lax.all_to_all(acts_send, 'dp', 0, 0, tiled=True)]
    unnamed x27 -> x32, local copies, waits for them, and re-layouts: 12.9 us -> 16.4 us
    convert_element_type x2 -> x4, other arithmetic: 14.7 us -> 14.3 us  [split_hi_lo(): return (hi.astype(BF16), (x - hi).astype(BF16))]
  transfers between devices with their start and end apart: 10 -> 7, of which waited for: 8 -> 6; matrix products, arithmetic and copies ran while one was open for 10% -> 11% of each run, Pallas kernels for 0% -> 0%
where the time goes in v4:
time: 537 us; the launch traced here: 527 us
  waiting for transfers between devices  146 us (27%)
  blocking collectives  138 us (26%)
  matrix products  97.7 us (18%)
  local copies, waits for them, and re-layouts  52 us (10%)
  other arithmetic  50 us (9%)
  starting transfers between devices  27.9 us (5%)
  between operations  14.7 us (3%)
    all_to_all x2, blocking collectives, ag_tokens(): lax.all_to_all(jnp.broadcast_to(x[None], (dp_count,) + x.shape), 'dp', 0,...  65.3 us
    all_to_all x1, blocking collectives, rs_tokens(): return jnp.sum(lax.all_to_all(y, 'dp', 0, 0, tiled=True), axis=0)  56.2 us
    all_to_all x1, waiting for transfers between devices, local(): lax.all_to_all(jnp.concatenate([gw.astype(BF16), genc], axis=1), ALL, 0,...  45.5 us
    all_to_all x1, waiting for transfers between devices, rs_tokens(): return jnp.sum(lax.all_to_all(y, 'dp', 0, 0, tiled=True), axis=0)  43.2 us
    dot_general x2, matrix products, slots_to_pairs(): out = jnp.einsum('btkq,bql->btkl', sel, both, preferred_element_type=F32)  31.1 us
    all_to_all x1, waiting for transfers between devices, local(): w_fs = lax.all_to_all(w_send, ALL, 0, 0, tiled=True)  27.9 us
    all_to_all x1, waiting for transfers between devices, local(): acts_got = lax.all_to_all(acts_send, 'dp', 0, 0, tiled=True)  21 us
    unnamed x32, local copies, waits for them, and re-layouts  16.4 us
  transfers between devices with their start and end apart: 7, of which 6 were waited for; matrix products, arithmetic and copies ran while one was open for 11% of the time, Pallas kernels for 0%

profile of v4, /device:TPU:0, one launch (start us, length us, event | category | flops | bytes accessed | tf_op | source)
XLA Modules:
  0.0 526.6 jit_solution(13576618143656918797)
XLA Ops:
  10.5 2.2 copy.175
  12.7 8.3 %all-to-all-start = ((bf16[16,132,256]{2,1,0:T(8,128)(2,1)}), bf16[16,132,256]{2,1,0:T(8,128)(2,1)S(1)}, u32[]{:S(2)}, u32[]{:S(2)}) async-start(bf16[16,132,256]{2,1,0:T(8,128)(2,1)} %copy.175), calls=%async_computation | async-start | bytes 2228224 | tf_op jit(solution)/shard_map/all_to_all | solution.py:74
  21.0 2.2 copy.222
  23.2 2.5 copy.183
  25.7 21.0 %all-to-all-done = bf16[16,132,256]{2,1,0:T(8,128)(2,1)S(1)} async-done(((bf16[16,132,256]{2,1,0:T(8,128)(2,1)}), bf16[16,132,256]{2,1,0:T(8,128)(2,1)S(1)}, u32[]{:S(2)}, u32[]{:S(2)}) %all-to-all-start) | async-done | bytes 1081376 | tf_op jit(solution)/shard_map/all_to_all | solution.py:74
  47.8 5.1 all-to-all-start.1
  56.0 2.3 fusion.53
  60.4 4.6 fusion.5
  65.0 1.9 copy-done.1
  66.9 6.8 %convolution_convert_fusion.1 = bf16[16,1024,256]{2,1,0:T(8,128)(2,1)} fusion(bf16[16,128,1024]{1,2,0:T(8,128)(2,1)S(1)} %fusion.5, bf16[16,132,256]{2,1,0:T(8,128)(2,1)} %copy-done.5), kind=kOutput, calls=%fused_computation.32 | convolution fusion | flops 1077936128 | bytes 13631488 | tf_op jit(solution)/shard_map/btq,btf->bqf/dot_general | solution.py:89
  73.7 27.9 %all-to-all-done.1 = bf16[32,128,256]{2,1,0:T(8,128)(2,1)S(1)} async-done(((bf16[32,128,256]{2,1,0:T(8,128)(2,1)}), bf16[32,128,256]{2,1,0:T(8,128)(2,1)S(1)}, u32[]{:S(2)}, u32[]{:S(2)}) %all-to-all-start.1) | async-done | bytes 2097184 | tf_op jit(solution)/shard_map/all_to_all | solution.py:84
  101.6 9.0 %add_bitcast_fusion = f32[16,32,32,128]{3,2,0,1:T(8,128)} fusion(f32[32,128]{1,0:T(8,128)S(1)} %broadcast_select_fusion, bf16[16,32,32,256]{3,2,1,0:T(8,128)(2,1)} %bitcast.119, bf16[32,128,256]{2,1,0:T(8,128)(2,1)S(1)} %all-to-all-done.1), kind=kOutput, calls=%fused_computation.30 | convolution fusion | flops 1075838976 | bytes 18890752 | tf_op jit(solution)/shard_map/borf,olf->borl/dot_general | solution.py:106
  110.6 5.2 copy.185
  115.8 5.4 %reduce-precision_convert_fusion.1 = (bf16[16,1024,128]{2,1,0:T(8,128)(2,1)}, bf16[16,1024,128]{2,1,0:T(8,128)(2,1)}) fusion(f32[16,32,32,128]{3,2,1,0:T(8,128)S(1)} %copy.185), kind=kLoop, calls=%fused_computation.14 | loop fusion | flops 8388608 | bytes 16777216 | tf_op jit(solution)/shard_map/convert_element_type | solution.py:31
  121.1 15.6 %fusion.3 = f32[16,128,4,256]{3,1,2,0:T(8,128)} fusion(s32[16,128,4]{1,2,0:T(4,128)S(1)} %copy.182, bf16[16,1024,128]{2,1,0:T(8,128)(2,1)} %get-tuple-element.35, bf16[16,1024,128]{2,1,0:T(8,128)(2,1)} %get-tuple-element.34), kind=kOutput, calls=%fused_computation.4 | convolution fusion | flops 4320133120 | bytes 16809984 | tf_op jit(solution)/shard_map/btkq,bql->btkl/dot_general | solution.py:96
  136.7 4.2 slice_add_fusion.1
  141.3 8.2 %all_to_all.50 = f32[2,16,64,4,128]{4,2,3,1,0:T(8,128)} all-to-all(f32[2,16,64,4,128]{4,2,3,1,0:T(8,128)S(1)} %bitcast.126), channel_id=1, replica_groups=mesh['dp'=16,'lat'=2] {'lat'}, dimensions={0} | all-to-all | bytes 8388608 | tf_op jit(solution)/shard_map/all_to_all | solution.py:55
  149.4 4.1 reduce_sum.101
  153.5 5.1 all-to-all-start.3
  158.8 43.2 %all-to-all-done.3 = f32[16,64,4,128]{3,1,2,0:T(8,128)} async-done(((f32[16,64,4,128]{3,1,2,0:T(8,128)}), f32[16,64,4,128]{3,1,2,0:T(8,128)}, u32[]{:S(2)}, u32[]{:S(2)}) %all-to-all-start.3) | async-done | bytes 2097184 | tf_op jit(solution)/shard_map/all_to_all | solution.py:56
  202.0 1.7 reduce_sum.102
  205.4 35.8 %all_to_all.51 = bf16[16,64,4,128]{3,1,2,0:T(8,128)(2,1)} all-to-all(bf16[16,64,4,128]{3,1,2,0:T(8,128)(2,1)S(1)} %broadcast_in_dim.36), channel_id=1, replica_groups=mesh['dp'=16,'lat'=2] {'dp'}, dimensions={0} | all-to-all | bytes 2097152 | tf_op jit(solution)/shard_map/all_to_all | solution.py:59
  242.0 8.2 %all-gather.5.cloned.1.call-done = bf16[16,128,4,128]{3,1,2,0:T(8,128)(2,1)} async-done(((bf16[16,64,4,128]{3,1,2,0:T(8,128)(2,1)}), bf16[16,128,4,128]{3,1,2,0:T(8,128)(2,1)}) %all-gather.5.cloned.1.call-update) | async-done | bytes 2097168 | tf_op jit(solution)/shard_map/all_gather | solution.py:60
  250.2 7.3 %bitcast_convert_fusion.1 = bf16[16,1024,128]{2,1,0:T(8,128)(2,1)S(1)} fusion(bf16[16,128,4,128]{3,1,2,0:T(8,128)(2,1)} %all-gather.5.cloned.1.call-done, s32[16,128,4]{1,2,0:T(4,128)S(1)} %copy.182), kind=kOutput, calls=%fused_computation.24 | convolution fusion | flops 2157969408 | bytes 6324224 | tf_op jit(solution)/shard_map/btkq,btkl->bql/dot_general | solution.py:102
  257.5 2.0 copy-done.3
  259.5 5.6 %convert_bitcast_fusion = bf16[16,32,32,256]{3,2,0,1:T(8,128)(2,1)} fusion(bf16[16,32,32,128]{3,2,1,0:T(8,128)(2,1)S(1)} %bitcast.124, bf16[32,128,256]{2,1,0:T(8,128)(2,1)S(1)} %all-to-all-done.1), kind=kOutput, calls=%fused_computation.29 | convolution fusion | flops 1077936128 | bytes 14680064 | tf_op jit(solution)/shard_map/borl,olf->borf/dot_general | solution.py:121
  265.1 8.2 %copy.190 = bf16[16,32,32,256]{3,2,1,0:T(8,128)(2,1)} copy(bf16[16,32,32,256]{3,2,0,1:T(8,128)(2,1)} %convert_bitcast_fusion) | data formatting | bytes 16777216 | tf_op jit(solution)/shard_map/convert_element_type | solution.py:122
  273.3 7.1 %add_convert_fusion = (bf16[16,128,256]{2,1,0:T(8,128)(2,1)}, f32[256]{0:T(256)S(1)}, f32[16,128,256]{2,1,0:T(8,128)}) fusion(f32[256]{0:T(256)S(1)} %dynamic_slice.10, bf16[16,132,256]{2,1,0:T(8,128)(2,1)} %copy-done.5, bf16[16,128,1024]{1,2,0:T(8,128)(2,1)S(1)} %copy-done.2, bf16[16,1024,256]{2,1,0:T(8,128)(2,1)} %bitcast.121), kind=kOutput, calls=%fused_computation.48 | convolution fusion | flops 1076363008 | bytes 16779264 | tf_op jit(solution)/shard_map/btq,bqf->btf/dot_general | solution.py:123
  280.4 4.0 convolution_convert_fusion
  284.4 5.7 %fusion.22 = f32[16,32,32,128]{3,2,0,1:T(8,128)} fusion(bf16[16,32,32,256]{3,2,1,0:T(8,128)(2,1)S(1)} %bitcast.117, bf16[32,128,256]{2,1,0:T(8,128)(2,1)S(1)} %all-to-all-done.1), kind=kOutput, calls=%fused_computation.41 | convolution fusion | flops 1073741824 | bytes 18874368 | tf_op jit(solution)/shard_map/borf,olf->borl/dot_general | solution.py:138
  290.1 8.0 %copy.194 = f32[16,32,32,128]{3,2,1,0:T(8,128)} copy(f32[16,32,32,128]{3,2,0,1:T(8,128)} %fusion.22) | data formatting | bytes 16777216 | tf_op jit(solution)/shard_map/borf,olf->borl/transpose | solution.py:138
  298.1 8.9 %reduce-precision_convert_fusion = (bf16[16,1024,128]{2,1,0:T(8,128)(2,1)}, bf16[16,1024,128]{2,1,0:T(8,128)(2,1)}) fusion(f32[16,32,32,128]{3,2,1,0:T(8,128)} %copy.194), kind=kLoop, calls=%fused_computation.12 | loop fusion | flops 8388608 | bytes 16777216 | tf_op jit(solution)/shard_map/convert_element_type | solution.py:31
  307.0 15.6 %fusion.1 = f32[16,128,4,256]{3,1,2,0:T(8,128)} fusion(s32[16,128,4]{1,2,0:T(4,128)S(1)} %copy.182, bf16[16,1024,128]{2,1,0:T(8,128)(2,1)} %get-tuple-element.33, bf16[16,1024,128]{2,1,0:T(8,128)(2,1)} %get-tuple-element.32), kind=kOutput, calls=%fused_computation.2 | convolution fusion | flops 4320133120 | bytes 16809984 | tf_op jit(solution)/shard_map/btkq,bql->btkl/dot_general | solution.py:96
  322.6 4.2 slice_add_fusion
  327.1 8.1 %all_to_all.52 = f32[2,16,64,4,128]{4,2,3,1,0:T(8,128)} all-to-all(f32[2,16,64,4,128]{4,2,3,1,0:T(8,128)S(1)} %bitcast.127), channel_id=1, replica_groups=mesh['dp'=16,'lat'=2] {'lat'}, dimensions={0} | all-to-all | bytes 8388608 | tf_op jit(solution)/shard_map/all_to_all | solution.py:55
  335.3 2.8 reduce_sum.105
  338.1 56.2 %all_to_all.53 = f32[16,64,4,128]{3,1,2,0:T(8,128)} all-to-all(f32[16,64,4,128]{3,1,2,0:T(8,128)S(1)} %reduce_sum.105), channel_id=1, replica_groups=mesh['dp'=16,'lat'=2] {'dp'}, dimensions={0} | all-to-all | bytes 4194304 | tf_op jit(solution)/shard_map/all_to_all | solution.py:56
  394.3 1.8 reduce_sum.106
  397.8 29.5 %all_to_all.54 = bf16[16,64,4,128]{3,1,2,0:T(8,128)(2,1)} all-to-all(bf16[16,64,4,128]{3,1,2,0:T(8,128)(2,1)S(1)} %broadcast_in_dim.38), channel_id=1, replica_groups=mesh['dp'=16,'lat'=2] {'dp'}, dimensions={0} | all-to-all | bytes 2097152 | tf_op jit(solution)/shard_map/all_to_all | solution.py:59
  428.8 3.9 all-to-all-start.5
  432.7 8.7 %fusion.54 = f32[32,128,256,1]{2,1,0,3:T(8,128)} fusion(bf16[16,32,32,128]{3,2,1,0:T(8,128)(2,1)} %bitcast.125, bf16[16,32,32,256]{3,2,1,0:T(8,128)(2,1)} %bitcast.118), kind=kOutput, calls=%fused_computation.122 | convolution fusion | flops 1073741824 | bytes 16777216 | tf_op jit(solution)/shard_map/borl,borf->olf/dot_general | solution.py:147
  442.9 7.3 %bitcast_convert_fusion = bf16[16,1024,128]{2,1,0:T(8,128)(2,1)S(1)} fusion(bf16[16,128,4,128]{3,1,2,0:T(8,128)(2,1)} %all-gather.7.cloned.1.call-done, s32[16,128,4]{1,2,0:T(4,128)S(1)} %copy.182), kind=kOutput, calls=%fused_computation.23 | convolution fusion | flops 2157969408 | bytes 6324224 | tf_op jit(solution)/shard_map/btkq,btkl->bql/dot_general | solution.py:102
  450.2 5.3 fusion.20
  457.6 5.5 %all-to-all-start.9 = ((bf16[32,129,256]{2,1,0:T(8,128)(2,1)}), bf16[32,129,256]{2,1,0:T(8,128)(2,1)S(1)}, u32[]{:S(2)}, u32[]{:S(2)}) async-start(bf16[32,129,256]{2,1,0:T(8,128)(2,1)} %pad_maximum_fusion), calls=%async_computation.9 | async-start | bytes 4456448 | tf_op jit(solution)/shard_map/all_to_all | solution.py:153
  464.1 2.3 copy.217
  466.4 2.3 copy.202
  469.3 45.5 %all-to-all-done.9 = bf16[32,129,256]{2,1,0:T(8,128)(2,1)S(1)} async-done(((bf16[32,129,256]{2,1,0:T(8,128)(2,1)}), bf16[32,129,256]{2,1,0:T(8,128)(2,1)S(1)}, u32[]{:S(2)}, u32[]{:S(2)}) %all-to-all-start.9) | async-done | bytes 2113568 | tf_op jit(solution)/shard_map/all_to_all | solution.py:153
  516.2 2.7 copy.223
  (82 shorter events, 23.1 us)
Async XLA Ops:
  12.7 34.1 %all-to-all-start = ((bf16[16,132,256]{2,1,0:T(8,128)(2,1)}), bf16[16,132,256]{2,1,0:T(8,128)(2,1)S(1)}, u32[]{:S(2)}, u32[]{:S(2)}) async-start(bf16[16,132,256]{2,1,0:T(8,128)(2,1)} %copy.175), calls=%async_computation | async-start | bytes 2228224 | tf_op jit(solution)/shard_map/all_to_all | solution.py:74
  23.2 29.7 %copy-start.10 = (f32[128]{0:T(128)S(1)}, f32[128]{0:T(128)}, u32[]{:S(2)}) copy-start(f32[128]{0:T(128)} %param.10) | copy-start | bytes 1540
  46.8 1.0 copy-start.5
  47.8 53.8 %all-to-all-start.1 = ((bf16[32,128,256]{2,1,0:T(8,128)(2,1)}), bf16[32,128,256]{2,1,0:T(8,128)(2,1)S(1)}, u32[]{:S(2)}, u32[]{:S(2)}) async-start(bf16[32,128,256]{2,1,0:T(8,128)(2,1)} %bitcast.128), calls=%async_computation.1 | async-start | bytes 4194304 | tf_op jit(solution)/shard_map/all_to_all | solution.py:84
  65.0 1.9 copy-start.1
  149.4 9.3 %copy-start.9 = (s32[128,4]{0,1:T(4,128)S(1)}, s32[128,4]{0,1:T(4,128)}, u32[]{:S(2)}) copy-start(s32[128,4]{0,1:T(4,128)} %param.8) | copy-start | bytes 6148
  153.5 48.4 %all-to-all-start.3 = ((f32[16,64,4,128]{3,1,2,0:T(8,128)}), f32[16,64,4,128]{3,1,2,0:T(8,128)}, u32[]{:S(2)}, u32[]{:S(2)}) async-start(f32[16,64,4,128]{3,1,2,0:T(8,128)} %reduce_sum.101), calls=%async_computation.3 | async-start | bytes 4194304 | tf_op jit(solution)/shard_map/all_to_all | solution.py:56
  158.6 91.6 %all-gather.5.cloned.1.call-start = ((), (), s32[]{:S(2)}) async-start(), calls=%async_computation.10 | async-start | bytes 3145728 | tf_op jit(solution)/shard_map/all_gather | solution.py:60
  241.2 201.7 %all-gather.7.cloned.1.call-start = ((), (), s32[]{:S(2)}) async-start(), calls=%async_computation.11 | async-start | bytes 3145728 | tf_op jit(solution)/shard_map/all_gather | solution.py:60
  257.5 2.1 copy-start.3
  265.1 8.2 %copy-start.2 = (bf16[16,128,1024]{1,2,0:T(8,128)(2,1)S(1)}, bf16[16,128,1024]{1,2,0:T(8,128)(2,1)}, u32[]{:S(2)}) copy-start(bf16[16,128,1024]{1,2,0:T(8,128)(2,1)} %copy-done.1) | copy-start | bytes 12582916
  273.3 7.1 %copy-start.6 = (bf16[16,132,256]{2,1,0:T(8,128)(2,1)S(1)}, bf16[16,132,256]{2,1,0:T(8,128)(2,1)}, u32[]{:S(2)}) copy-start(bf16[16,132,256]{2,1,0:T(8,128)(2,1)} %copy-done.5) | copy-start | bytes 3244036
  284.4 5.7 %copy-start = (bf16[16,1024,256]{2,1,0:T(8,128)(2,1)}, bf16[16,1024,256]{2,1,0:T(8,128)(2,1)S(1)}, u32[]{:S(2)}) copy-start(bf16[16,1024,256]{2,1,0:T(8,128)(2,1)S(1)} %convolution_convert_fusion) | copy-start | bytes 25165828
  394.3 33.1 %copy-start.8 = (s32[128,4]{0,1:T(4,128)S(1)}, s32[128,4]{0,1:T(4,128)}, u32[]{:S(2)}) copy-start(s32[128,4]{0,1:T(4,128)} %param.7) | copy-start | bytes 6148
  394.3 33.4 %copy-start.7 = (bf16[16,128,256]{2,1,0:T(8,128)(2,1)S(1)}, bf16[16,128,256]{2,1,0:T(8,128)(2,1)}, u32[]{:S(2)}) copy-start(bf16[16,128,256]{2,1,0:T(8,128)(2,1)} %get-tuple-element.36) | copy-start | bytes 3145732
  428.8 28.8 %all-to-all-start.5 = ((bf16[16,130,256]{2,1,0:T(8,128)(2,1)}), bf16[16,130,256]{2,1,0:T(8,128)(2,1)S(1)}, u32[]{:S(2)}, u32[]{:S(2)}) async-start(bf16[16,130,256]{2,1,0:T(8,128)(2,1)} %pad_maximum_fusion.2), calls=%async_computation.5 | async-start | bytes 2228224 | tf_op jit(solution)/shard_map/all_to_all | solution.py:132
  442.9 7.3 %copy-start.4 = (f32[32,128,256,1]{2,1,0,3:T(8,128)S(1)}, f32[32,128,256,1]{2,1,0,3:T(8,128)}, u32[]{:S(2)}) copy-start(f32[32,128,256,1]{2,1,0,3:T(8,128)} %fusion.54) | copy-start | bytes 12582916
  457.6 57.2 %all-to-all-start.9 = ((bf16[32,129,256]{2,1,0:T(8,128)(2,1)}), bf16[32,129,256]{2,1,0:T(8,128)(2,1)S(1)}, u32[]{:S(2)}, u32[]{:S(2)}) async-start(bf16[32,129,256]{2,1,0:T(8,128)(2,1)} %pad_maximum_fusion), calls=%async_computation.9 | async-start | bytes 4456448 | tf_op jit(solution)/shard_map/all_to_all | solution.py:153
Sparse Core Ops, SparseCore 0:
  241.3 8.8 all-gather.4
  427.5 8.8 all-gather.6

commit v5 on v4

--- a/solution.py
+++ b/solution.py
@@ -64,24 +64,27 @@
     id_rows = -(-id_vals // fs)
     id_code = jnp.concatenate([owner_ids // 16, owner_ids % 16], axis=1).astype(BF16).reshape(-1)
     id_code = jnp.pad(id_code, (0, id_rows * fs - id_vals)).reshape(id_rows, fs)
+    w_dp = (
+        weights.reshape(lat_own, lat_count, dp_count, fs)
+        .transpose(2, 1, 0, 3)
+        .reshape(dp_count, lat_count * lat_own, fs)
+    )
     acts_send = jnp.concatenate(
         [
             acts.reshape(tok_rows, dp_count, fs).transpose(1, 0, 2),
             jnp.broadcast_to(id_code[None], (dp_count, id_rows, fs)),
+            w_dp,
         ],
         axis=1,
     )
     acts_got = lax.all_to_all(acts_send, "dp", 0, 0, tiled=True)
     acts_fs = acts_got[:, :tok_rows]
-    id_got = acts_got[:, tok_rows:].reshape(dp_count, id_rows * fs)[:, :id_vals]
+    w_got = acts_got[:, tok_rows + id_rows :].reshape(dp_count, lat_count, lat_own, fs)
+    w_got = lax.all_to_all(w_got.transpose(1, 0, 2, 3), "lat", 0, 0, tiled=True)
+    w_fs = w_got.transpose(1, 0, 2, 3).reshape(owner_total, lat_own, fs)
+    id_got = acts_got[:, tok_rows : tok_rows + id_rows].reshape(dp_count, id_rows * fs)[:, :id_vals]
     id_got = id_got.astype(jnp.int32).reshape(dp_count, tok_rows, 2, own_count)
     ids_all = (id_got[:, :, 0] * 16 + id_got[:, :, 1]).reshape(tokens, own_count)
-    w_send = (
-        weights.reshape(lat_own, lat_count, dp_count, fs)
-        .transpose(2, 1, 0, 3)
-        .reshape(owner_total, lat_own, fs)
-    )
-    w_fs = lax.all_to_all(w_send, ALL, 0, 0, tiled=True)
 
     sel, place = slot_tables(ids_all, owner_total, tok_rows, slot_cap)
 

time: 537 us -> 571 us (1.063)
  waiting for transfers between devices: 146 us -> 159 us
  local copies, waits for them, and re-layouts: 52 us -> 60.6 us
    all_to_all x1, waiting for transfers between devices: 21 us -> 62 us  [local(): acts_got = lax.all_to_all(acts_send, 'dp', 0, 0, tiled=True)]
    all_to_all x1 -> x0, waiting for transfers between devices: 27.9 us -> none  [local(): w_fs = lax.all_to_all(w_send, ALL, 0, 0, tiled=True)]
    all_to_all x1, starting transfers between devices: 5.07 us -> 15.3 us  [rs_tokens(): return jnp.sum(lax.all_to_all(y, 'dp', 0, 0, tiled=True), axis=0)]
    unnamed x32 -> x36, local copies, waits for them, and re-layouts: 16.4 us -> 15.5 us
  transfers between devices with their start and end apart: 7 -> 6, of which waited for: 6 -> 5; matrix products, arithmetic and copies ran while one was open for 11% -> 6% of each run, Pallas kernels for 0% -> 0%
where the time goes in v5:
time: 571 us; the launch traced here: 562 us
  waiting for transfers between devices  159 us (28%)
  blocking collectives  143 us (25%)
  matrix products  95.6 us (17%)
  local copies, waits for them, and re-layouts  60.6 us (11%)
  other arithmetic  55.3 us (10%)
  starting transfers between devices  33.3 us (6%)
  between operations  14.7 us (3%)
    all_to_all x2, blocking collectives, ag_tokens(): lax.all_to_all(jnp.broadcast_to(x[None], (dp_count,) + x.shape), 'dp', 0,...  65.3 us
    all_to_all x1, waiting for transfers between devices, local(): acts_got = lax.all_to_all(acts_send, 'dp', 0, 0, tiled=True)  62 us
    all_to_all x1, blocking collectives, rs_tokens(): return jnp.sum(lax.all_to_all(y, 'dp', 0, 0, tiled=True), axis=0)  56 us
    all_to_all x1, waiting for transfers between devices, local(): lax.all_to_all(jnp.concatenate([gw.astype(BF16), genc], axis=1), ALL, 0,...  45.5 us
    all_to_all x1, waiting for transfers between devices, rs_tokens(): return jnp.sum(lax.all_to_all(y, 'dp', 0, 0, tiled=True), axis=0)  43.1 us
    dot_general x2, matrix products, slots_to_pairs(): out = jnp.einsum('btkq,bql->btkl', sel, both, preferred_element_type=F32)  31.5 us
    convert_element_type x4, other arithmetic, split_hi_lo(): return (hi.astype(BF16), (x - hi).astype(BF16))  17.4 us
    all_to_all x2, blocking collectives, rs_tokens(): y = jnp.sum(lax.all_to_all(y, 'lat', 0, 0, tiled=True), axis=0)  16.3 us
  transfers between devices with their start and end apart: 6, of which 5 were waited for; matrix products, arithmetic and copies ran while one was open for 6% of the time, Pallas kernels for 0%

profile of v5, /device:TPU:0, one launch (start us, length us, event | category | flops | bytes accessed | tf_op | source)
XLA Modules:
  0.0 561.9 jit_solution(14062937731010848855)
XLA Ops:
  8.1 2.3 copy.225
  14.4 2.5 pad_maximum_fusion
  16.9 8.4 %all-to-all-start = ((bf16[16,388,256]{2,1,0:T(8,128)(2,1)}), bf16[16,388,256]{2,1,0:T(8,128)(2,1)S(1)}, u32[]{:S(2)}, u32[]{:S(2)}) async-start(bf16[16,388,256]{2,1,0:T(8,128)(2,1)} %pad_maximum_fusion), calls=%async_computation | async-start | bytes 6422528 | tf_op jit(solution)/shard_map/all_to_all | solution.py:80
  25.5 62.0 %all-to-all-done = bf16[16,388,256]{2,1,0:T(8,128)(2,1)S(1)} async-done(((bf16[16,388,256]{2,1,0:T(8,128)(2,1)}), bf16[16,388,256]{2,1,0:T(8,128)(2,1)S(1)}, u32[]{:S(2)}, u32[]{:S(2)}) %all-to-all-start) | async-done | bytes 3178528 | tf_op jit(solution)/shard_map/all_to_all | solution.py:80
  88.7 1.8 fusion.49
  93.1 2.3 copy.186
  95.5 2.3 fusion.50
  97.8 2.4 copy.187
  102.2 4.6 fusion.5
  106.8 3.9 slice.71
  111.0 5.4 all_to_all.50
  117.8 3.5 convolution_convert_fusion.1
  121.4 8.7 %add_bitcast_fusion = f32[16,32,32,128]{3,2,0,1:T(8,128)} fusion(f32[32,128]{1,0:T(8,128)S(1)} %broadcast_select_fusion, bf16[32,128,256,1]{2,1,3,0:T(8,128)(2,1)} %bitcast.126, bf16[16,32,32,256]{3,2,1,0:T(8,128)(2,1)S(1)} %bitcast.123), kind=kOutput, calls=%fused_computation.30 | convolution fusion | flops 1075838976 | bytes 18890752 | tf_op jit(solution)/shard_map/borf,olf->borl/dot_general | solution.py:109
  130.1 8.0 %copy.192 = f32[16,32,32,128]{3,2,1,0:T(8,128)} copy(f32[16,32,32,128]{3,2,0,1:T(8,128)} %add_bitcast_fusion) | data formatting | bytes 16777216 | tf_op jit(solution)/shard_map/add | solution.py:113
  138.2 8.7 %reduce-precision_convert_fusion.1 = (bf16[16,1024,128]{2,1,0:T(8,128)(2,1)}, bf16[16,1024,128]{2,1,0:T(8,128)(2,1)}) fusion(f32[16,32,32,128]{3,2,1,0:T(8,128)} %copy.192), kind=kLoop, calls=%fused_computation.14 | loop fusion | flops 8388608 | bytes 16777216 | tf_op jit(solution)/shard_map/convert_element_type | solution.py:31
  146.9 15.8 %fusion.3 = f32[16,128,4,256]{3,1,2,0:T(8,128)} fusion(s32[16,128,4]{1,2,0:T(4,128)S(1)} %copy.188, bf16[16,1024,128]{2,1,0:T(8,128)(2,1)} %get-tuple-element.35, bf16[16,1024,128]{2,1,0:T(8,128)(2,1)} %get-tuple-element.34), kind=kOutput, calls=%fused_computation.4 | convolution fusion | flops 4320133120 | bytes 16809984 | tf_op jit(solution)/shard_map/btkq,bql->btkl/dot_general | solution.py:99
  162.6 4.2 slice_add_fusion.1
  167.2 8.2 %all_to_all.51 = f32[2,16,64,4,128]{4,2,3,1,0:T(8,128)} all-to-all(f32[2,16,64,4,128]{4,2,3,1,0:T(8,128)S(1)} %bitcast.131), channel_id=1, replica_groups=mesh['dp'=16,'lat'=2] {'lat'}, dimensions={0} | all-to-all | bytes 8388608 | tf_op jit(solution)/shard_map/all_to_all | solution.py:55
  175.4 4.1 reduce_sum.101
  179.5 15.3 %all-to-all-start.3 = ((f32[16,64,4,128]{3,1,2,0:T(8,128)}), f32[16,64,4,128]{3,1,2,0:T(8,128)S(1)}, u32[]{:S(2)}, u32[]{:S(2)}) async-start(f32[16,64,4,128]{3,1,2,0:T(8,128)} %reduce_sum.101), calls=%async_computation.3 | async-start | bytes 4194304 | tf_op jit(solution)/shard_map/all_to_all | solution.py:56
  195.0 43.1 %all-to-all-done.3 = f32[16,64,4,128]{3,1,2,0:T(8,128)S(1)} async-done(((f32[16,64,4,128]{3,1,2,0:T(8,128)}), f32[16,64,4,128]{3,1,2,0:T(8,128)S(1)}, u32[]{:S(2)}, u32[]{:S(2)}) %all-to-all-start.3) | async-done | bytes 2097184 | tf_op jit(solution)/shard_map/all_to_all | solution.py:56
  239.9 35.8 %all_to_all.52 = bf16[16,64,4,128]{3,1,2,0:T(8,128)(2,1)} all-to-all(bf16[16,64,4,128]{3,1,2,0:T(8,128)(2,1)S(1)} %broadcast_in_dim.36), channel_id=1, replica_groups=mesh['dp'=16,'lat'=2] {'dp'}, dimensions={0} | all-to-all | bytes 2097152 | tf_op jit(solution)/shard_map/all_to_all | solution.py:59
  276.5 8.2 %all-gather.5.cloned.1.call-done = bf16[16,128,4,128]{3,1,2,0:T(8,128)(2,1)} async-done(((bf16[16,64,4,128]{3,1,2,0:T(8,128)(2,1)}), bf16[16,128,4,128]{3,1,2,0:T(8,128)(2,1)}) %all-gather.5.cloned.1.call-update) | async-done | bytes 2097168 | tf_op jit(solution)/shard_map/all_gather | solution.py:60
  284.7 7.5 %bitcast_convert_fusion.1 = bf16[16,1024,128]{2,1,0:T(8,128)(2,1)S(1)} fusion(bf16[16,128,4,128]{3,1,2,0:T(8,128)(2,1)} %all-gather.5.cloned.1.call-done, s32[16,128,4]{1,2,0:T(4,128)S(1)} %copy.188), kind=kOutput, calls=%fused_computation.24 | convolution fusion | flops 2157969408 | bytes 6324224 | tf_op jit(solution)/shard_map/btkq,btkl->bql/dot_general | solution.py:105
  292.3 2.0 copy-done.7
  294.3 5.5 convert_bitcast_fusion
  299.9 8.2 %copy.197 = bf16[16,32,32,256]{3,2,1,0:T(8,128)(2,1)} copy(bf16[16,32,32,256]{3,2,0,1:T(8,128)(2,1)} %convert_bitcast_fusion) | data formatting | bytes 16777216 | tf_op jit(solution)/shard_map/convert_element_type | solution.py:125
  308.0 5.2 add_convert_fusion
  313.2 3.6 convolution_convert_fusion
  316.9 8.7 %fusion.22 = f32[16,32,32,128]{3,2,0,1:T(8,128)} fusion(bf16[32,128,256,1]{2,1,3,0:T(8,128)(2,1)} %bitcast.127, bf16[16,32,32,256]{3,2,1,0:T(8,128)(2,1)S(1)} %bitcast.121), kind=kOutput, calls=%fused_computation.42 | convolution fusion | flops 1073741824 | bytes 18874368 | tf_op jit(solution)/shard_map/borf,olf->borl/dot_general | solution.py:141
  325.6 8.0 %copy.201 = f32[16,32,32,128]{3,2,1,0:T(8,128)} copy(f32[16,32,32,128]{3,2,0,1:T(8,128)} %fusion.22) | data formatting | bytes 16777216 | tf_op jit(solution)/shard_map/borf,olf->borl/transpose | solution.py:141
  333.6 8.7 %reduce-precision_convert_fusion = (bf16[16,1024,128]{2,1,0:T(8,128)(2,1)}, bf16[16,1024,128]{2,1,0:T(8,128)(2,1)}) fusion(f32[16,32,32,128]{3,2,1,0:T(8,128)} %copy.201), kind=kLoop, calls=%fused_computation.12 | loop fusion | flops 8388608 | bytes 16777216 | tf_op jit(solution)/shard_map/convert_element_type | solution.py:31
  342.3 15.7 %fusion.1 = f32[16,128,4,256]{3,1,2,0:T(8,128)} fusion(s32[16,128,4]{1,2,0:T(4,128)S(1)} %copy.188, bf16[16,1024,128]{2,1,0:T(8,128)(2,1)} %get-tuple-element.33, bf16[16,1024,128]{2,1,0:T(8,128)(2,1)} %get-tuple-element.32), kind=kOutput, calls=%fused_computation.2 | convolution fusion | flops 4320133120 | bytes 16809984 | tf_op jit(solution)/shard_map/btkq,bql->btkl/dot_general | solution.py:99
  358.0 4.2 slice_add_fusion
  362.6 8.1 %all_to_all.53 = f32[2,16,64,4,128]{4,2,3,1,0:T(8,128)} all-to-all(f32[2,16,64,4,128]{4,2,3,1,0:T(8,128)S(1)} %bitcast.132), channel_id=1, replica_groups=mesh['dp'=16,'lat'=2] {'lat'}, dimensions={0} | all-to-all | bytes 8388608 | tf_op jit(solution)/shard_map/all_to_all | solution.py:55
  370.7 2.8 reduce_sum.105
  373.5 56.0 %all_to_all.54 = f32[16,64,4,128]{3,1,2,0:T(8,128)} all-to-all(f32[16,64,4,128]{3,1,2,0:T(8,128)S(1)} %reduce_sum.105), channel_id=1, replica_groups=mesh['dp'=16,'lat'=2] {'dp'}, dimensions={0} | all-to-all | bytes 4194304 | tf_op jit(solution)/shard_map/all_to_all | solution.py:56
  429.5 1.7 reduce_sum.106
  433.0 29.5 %all_to_all.55 = bf16[16,64,4,128]{3,1,2,0:T(8,128)(2,1)} all-to-all(bf16[16,64,4,128]{3,1,2,0:T(8,128)(2,1)S(1)} %broadcast_in_dim.38), channel_id=1, replica_groups=mesh['dp'=16,'lat'=2] {'dp'}, dimensions={0} | all-to-all | bytes 2097152 | tf_op jit(solution)/shard_map/all_to_all | solution.py:59
  463.9 3.9 all-to-all-start.5
  467.8 8.7 %fusion.51 = f32[32,128,256,1]{2,1,0,3:T(8,128)} fusion(bf16[16,32,32,128]{3,2,1,0:T(8,128)(2,1)} %bitcast.143, bf16[16,32,32,256]{3,2,1,0:T(8,128)(2,1)} %bitcast.122), kind=kOutput, calls=%fused_computation.120 | convolution fusion | flops 1073741824 | bytes 16777216 | tf_op jit(solution)/shard_map/borl,borf->olf/dot_general | solution.py:150
  478.0 7.3 %bitcast_convert_fusion = bf16[16,1024,128]{2,1,0:T(8,128)(2,1)S(1)} fusion(bf16[16,128,4,128]{3,1,2,0:T(8,128)(2,1)} %all-gather.7.cloned.1.call-done, s32[16,128,4]{1,2,0:T(4,128)S(1)} %copy.188), kind=kOutput, calls=%fused_computation.23 | convolution fusion | flops 2157969408 | bytes 6324224 | tf_op jit(solution)/shard_map/btkq,btkl->bql/dot_general | solution.py:105
  485.3 5.3 fusion.20
  492.7 5.6 all-to-all-start.9
  499.4 2.3 copy.224
  501.6 2.3 copy.209
  504.5 45.5 %all-to-all-done.9 = bf16[32,129,256]{2,1,0:T(8,128)(2,1)S(1)} async-done(((bf16[32,129,256]{2,1,0:T(8,128)(2,1)}), bf16[32,129,256]{2,1,0:T(8,128)(2,1)S(1)}, u32[]{:S(2)}, u32[]{:S(2)}) %all-to-all-start.9) | async-done | bytes 2113568 | tf_op jit(solution)/shard_map/all_to_all | solution.py:156
  551.5 2.7 copy.230
  (87 shorter events, 26.4 us)
Async XLA Ops:
  8.1 3.5 copy-start.8
  16.9 8.5 %copy-start.12 = (f32[128]{0:T(128)S(1)}, f32[128]{0:T(128)}, u32[]{:S(2)}) copy-start(f32[128]{0:T(128)} %param.10) | copy-start | bytes 1540
  16.9 70.5 %all-to-all-start = ((bf16[16,388,256]{2,1,0:T(8,128)(2,1)}), bf16[16,388,256]{2,1,0:T(8,128)(2,1)S(1)}, u32[]{:S(2)}, u32[]{:S(2)}) async-start(bf16[16,388,256]{2,1,0:T(8,128)(2,1)} %pad_maximum_fusion), calls=%async_computation | async-start | bytes 6422528 | tf_op jit(solution)/shard_map/all_to_all | solution.py:80
  87.4 13.8 %copy-start.4 = (bf16[16,388,256]{2,1,0:T(8,128)(2,1)}, bf16[16,388,256]{2,1,0:T(8,128)(2,1)S(1)}, u32[]{:S(2)}) copy-start(bf16[16,388,256]{2,1,0:T(8,128)(2,1)S(1)} %all-to-all-done) | copy-start | bytes 9535492
  91.6 0.6 copy-start.9
  106.8 11.0 %copy-start.2 = (bf16[16,128,1024]{1,2,0:T(8,128)(2,1)}, bf16[16,128,1024]{1,2,0:T(8,128)(2,1)S(1)}, u32[]{:S(2)}) copy-start(bf16[16,128,1024]{1,2,0:T(8,128)(2,1)S(1)} %fusion.5) | copy-start | bytes 12582916
  121.4 8.7 %copy-start.1 = (bf16[16,1024,256]{2,1,0:T(8,128)(2,1)}, bf16[16,1024,256]{2,1,0:T(8,128)(2,1)S(1)}, u32[]{:S(2)}) copy-start(bf16[16,1024,256]{2,1,0:T(8,128)(2,1)S(1)} %convolution_convert_fusion.1) | copy-start | bytes 25165828
  175.4 19.5 %copy-start.11 = (s32[128,4]{0,1:T(4,128)S(1)}, s32[128,4]{0,1:T(4,128)}, u32[]{:S(2)}) copy-start(s32[128,4]{0,1:T(4,128)} %param.8) | copy-start | bytes 6148
  179.5 58.6 %all-to-all-start.3 = ((f32[16,64,4,128]{3,1,2,0:T(8,128)}), f32[16,64,4,128]{3,1,2,0:T(8,128)S(1)}, u32[]{:S(2)}, u32[]{:S(2)}) async-start(f32[16,64,4,128]{3,1,2,0:T(8,128)} %reduce_sum.101), calls=%async_computation.3 | async-start | bytes 4194304 | tf_op jit(solution)/shard_map/all_to_all | solution.py:56
  194.8 89.9 %all-gather.5.cloned.1.call-start = ((), (), s32[]{:S(2)}) async-start(), calls=%async_computation.10 | async-start | bytes 3145728 | tf_op jit(solution)/shard_map/all_gather | solution.py:60
  275.7 202.3 %all-gather.7.cloned.1.call-start = ((), (), s32[]{:S(2)}) async-start(), calls=%async_computation.11 | async-start | bytes 3145728 | tf_op jit(solution)/shard_map/all_gather | solution.py:60
  276.5 17.8 %copy-start.5 = (bf16[16,2,128,256]{3,2,1,0:T(8,128)(2,1)S(1)}, bf16[16,2,128,256]{3,2,1,0:T(8,128)(2,1)}, u32[]{:S(2)}) copy-start(bf16[16,2,128,256]{3,2,1,0:T(8,128)(2,1)} %copy.190) | copy-start | bytes 6291460
  292.3 2.1 copy-start.7
  299.9 8.2 %copy-start.3 = (bf16[16,128,1024]{1,2,0:T(8,128)(2,1)S(1)}, bf16[16,128,1024]{1,2,0:T(8,128)(2,1)}, u32[]{:S(2)}) copy-start(bf16[16,128,1024]{1,2,0:T(8,128)(2,1)} %copy-done.2) | copy-start | bytes 12582916
  316.9 8.7 %copy-start = (bf16[16,1024,256]{2,1,0:T(8,128)(2,1)}, bf16[16,1024,256]{2,1,0:T(8,128)(2,1)S(1)}, u32[]{:S(2)}) copy-start(bf16[16,1024,256]{2,1,0:T(8,128)(2,1)S(1)} %convolution_convert_fusion) | copy-start | bytes 25165828
  429.5 33.0 %copy-start.10 = (s32[128,4]{0,1:T(4,128)S(1)}, s32[128,4]{0,1:T(4,128)}, u32[]{:S(2)}) copy-start(s32[128,4]{0,1:T(4,128)} %param.7) | copy-start | bytes 6148
  463.9 28.8 %all-to-all-start.5 = ((bf16[16,130,256]{2,1,0:T(8,128)(2,1)}), bf16[16,130,256]{2,1,0:T(8,128)(2,1)S(1)}, u32[]{:S(2)}, u32[]{:S(2)}) async-start(bf16[16,130,256]{2,1,0:T(8,128)(2,1)} %pad_maximum_fusion.2), calls=%async_computation.5 | async-start | bytes 2228224 | tf_op jit(solution)/shard_map/all_to_all | solution.py:135
  478.0 7.3 %copy-start.6 = (f32[32,128,256,1]{2,1,0,3:T(8,128)S(1)}, f32[32,128,256,1]{2,1,0,3:T(8,128)}, u32[]{:S(2)}) copy-start(f32[32,128,256,1]{2,1,0,3:T(8,128)} %fusion.51) | copy-start | bytes 12582916
  492.7 57.3 %all-to-all-start.9 = ((bf16[32,129,256]{2,1,0:T(8,128)(2,1)}), bf16[32,129,256]{2,1,0:T(8,128)(2,1)S(1)}, u32[]{:S(2)}, u32[]{:S(2)}) async-start(bf16[32,129,256]{2,1,0:T(8,128)(2,1)} %pad_maximum_fusion.1), calls=%async_computation.9 | async-start | bytes 4456448 | tf_op jit(solution)/shard_map/all_to_all | solution.py:156
Sparse Core Ops, SparseCore 0:
  275.8 8.8 all-gather.4
  462.6 8.8 all-gather.6

commit v6 on v4

--- a/solution.py
+++ b/solution.py
@@ -1,10 +1,11 @@
 import jax
 import jax.numpy as jnp
 from jax import lax
-from jax.sharding import PartitionSpec as P
+from jax.sharding import Mesh, PartitionSpec as P
 
 BLK_DEV = 2
-ALL = ("dp", "lat")
+DP = ("dh", "dl")
+ALL = ("dh", "dl", "lat")
 F32 = jnp.float32
 BF16 = jnp.bfloat16
 
@@ -32,9 +33,11 @@
 
 
 def local(acts, owner_ids, block_codes, weights, enc_bias, dec_bias):
-    dp_count = lax.axis_size("dp")
+    dp_count = lax.axis_size(DP)
+    dh_count = lax.axis_size("dh")
+    dl_count = lax.axis_size("dl")
     lat_count = lax.axis_size("lat")
-    dp_idx = lax.axis_index("dp")
+    dp_idx = lax.axis_index("dh") * dl_count + lax.axis_index("dl")
     lat_idx = lax.axis_index("lat")
     me = dp_idx * lat_count + lat_idx
     owner_total = dp_count * lat_count
@@ -53,10 +56,16 @@
         tail = x.shape[1:]
         y = x.reshape((dp_count, lat_count, mine_rows) + tail).swapaxes(0, 1)
         y = jnp.sum(lax.all_to_all(y, "lat", 0, 0, tiled=True), axis=0)
-        return jnp.sum(lax.all_to_all(y, "dp", 0, 0, tiled=True), axis=0)
+        y = y.reshape((dh_count, dl_count) + y.shape[1:]).swapaxes(0, 1)
+        y = jnp.sum(lax.all_to_all(y, "dl", 0, 0, tiled=True), axis=0)
+        return jnp.sum(lax.all_to_all(y, "dh", 0, 0, tiled=True), axis=0)
 
     def ag_tokens(x):
-        y = lax.all_to_all(jnp.broadcast_to(x[None], (dp_count,) + x.shape), "dp", 0, 0, tiled=True)
+        y = lax.all_to_all(jnp.broadcast_to(x[None], (dh_count,) + x.shape), "dh", 0, 0, tiled=True)
+        y = lax.all_to_all(
+            jnp.broadcast_to(y[None], (dl_count,) + y.shape), "dl", 0, 0, tiled=True
+        ).swapaxes(0, 1)
+        y = y.reshape((dp_count,) + x.shape)
         y = lax.all_gather(y, "lat", axis=1, tiled=False)
         return y.reshape((tokens,) + x.shape[1:])
 
@@ -71,7 +80,7 @@
         ],
         axis=1,
     )
-    acts_got = lax.all_to_all(acts_send, "dp", 0, 0, tiled=True)
+    acts_got = lax.all_to_all(acts_send, DP, 0, 0, tiled=True)
     acts_fs = acts_got[:, :tok_rows]
     id_got = acts_got[:, tok_rows:].reshape(dp_count, id_rows * fs)[:, :id_vals]
     id_got = id_got.astype(jnp.int32).reshape(dp_count, tok_rows, 2, own_count)
@@ -129,7 +138,7 @@
     recon_send = jnp.concatenate(
         [full.astype(BF16), jnp.broadcast_to(gdb[None], (dp_count, 2, fs))], axis=1
     )
-    recon_got = lax.all_to_all(recon_send, "dp", 0, 0, tiled=True)
+    recon_got = lax.all_to_all(recon_send, DP, 0, 0, tiled=True)
     recon = recon_got[:, :tok_rows].transpose(1, 0, 2).reshape(tok_rows, half)
     gdb_got = recon_got[:, tok_rows:].astype(F32)
     grad_dec_bias = (gdb_got[:, 0] + gdb_got[:, 1]).reshape(half)
@@ -165,13 +174,16 @@
 
 
 def solution(mesh):
+    dp_count, lat_count = mesh.devices.shape
+    halves = 2 if dp_count % 2 == 0 else 1
+    split = Mesh(mesh.devices.reshape(halves, dp_count // halves, lat_count), ("dh", "dl", "lat"))
     in_specs = (
-        P("dp", "lat"),
-        P("dp", None),
-        P("dp", None),
-        P(("dp", "lat"), None),
-        P(("dp", "lat")),
+        P(DP, "lat"),
+        P(DP, None),
+        P(DP, None),
+        P(ALL, None),
+        P(ALL),
         P("lat"),
     )
-    out_specs = (P("dp", "lat"), P(("dp", "lat"), None), P(("dp", "lat")), P("lat"))
-    return jax.shard_map(local, mesh=mesh, in_specs=in_specs, out_specs=out_specs, check_vma=False)
+    out_specs = (P(DP, "lat"), P(ALL, None), P(ALL), P("lat"))
+    return jax.shard_map(local, mesh=split, in_specs=in_specs, out_specs=out_specs, check_vma=False)

time: 537 us -> 499 us (0.929); the launches traced: 527 us -> 494 us
  waiting for transfers between devices: 146 us -> 109 us
  local copies, waits for them, and re-layouts: 52 us -> 62 us
    all_to_all x3, waiting for transfers between devices: 64.8 us -> 28.7 us  [the longest x1 21 us: local(): acts_got = lax.all_to_all(acts_send, DP, 0, 0, tiled=True)]
    all_to_all x3 -> x7, blocking collectives: 121 us -> 121 us  [the longest x2 61.2 us: rs_tokens(): y = jnp.sum(lax.all_to_all(y, 'dl', 0, 0, tiled=True), axis=0)]
  transfers between devices with their start and end apart: 7 -> 7, of which waited for: 6 -> 5; matrix products, arithmetic and copies ran while one was open for 11% -> 11% of each run, Pallas kernels for 0% -> 0%
where the time goes in v6:
time: 499 us; the launch traced here: 494 us
  blocking collectives  138 us (28%)
  waiting for transfers between devices  109 us (22%)
  matrix products  94.3 us (19%)
  local copies, waits for them, and re-layouts  62 us (12%)
  other arithmetic  50 us (10%)
  starting transfers between devices  26.8 us (5%)
  between operations  14.8 us (3%)
    all_to_all x2, blocking collectives, rs_tokens(): y = jnp.sum(lax.all_to_all(y, 'dl', 0, 0, tiled=True), axis=0)  61.2 us
    all_to_all x1, waiting for transfers between devices, local(): lax.all_to_all(jnp.concatenate([gw.astype(BF16), genc], axis=1), ALL, 0,...  45.5 us
    all_to_all x2, blocking collectives, ag_tokens(): lax.all_to_all(jnp.broadcast_to(y[None], (dl_count,) + y.shape), 'dl', 0,...  31.7 us
    dot_general x2, matrix products, slots_to_pairs(): out = jnp.einsum('btkq,bql->btkl', sel, both, preferred_element_type=F32)  31.1 us
    all_to_all x1, waiting for transfers between devices, local(): w_fs = lax.all_to_all(w_send, ALL, 0, 0, tiled=True)  27.9 us
    all_to_all x1, waiting for transfers between devices, local(): acts_got = lax.all_to_all(acts_send, DP, 0, 0, tiled=True)  21 us
    all_to_all x2, blocking collectives, rs_tokens(): y = jnp.sum(lax.all_to_all(y, 'lat', 0, 0, tiled=True), axis=0)  16.8 us
    all_to_all x2, blocking collectives, ag_tokens(): lax.all_to_all(jnp.broadcast_to(x[None], (dh_count,) + x.shape), 'dh', 0,...  16.7 us
  transfers between devices with their start and end apart: 7, of which 5 were waited for; matrix products, arithmetic and copies ran while one was open for 11% of the time, Pallas kernels for 0%

profile of v6, /device:TPU:0, one launch (start us, length us, event | category | flops | bytes accessed | tf_op | source)
XLA Modules:
  0.0 494.0 jit_solution(761110372035943757)
XLA Ops:
  12.7 8.3 %all-to-all-start = ((bf16[16,132,256]{2,1,0:T(8,128)(2,1)}), bf16[16,132,256]{2,1,0:T(8,128)(2,1)S(1)}, u32[]{:S(2)}, u32[]{:S(2)}) async-start(bf16[16,132,256]{2,1,0:T(8,128)(2,1)} %copy.265), calls=%async_computation | async-start | bytes 2228224 | tf_op jit(solution)/shard_map/all_to_all | solution.py:83
  23.2 2.5 copy.273
  25.7 21.0 %all-to-all-done = bf16[16,132,256]{2,1,0:T(8,128)(2,1)S(1)} async-done(((bf16[16,132,256]{2,1,0:T(8,128)(2,1)}), bf16[16,132,256]{2,1,0:T(8,128)(2,1)S(1)}, u32[]{:S(2)}, u32[]{:S(2)}) %all-to-all-start) | async-done | bytes 1081376 | tf_op jit(solution)/shard_map/all_to_all | solution.py:83
  47.8 5.1 %all-to-all-start.1 = ((bf16[32,128,256]{2,1,0:T(8,128)(2,1)}), bf16[32,128,256]{2,1,0:T(8,128)(2,1)S(1)}, u32[]{:S(2)}, u32[]{:S(2)}) async-start(bf16[32,128,256]{2,1,0:T(8,128)(2,1)} %bitcast.146), calls=%async_computation.1 | async-start | bytes 4194304 | tf_op jit(solution)/shard_map/all_to_all | solution.py:93
  56.0 2.3 fusion.55
  60.4 4.6 fusion.5
  67.0 6.8 %convolution_convert_fusion.1 = bf16[16,1024,256]{2,1,0:T(8,128)(2,1)} fusion(bf16[16,128,1024]{1,2,0:T(8,128)(2,1)S(1)} %fusion.5, bf16[16,132,256]{2,1,0:T(8,128)(2,1)} %copy-done.5), kind=kOutput, calls=%fused_computation.32 | convolution fusion | flops 1077936128 | bytes 13631488 | tf_op jit(solution)/shard_map/btq,btf->bqf/dot_general | solution.py:98
  73.7 27.9 %all-to-all-done.1 = bf16[32,128,256]{2,1,0:T(8,128)(2,1)S(1)} async-done(((bf16[32,128,256]{2,1,0:T(8,128)(2,1)}), bf16[32,128,256]{2,1,0:T(8,128)(2,1)S(1)}, u32[]{:S(2)}, u32[]{:S(2)}) %all-to-all-start.1) | async-done | bytes 2097184 | tf_op jit(solution)/shard_map/all_to_all | solution.py:93
  101.6 8.9 %add_bitcast_fusion = f32[16,32,32,128]{3,2,0,1:T(8,128)} fusion(f32[32,128]{1,0:T(8,128)S(1)} %broadcast_select_fusion, bf16[16,32,32,256]{3,2,1,0:T(8,128)(2,1)} %bitcast.135, bf16[32,128,256]{2,1,0:T(8,128)(2,1)S(1)} %all-to-all-done.1), kind=kOutput, calls=%fused_computation.30 | convolution fusion | flops 1075838976 | bytes 18890752 | tf_op jit(solution)/shard_map/borf,olf->borl/dot_general | solution.py:115
  110.6 5.0 %copy.275 = f32[16,32,32,128]{3,2,1,0:T(8,128)S(1)} copy(f32[16,32,32,128]{3,2,0,1:T(8,128)} %add_bitcast_fusion) | data formatting | bytes 16777216 | tf_op jit(solution)/shard_map/add | solution.py:119
  115.6 5.4 %reduce-precision_convert_fusion.1 = (bf16[16,1024,128]{2,1,0:T(8,128)(2,1)}, bf16[16,1024,128]{2,1,0:T(8,128)(2,1)}) fusion(f32[16,32,32,128]{3,2,1,0:T(8,128)S(1)} %copy.275), kind=kLoop, calls=%fused_computation.14 | loop fusion | flops 8388608 | bytes 16777216 | tf_op jit(solution)/shard_map/convert_element_type | solution.py:32
  120.9 15.6 %fusion.3 = f32[16,128,4,256]{3,1,2,0:T(8,128)} fusion(s32[16,128,4]{1,2,0:T(4,128)S(1)} %copy.272, bf16[16,1024,128]{2,1,0:T(8,128)(2,1)} %get-tuple-element.43, bf16[16,1024,128]{2,1,0:T(8,128)(2,1)} %get-tuple-element.42), kind=kOutput, calls=%fused_computation.4 | convolution fusion | flops 4320133120 | bytes 16809984 | tf_op jit(solution)/shard_map/btkq,bql->btkl/dot_general | solution.py:105
  136.5 4.2 slice_add_fusion.1
  141.0 8.6 %all_to_all.70 = f32[2,16,64,4,128]{4,2,3,1,0:T(8,128)} all-to-all(f32[2,16,64,4,128]{4,2,3,1,0:T(8,128)S(1)} %bitcast.142), channel_id=1, replica_groups=mesh['dh'=2,'dl'=8,'lat'=2] {'lat'}, dimensions={0} | all-to-all | bytes 8388608 | tf_op jit(solution)/shard_map/all_to_all | solution.py:58
  149.6 4.1 reduce_sum.119
  153.7 3.0 copy.353
  156.8 30.0 %all_to_all.71 = f32[8,2,64,4,128]{4,3,2,1,0:T(4,128)} all-to-all(f32[8,2,64,4,128]{4,3,2,1,0:T(4,128)S(1)} %bitcast.147), channel_id=1, replica_groups=mesh['dh'=2,'dl'=8,'lat'=2] {'dl'}, dimensions={0} | all-to-all | bytes 4194304 | tf_op jit(solution)/shard_map/all_to_all | solution.py:60
  186.8 2.7 reduce_sum.120
  189.5 3.4 all-to-all-start.4
  193.1 7.7 %all-to-all-done.4 = f32[2,64,4,128]{3,2,1,0:T(4,128)S(1)} async-done(((f32[2,64,4,128]{3,2,1,0:T(4,128)}), f32[2,64,4,128]{3,2,1,0:T(4,128)S(1)}, u32[]{:S(2)}, u32[]{:S(2)}) %all-to-all-start.4) | async-done | bytes 262176 | tf_op jit(solution)/shard_map/all_to_all | solution.py:61
  202.4 8.3 %all_to_all.72 = bf16[2,64,4,128]{3,1,2,0:T(8,128)(2,1)S(1)} all-to-all(bf16[2,64,4,128]{3,1,2,0:T(8,128)(2,1)S(1)} %broadcast_in_dim.40), channel_id=1, replica_groups=mesh['dh'=2,'dl'=8,'lat'=2] {'dh'}, dimensions={0} | all-to-all | bytes 262144 | tf_op jit(solution)/shard_map/all_to_all | solution.py:64
  210.9 15.9 %all_to_all.73 = bf16[8,2,64,4,128]{4,2,3,1,0:T(8,128)(2,1)S(1)} all-to-all(bf16[8,2,64,4,128]{4,2,3,1,0:T(8,128)(2,1)S(1)} %broadcast_in_dim.41), channel_id=1, replica_groups=mesh['dh'=2,'dl'=8,'lat'=2] {'dl'}, dimensions={0} | all-to-all | bytes 2097152 | tf_op jit(solution)/shard_map/all_to_all | solution.py:65
  228.7 6.6 %all-gather.3.cloned.1.call-done = bf16[16,2,64,4,128]{4,2,3,1,0:T(8,128)(2,1)} async-done(((bf16[16,1,64,4,128]{4,2,3,1,0:T(8,128)(2,1)}), bf16[16,2,64,4,128]{4,2,3,1,0:T(8,128)(2,1)}) %all-gather.3.cloned.1.call-update) | async-done | bytes 2097168 | tf_op jit(solution)/shard_map/all_gather | solution.py:69
  237.1 5.9 %bitcast_convert_fusion.1 = bf16[16,1024,128]{2,1,0:T(8,128)(2,1)S(1)} fusion(bf16[16,128,4,128]{3,1,2,0:T(8,128)(2,1)S(1)} %bitcast.161, s32[16,128,4]{1,2,0:T(4,128)S(1)} %copy.272), kind=kOutput, calls=%fused_computation.24 | convolution fusion | flops 2157969408 | bytes 6324224 | tf_op jit(solution)/shard_map/btkq,btkl->bql/dot_general | solution.py:111
  245.1 5.6 %convert_bitcast_fusion = bf16[16,32,32,256]{3,2,0,1:T(8,128)(2,1)} fusion(bf16[16,32,32,128]{3,2,1,0:T(8,128)(2,1)S(1)} %bitcast.140, bf16[32,128,256]{2,1,0:T(8,128)(2,1)S(1)} %all-to-all-done.1), kind=kOutput, calls=%fused_computation.29 | convolution fusion | flops 1077936128 | bytes 14680064 | tf_op jit(solution)/shard_map/borl,olf->borf/dot_general | solution.py:130
  250.7 8.2 %copy.284 = bf16[16,32,32,256]{3,2,1,0:T(8,128)(2,1)} copy(bf16[16,32,32,256]{3,2,0,1:T(8,128)(2,1)} %convert_bitcast_fusion) | data formatting | bytes 16777216 | tf_op jit(solution)/shard_map/convert_element_type | solution.py:131
  258.8 7.1 %add_convert_fusion = (bf16[16,128,256]{2,1,0:T(8,128)(2,1)}, f32[256]{0:T(256)S(1)}, f32[16,128,256]{2,1,0:T(8,128)}) fusion(f32[256]{0:T(256)S(1)} %dynamic_slice.10, bf16[16,132,256]{2,1,0:T(8,128)(2,1)} %copy-done.5, bf16[16,128,1024]{1,2,0:T(8,128)(2,1)S(1)} %copy-done.2, bf16[16,1024,256]{2,1,0:T(8,128)(2,1)} %bitcast.137), kind=kOutput, calls=%fused_computation.50 | convolution fusion | flops 1076363008 | bytes 16779264 | tf_op jit(solution)/shard_map/btq,bqf->btf/dot_general | solution.py:132
  266.0 4.0 convolution_convert_fusion
  270.0 5.7 %fusion.22 = f32[16,32,32,128]{3,2,0,1:T(8,128)} fusion(bf16[16,32,32,256]{3,2,1,0:T(8,128)(2,1)S(1)} %bitcast.133, bf16[32,128,256]{2,1,0:T(8,128)(2,1)S(1)} %all-to-all-done.1), kind=kOutput, calls=%fused_computation.41 | convolution fusion | flops 1073741824 | bytes 18874368 | tf_op jit(solution)/shard_map/borf,olf->borl/dot_general | solution.py:147
  275.7 8.0 %copy.288 = f32[16,32,32,128]{3,2,1,0:T(8,128)} copy(f32[16,32,32,128]{3,2,0,1:T(8,128)} %fusion.22) | data formatting | bytes 16777216 | tf_op jit(solution)/shard_map/borf,olf->borl/transpose | solution.py:147
  283.7 9.1 %reduce-precision_convert_fusion = (bf16[16,1024,128]{2,1,0:T(8,128)(2,1)}, bf16[16,1024,128]{2,1,0:T(8,128)(2,1)}) fusion(f32[16,32,32,128]{3,2,1,0:T(8,128)} %copy.288), kind=kLoop, calls=%fused_computation.12 | loop fusion | flops 8388608 | bytes 16777216 | tf_op jit(solution)/shard_map/convert_element_type | solution.py:32
  292.8 15.6 %fusion.1 = f32[16,128,4,256]{3,1,2,0:T(8,128)} fusion(s32[16,128,4]{1,2,0:T(4,128)S(1)} %copy.272, bf16[16,1024,128]{2,1,0:T(8,128)(2,1)} %get-tuple-element.41, bf16[16,1024,128]{2,1,0:T(8,128)(2,1)} %get-tuple-element.40), kind=kOutput, calls=%fused_computation.2 | convolution fusion | flops 4320133120 | bytes 16809984 | tf_op jit(solution)/shard_map/btkq,bql->btkl/dot_general | solution.py:105
  308.4 4.2 slice_add_fusion
  312.9 8.2 %all_to_all.74 = f32[2,16,64,4,128]{4,2,3,1,0:T(8,128)} all-to-all(f32[2,16,64,4,128]{4,2,3,1,0:T(8,128)S(1)} %bitcast.143), channel_id=1, replica_groups=mesh['dh'=2,'dl'=8,'lat'=2] {'lat'}, dimensions={0} | all-to-all | bytes 8388608 | tf_op jit(solution)/shard_map/all_to_all | solution.py:58
  321.1 2.8 reduce_sum.124
  325.3 31.2 %all_to_all.75 = f32[8,2,64,4,128]{4,3,2,1,0:T(4,128)S(1)} all-to-all(f32[8,2,64,4,128]{4,3,2,1,0:T(4,128)S(1)} %bitcast.148), channel_id=1, replica_groups=mesh['dh'=2,'dl'=8,'lat'=2] {'dl'}, dimensions={0} | all-to-all | bytes 4194304 | tf_op jit(solution)/shard_map/all_to_all | solution.py:60
  357.0 11.1 %all_to_all.76 = f32[2,64,4,128]{3,2,1,0:T(4,128)S(1)} all-to-all(f32[2,64,4,128]{3,2,1,0:T(4,128)S(1)} %reduce_sum.125), channel_id=1, replica_groups=mesh['dh'=2,'dl'=8,'lat'=2] {'dh'}, dimensions={0} | all-to-all | bytes 524288 | tf_op jit(solution)/shard_map/all_to_all | solution.py:61
  369.6 8.3 %all_to_all.77 = bf16[2,64,4,128]{3,1,2,0:T(8,128)(2,1)S(1)} all-to-all(bf16[2,64,4,128]{3,1,2,0:T(8,128)(2,1)S(1)} %broadcast_in_dim.43), channel_id=1, replica_groups=mesh['dh'=2,'dl'=8,'lat'=2] {'dh'}, dimensions={0} | all-to-all | bytes 262144 | tf_op jit(solution)/shard_map/all_to_all | solution.py:64
  378.2 15.9 %all_to_all.78 = bf16[8,2,64,4,128]{4,2,3,1,0:T(8,128)(2,1)S(1)} all-to-all(bf16[8,2,64,4,128]{4,2,3,1,0:T(8,128)(2,1)S(1)} %broadcast_in_dim.44), channel_id=1, replica_groups=mesh['dh'=2,'dl'=8,'lat'=2] {'dl'}, dimensions={0} | all-to-all | bytes 2097152 | tf_op jit(solution)/shard_map/all_to_all | solution.py:65
  396.7 3.9 all-to-all-start.7
  400.6 8.1 %fusion.56 = f32[32,128,256,1]{2,1,0,3:T(8,128)} fusion(bf16[16,32,32,128]{3,2,1,0:T(8,128)(2,1)} %bitcast.141, bf16[16,32,32,256]{3,2,1,0:T(8,128)(2,1)} %bitcast.134), kind=kOutput, calls=%fused_computation.125 | convolution fusion | flops 1073741824 | bytes 16777216 | tf_op jit(solution)/shard_map/borl,borf->olf/dot_general | solution.py:156
  412.0 5.7 %bitcast_convert_fusion = bf16[16,1024,128]{2,1,0:T(8,128)(2,1)S(1)} fusion(bf16[16,128,4,128]{3,1,2,0:T(8,128)(2,1)S(1)} %bitcast.160, s32[16,128,4]{1,2,0:T(4,128)S(1)} %copy.272), kind=kOutput, calls=%fused_computation.23 | convolution fusion | flops 2157969408 | bytes 6324224 | tf_op jit(solution)/shard_map/btkq,btkl->bql/dot_general | solution.py:111
  417.7 5.3 %fusion.20 = bf16[32,128,256]{2,1,0:T(8,128)(2,1)S(1)} fusion(f32[32,128,256,1]{2,1,0,3:T(8,128)S(1)} %copy-done.4, bf16[16,32,32,128]{3,2,1,0:T(8,128)(2,1)S(1)} %bitcast.156, bf16[16,32,32,256]{3,2,1,0:T(8,128)(2,1)} %bitcast.136), kind=kOutput, calls=%fused_computation.36 | convolution fusion | flops 1075838976 | bytes 18874368 | tf_op jit(solution)/shard_map/borl,borf->olf/dot_general | solution.py:157
  424.6 6.0 %all-to-all-start.13 = ((bf16[32,129,256]{2,1,0:T(8,128)(2,1)}), bf16[32,129,256]{2,1,0:T(8,128)(2,1)S(1)}, u32[]{:S(2)}, u32[]{:S(2)}) async-start(bf16[32,129,256]{2,1,0:T(8,128)(2,1)} %pad_maximum_fusion), calls=%async_computation.13 | async-start | bytes 4456448 | tf_op jit(solution)/shard_map/all_to_all | solution.py:162
  431.6 2.3 copy.317
  433.9 2.3 copy.300
  436.8 45.5 %all-to-all-done.13 = bf16[32,129,256]{2,1,0:T(8,128)(2,1)S(1)} async-done(((bf16[32,129,256]{2,1,0:T(8,128)(2,1)}), bf16[32,129,256]{2,1,0:T(8,128)(2,1)S(1)}, u32[]{:S(2)}, u32[]{:S(2)}) %all-to-all-start.13) | async-done | bytes 2113568 | tf_op jit(solution)/shard_map/all_to_all | solution.py:162
  483.7 2.7 copy.323
  (96 shorter events, 38.7 us)
Async XLA Ops:
  12.7 34.1 %all-to-all-start = ((bf16[16,132,256]{2,1,0:T(8,128)(2,1)}), bf16[16,132,256]{2,1,0:T(8,128)(2,1)S(1)}, u32[]{:S(2)}, u32[]{:S(2)}) async-start(bf16[16,132,256]{2,1,0:T(8,128)(2,1)} %copy.265), calls=%async_computation | async-start | bytes 2228224 | tf_op jit(solution)/shard_map/all_to_all | solution.py:83
  23.2 29.7 %copy-start.10 = (f32[128]{0:T(128)S(1)}, f32[128]{0:T(128)}, u32[]{:S(2)}) copy-start(f32[128]{0:T(128)} %param.10) | copy-start | bytes 1540
  46.7 1.1 copy-start.5
  47.8 53.8 %all-to-all-start.1 = ((bf16[32,128,256]{2,1,0:T(8,128)(2,1)}), bf16[32,128,256]{2,1,0:T(8,128)(2,1)S(1)}, u32[]{:S(2)}, u32[]{:S(2)}) async-start(bf16[32,128,256]{2,1,0:T(8,128)(2,1)} %bitcast.146), calls=%async_computation.1 | async-start | bytes 4194304 | tf_op jit(solution)/shard_map/all_to_all | solution.py:93
  65.0 2.0 copy-start.1
  156.7 36.2 %copy-start.9 = (s32[128,4]{0,1:T(4,128)S(1)}, s32[128,4]{0,1:T(4,128)}, u32[]{:S(2)}) copy-start(s32[128,4]{0,1:T(4,128)} %param.8) | copy-start | bytes 6148
  189.5 11.3 %all-to-all-start.4 = ((f32[2,64,4,128]{3,2,1,0:T(4,128)}), f32[2,64,4,128]{3,2,1,0:T(4,128)S(1)}, u32[]{:S(2)}, u32[]{:S(2)}) async-start(f32[2,64,4,128]{3,2,1,0:T(4,128)} %reduce_sum.120), calls=%async_computation.4 | async-start | bytes 524288 | tf_op jit(solution)/shard_map/all_to_all | solution.py:61
  192.9 42.4 %all-gather.3.cloned.1.call-start = ((), (), s32[]{:S(2)}) async-start(), calls=%async_computation.14 | async-start | bytes 3145728 | tf_op jit(solution)/shard_map/all_gather | solution.py:69
  227.9 182.3 %all-gather.5.cloned.1.call-start = ((), (), s32[]{:S(2)}) async-start(), calls=%async_computation.15 | async-start | bytes 3145728 | tf_op jit(solution)/shard_map/all_gather | solution.py:69
  243.1 2.0 copy-start.3
  250.7 8.2 %copy-start.2 = (bf16[16,128,1024]{1,2,0:T(8,128)(2,1)S(1)}, bf16[16,128,1024]{1,2,0:T(8,128)(2,1)}, u32[]{:S(2)}) copy-start(bf16[16,128,1024]{1,2,0:T(8,128)(2,1)} %copy-done.1) | copy-start | bytes 12582916
  258.8 7.1 %copy-start.6 = (bf16[16,132,256]{2,1,0:T(8,128)(2,1)S(1)}, bf16[16,132,256]{2,1,0:T(8,128)(2,1)}, u32[]{:S(2)}) copy-start(bf16[16,132,256]{2,1,0:T(8,128)(2,1)} %copy-done.5) | copy-start | bytes 3244036
  269.9 5.7 %copy-start = (bf16[16,1024,256]{2,1,0:T(8,128)(2,1)}, bf16[16,1024,256]{2,1,0:T(8,128)(2,1)S(1)}, u32[]{:S(2)}) copy-start(bf16[16,1024,256]{2,1,0:T(8,128)(2,1)S(1)} %convolution_convert_fusion) | copy-start | bytes 25165828
  356.9 38.3 %copy-start.8 = (s32[128,4]{0,1:T(4,128)S(1)}, s32[128,4]{0,1:T(4,128)}, u32[]{:S(2)}) copy-start(s32[128,4]{0,1:T(4,128)} %param.7) | copy-start | bytes 6148
  357.0 38.6 %copy-start.7 = (bf16[16,128,256]{2,1,0:T(8,128)(2,1)S(1)}, bf16[16,128,256]{2,1,0:T(8,128)(2,1)}, u32[]{:S(2)}) copy-start(bf16[16,128,256]{2,1,0:T(8,128)(2,1)} %get-tuple-element.44) | copy-start | bytes 3145732
  396.7 27.9 %all-to-all-start.7 = ((bf16[16,130,256]{2,1,0:T(8,128)(2,1)}), bf16[16,130,256]{2,1,0:T(8,128)(2,1)S(1)}, u32[]{:S(2)}, u32[]{:S(2)}) async-start(bf16[16,130,256]{2,1,0:T(8,128)(2,1)} %pad_maximum_fusion.2), calls=%async_computation.7 | async-start | bytes 2228224 | tf_op jit(solution)/shard_map/all_to_all | solution.py:141
  412.0 5.8 %copy-start.4 = (f32[32,128,256,1]{2,1,0,3:T(8,128)S(1)}, f32[32,128,256,1]{2,1,0,3:T(8,128)}, u32[]{:S(2)}) copy-start(f32[32,128,256,1]{2,1,0,3:T(8,128)} %fusion.56) | copy-start | bytes 12582916
  424.6 57.7 %all-to-all-start.13 = ((bf16[32,129,256]{2,1,0:T(8,128)(2,1)}), bf16[32,129,256]{2,1,0:T(8,128)(2,1)S(1)}, u32[]{:S(2)}, u32[]{:S(2)}) async-start(bf16[32,129,256]{2,1,0:T(8,128)(2,1)} %pad_maximum_fusion), calls=%async_computation.13 | async-start | bytes 4456448 | tf_op jit(solution)/shard_map/all_to_all | solution.py:162
Sparse Core Ops, SparseCore 0:
  228.0 7.2 all-gather.2
  395.3 7.2 all-gather.4

commit v7 on v6

--- a/solution.py
+++ b/solution.py
@@ -4,8 +4,8 @@
 from jax.sharding import Mesh, PartitionSpec as P
 
 BLK_DEV = 2
-DP = ("dh", "dl")
-ALL = ("dh", "dl", "lat")
+DP = ("dh", "dm", "dn")
+ALL = ("dh", "dm", "dn", "lat")
 F32 = jnp.float32
 BF16 = jnp.bfloat16
 
@@ -35,9 +35,12 @@
 def local(acts, owner_ids, block_codes, weights, enc_bias, dec_bias):
     dp_count = lax.axis_size(DP)
     dh_count = lax.axis_size("dh")
-    dl_count = lax.axis_size("dl")
+    dm_count = lax.axis_size("dm")
+    dn_count = lax.axis_size("dn")
     lat_count = lax.axis_size("lat")
-    dp_idx = lax.axis_index("dh") * dl_count + lax.axis_index("dl")
+    dp_idx = (lax.axis_index("dh") * dm_count + lax.axis_index("dm")) * dn_count + lax.axis_index(
+        "dn"
+    )
     lat_idx = lax.axis_index("lat")
     me = dp_idx * lat_count + lat_idx
     owner_total = dp_count * lat_count
@@ -56,16 +59,21 @@
         tail = x.shape[1:]
         y = x.reshape((dp_count, lat_count, mine_rows) + tail).swapaxes(0, 1)
         y = jnp.sum(lax.all_to_all(y, "lat", 0, 0, tiled=True), axis=0)
-        y = y.reshape((dh_count, dl_count) + y.shape[1:]).swapaxes(0, 1)
-        y = jnp.sum(lax.all_to_all(y, "dl", 0, 0, tiled=True), axis=0)
+        y = y.reshape((dh_count, dm_count, dn_count) + y.shape[1:])
+        y = jnp.moveaxis(y, 2, 0)
+        y = jnp.sum(lax.all_to_all(y, "dn", 0, 0, tiled=True), axis=0).swapaxes(0, 1)
+        y = jnp.sum(lax.all_to_all(y, "dm", 0, 0, tiled=True), axis=0)
         return jnp.sum(lax.all_to_all(y, "dh", 0, 0, tiled=True), axis=0)
 
     def ag_tokens(x):
         y = lax.all_to_all(jnp.broadcast_to(x[None], (dh_count,) + x.shape), "dh", 0, 0, tiled=True)
         y = lax.all_to_all(
-            jnp.broadcast_to(y[None], (dl_count,) + y.shape), "dl", 0, 0, tiled=True
-        ).swapaxes(0, 1)
-        y = y.reshape((dp_count,) + x.shape)
+            jnp.broadcast_to(y[None], (dm_count,) + y.shape), "dm", 0, 0, tiled=True
+        )
+        y = lax.all_to_all(
+            jnp.broadcast_to(y[None], (dn_count,) + y.shape), "dn", 0, 0, tiled=True
+        )
+        y = jnp.moveaxis(y, 0, 2).swapaxes(0, 1).reshape((dp_count,) + x.shape)
         y = lax.all_gather(y, "lat", axis=1, tiled=False)
         return y.reshape((tokens,) + x.shape[1:])
 
@@ -175,8 +183,11 @@
 
 def solution(mesh):
     dp_count, lat_count = mesh.devices.shape
-    halves = 2 if dp_count % 2 == 0 else 1
-    split = Mesh(mesh.devices.reshape(halves, dp_count // halves, lat_count), ("dh", "dl", "lat"))
+    halves = 2 if dp_count % 4 == 0 else 1
+    split = Mesh(
+        mesh.devices.reshape(halves, halves, dp_count // halves // halves, lat_count),
+        ("dh", "dm", "dn", "lat"),
+    )
     in_specs = (
         P(DP, "lat"),
         P(DP, None),

time: 499 us -> 523 us (1.048)
  blocking collectives: 138 us -> 162 us
    all_to_all x4 -> x8, blocking collectives: 93 us -> 119 us  [the longest x2 58.6 us: rs_tokens(): lax.all_to_all(y, 'dn', 0, 0, tiled=True)]
where the time goes in v7:
time: 523 us; the launch traced here: 519 us
  blocking collectives  162 us (31%)
  waiting for transfers between devices  108 us (21%)
  matrix products  94.5 us (18%)
  local copies, waits for them, and re-layouts  62.1 us (12%)
  other arithmetic  50.5 us (10%)
  starting transfers between devices  27.1 us (5%)
  between operations  14.9 us (3%)
    all_to_all x2, blocking collectives, rs_tokens(): lax.all_to_all(y, 'dn', 0, 0, tiled=True)  58.6 us
    all_to_all x1, waiting for transfers between devices, local(): lax.all_to_all(jnp.concatenate([gw.astype(BF16), genc], axis=1), ALL, 0,...  45.5 us
    dot_general x2, matrix products, slots_to_pairs(): out = jnp.einsum('btkq,bql->btkl', sel, both, preferred_element_type=F32)  31.1 us
    all_to_all x1, waiting for transfers between devices, local(): w_fs = lax.all_to_all(w_send, ALL, 0, 0, tiled=True)  27.6 us
    all_to_all x2, blocking collectives, ag_tokens(): lax.all_to_all(jnp.broadcast_to(y[None], (dn_count,) + y.shape), 'dn', 0,...  26.1 us
    all_to_all x1, waiting for transfers between devices, local(): acts_got = lax.all_to_all(acts_send, DP, 0, 0, tiled=True)  21 us
    all_to_all x2, blocking collectives, rs_tokens(): y = jnp.sum(lax.all_to_all(y, 'dm', 0, 0, tiled=True), axis=0)  18.9 us
    all_to_all x2, blocking collectives, rs_tokens(): y = jnp.sum(lax.all_to_all(y, 'lat', 0, 0, tiled=True), axis=0)  16.6 us
  transfers between devices with their start and end apart: 7, of which 5 were waited for; matrix products, arithmetic and copies ran while one was open for 11% of the time, Pallas kernels for 0%

profile of v7, /device:TPU:0, one launch (start us, length us, event | category | flops | bytes accessed | tf_op | source)
XLA Modules:
  0.0 518.5 jit_solution(15700582923127051061)
XLA Ops:
  12.7 8.3 %all-to-all-start = ((bf16[16,132,256]{2,1,0:T(8,128)(2,1)}), bf16[16,132,256]{2,1,0:T(8,128)(2,1)S(1)}, u32[]{:S(2)}, u32[]{:S(2)}) async-start(bf16[16,132,256]{2,1,0:T(8,128)(2,1)} %copy.322), calls=%async_computation | async-start | bytes 2228224 | tf_op jit(solution)/shard_map/all_to_all | solution.py:91
  23.2 2.5 copy.330
  25.7 21.0 %all-to-all-done = bf16[16,132,256]{2,1,0:T(8,128)(2,1)S(1)} async-done(((bf16[16,132,256]{2,1,0:T(8,128)(2,1)}), bf16[16,132,256]{2,1,0:T(8,128)(2,1)S(1)}, u32[]{:S(2)}, u32[]{:S(2)}) %all-to-all-start) | async-done | bytes 1081376 | tf_op jit(solution)/shard_map/all_to_all | solution.py:91
  47.8 5.4 %all-to-all-start.1 = ((bf16[32,128,256]{2,1,0:T(8,128)(2,1)}), bf16[32,128,256]{2,1,0:T(8,128)(2,1)S(1)}, u32[]{:S(2)}, u32[]{:S(2)}) async-start(bf16[32,128,256]{2,1,0:T(8,128)(2,1)} %bitcast.148), calls=%async_computation.1 | async-start | bytes 4194304 | tf_op jit(solution)/shard_map/all_to_all | solution.py:101
  60.7 4.6 fusion.5
  67.3 6.8 %convolution_convert_fusion.1 = bf16[16,1024,256]{2,1,0:T(8,128)(2,1)} fusion(bf16[16,128,1024]{1,2,0:T(8,128)(2,1)S(1)} %fusion.5, bf16[16,132,256]{2,1,0:T(8,128)(2,1)} %copy-done.5), kind=kOutput, calls=%fused_computation.32 | convolution fusion | flops 1077936128 | bytes 13631488 | tf_op jit(solution)/shard_map/btq,btf->bqf/dot_general | solution.py:106
  74.0 27.6 %all-to-all-done.1 = bf16[32,128,256]{2,1,0:T(8,128)(2,1)S(1)} async-done(((bf16[32,128,256]{2,1,0:T(8,128)(2,1)}), bf16[32,128,256]{2,1,0:T(8,128)(2,1)S(1)}, u32[]{:S(2)}, u32[]{:S(2)}) %all-to-all-start.1) | async-done | bytes 2097184 | tf_op jit(solution)/shard_map/all_to_all | solution.py:101
  101.6 8.9 %add_bitcast_fusion = f32[16,32,32,128]{3,2,0,1:T(8,128)} fusion(f32[32,128]{1,0:T(8,128)S(1)} %broadcast_select_fusion, bf16[16,32,32,256]{3,2,1,0:T(8,128)(2,1)} %bitcast.137, bf16[32,128,256]{2,1,0:T(8,128)(2,1)S(1)} %all-to-all-done.1), kind=kOutput, calls=%fused_computation.30 | convolution fusion | flops 1075838976 | bytes 18890752 | tf_op jit(solution)/shard_map/borf,olf->borl/dot_general | solution.py:123
  110.6 5.0 copy.332
  115.5 5.4 %reduce-precision_convert_fusion.1 = (bf16[16,1024,128]{2,1,0:T(8,128)(2,1)}, bf16[16,1024,128]{2,1,0:T(8,128)(2,1)}) fusion(f32[16,32,32,128]{3,2,1,0:T(8,128)S(1)} %copy.332), kind=kLoop, calls=%fused_computation.14 | loop fusion | flops 8388608 | bytes 16777216 | tf_op jit(solution)/shard_map/convert_element_type | solution.py:32
  120.9 15.6 %fusion.3 = f32[16,128,4,256]{3,1,2,0:T(8,128)} fusion(s32[16,128,4]{1,2,0:T(4,128)S(1)} %copy.329, bf16[16,1024,128]{2,1,0:T(8,128)(2,1)} %get-tuple-element.47, bf16[16,1024,128]{2,1,0:T(8,128)(2,1)} %get-tuple-element.46), kind=kOutput, calls=%fused_computation.4 | convolution fusion | flops 4320133120 | bytes 16809984 | tf_op jit(solution)/shard_map/btkq,bql->btkl/dot_general | solution.py:113
  136.4 4.2 slice_add_fusion.1
  141.0 8.4 %all_to_all.90 = f32[2,16,64,4,128]{4,2,3,1,0:T(8,128)} all-to-all(f32[2,16,64,4,128]{4,2,3,1,0:T(8,128)S(1)} %bitcast.144), channel_id=1, replica_groups=mesh['dh'=2,'dm'=2,'dn'=4,'lat'=2] {'lat'}, dimensions={0} | all-to-all | bytes 8388608 | tf_op jit(solution)/shard_map/all_to_all | solution.py:61
  149.4 4.1 reduce_sum.137
  153.5 3.0 copy.414
  156.5 29.2 %all_to_all.91 = f32[4,2,2,64,4,128]{5,4,3,2,1,0:T(4,128)} all-to-all(f32[4,2,2,64,4,128]{5,4,3,2,1,0:T(4,128)S(1)} %bitcast.149), channel_id=1, replica_groups=mesh['dh'=2,'dm'=2,'dn'=4,'lat'=2] {'dn'}, dimensions={0} | all-to-all | bytes 4194304 | tf_op jit(solution)/shard_map/all_to_all | solution.py:64
  188.0 9.7 %all_to_all.92 = f32[2,2,64,4,128]{4,3,2,1,0:T(4,128)S(1)} all-to-all(f32[2,2,64,4,128]{4,3,2,1,0:T(4,128)S(1)} %copy.337), channel_id=1, replica_groups=mesh['dh'=2,'dm'=2,'dn'=4,'lat'=2] {'dm'}, dimensions={0} | all-to-all | bytes 1048576 | tf_op jit(solution)/shard_map/all_to_all | solution.py:65
  198.5 3.4 all-to-all-start.5
  202.1 7.0 %all-to-all-done.5 = f32[2,64,4,128]{3,2,1,0:T(4,128)S(1)} async-done(((f32[2,64,4,128]{3,2,1,0:T(4,128)}), f32[2,64,4,128]{3,2,1,0:T(4,128)S(1)}, u32[]{:S(2)}, u32[]{:S(2)}) %all-to-all-start.5) | async-done | bytes 262176 | tf_op jit(solution)/shard_map/all_to_all | solution.py:66
  210.7 7.7 %all_to_all.93 = bf16[2,64,4,128]{3,1,2,0:T(8,128)(2,1)S(1)} all-to-all(bf16[2,64,4,128]{3,1,2,0:T(8,128)(2,1)S(1)} %broadcast_in_dim.44), channel_id=1, replica_groups=mesh['dh'=2,'dm'=2,'dn'=4,'lat'=2] {'dh'}, dimensions={0} | all-to-all | bytes 262144 | tf_op jit(solution)/shard_map/all_to_all | solution.py:69
  218.5 7.6 %all_to_all.94 = bf16[2,2,64,4,128]{4,2,3,1,0:T(8,128)(2,1)S(1)} all-to-all(bf16[2,2,64,4,128]{4,2,3,1,0:T(8,128)(2,1)S(1)} %broadcast_in_dim.45), channel_id=1, replica_groups=mesh['dh'=2,'dm'=2,'dn'=4,'lat'=2] {'dm'}, dimensions={0} | all-to-all | bytes 524288 | tf_op jit(solution)/shard_map/all_to_all | solution.py:70
  226.3 13.6 %all_to_all.95 = bf16[4,2,2,64,4,128]{5,3,4,1,2,0:T(8,128)(2,1)S(1)} all-to-all(bf16[4,2,2,64,4,128]{5,3,4,1,2,0:T(8,128)(2,1)S(1)} %broadcast_in_dim.46), channel_id=1, replica_groups=mesh['dh'=2,'dm'=2,'dn'=4,'lat'=2] {'dn'}, dimensions={0} | all-to-all | bytes 2097152 | tf_op jit(solution)/shard_map/all_to_all | solution.py:73
  241.8 6.6 %all-gather.3.cloned.1.call-done = bf16[16,2,64,4,128]{4,2,3,1,0:T(8,128)(2,1)} async-done(((bf16[16,1,64,4,128]{4,2,3,1,0:T(8,128)(2,1)}), bf16[16,2,64,4,128]{4,2,3,1,0:T(8,128)(2,1)}) %all-gather.3.cloned.1.call-update) | async-done | bytes 2097168 | tf_op jit(solution)/shard_map/all_gather | solution.py:77
  250.3 6.2 %bitcast_convert_fusion.1 = bf16[16,1024,128]{2,1,0:T(8,128)(2,1)S(1)} fusion(bf16[16,128,4,128]{3,1,2,0:T(8,128)(2,1)S(1)} %bitcast.163, s32[16,128,4]{1,2,0:T(4,128)S(1)} %copy.329), kind=kOutput, calls=%fused_computation.24 | convolution fusion | flops 2157969408 | bytes 6324224 | tf_op jit(solution)/shard_map/btkq,btkl->bql/dot_general | solution.py:119
  258.5 5.6 %convert_bitcast_fusion = bf16[16,32,32,256]{3,2,0,1:T(8,128)(2,1)} fusion(bf16[16,32,32,128]{3,2,1,0:T(8,128)(2,1)S(1)} %bitcast.142, bf16[32,128,256]{2,1,0:T(8,128)(2,1)S(1)} %all-to-all-done.1), kind=kOutput, calls=%fused_computation.29 | convolution fusion | flops 1077936128 | bytes 14680064 | tf_op jit(solution)/shard_map/borl,olf->borf/dot_general | solution.py:138
  264.1 8.2 %copy.343 = bf16[16,32,32,256]{3,2,1,0:T(8,128)(2,1)} copy(bf16[16,32,32,256]{3,2,0,1:T(8,128)(2,1)} %convert_bitcast_fusion) | data formatting | bytes 16777216 | tf_op jit(solution)/shard_map/convert_element_type | solution.py:139
  272.3 7.1 %add_convert_fusion = (bf16[16,128,256]{2,1,0:T(8,128)(2,1)}, f32[256]{0:T(256)S(1)}, f32[16,128,256]{2,1,0:T(8,128)}) fusion(f32[256]{0:T(256)S(1)} %dynamic_slice.10, bf16[16,132,256]{2,1,0:T(8,128)(2,1)} %copy-done.5, bf16[16,128,1024]{1,2,0:T(8,128)(2,1)S(1)} %copy-done.2, bf16[16,1024,256]{2,1,0:T(8,128)(2,1)} %bitcast.139), kind=kOutput, calls=%fused_computation.50 | convolution fusion | flops 1076363008 | bytes 16779264 | tf_op jit(solution)/shard_map/btq,bqf->btf/dot_general | solution.py:140
  279.4 4.0 convolution_convert_fusion
  283.4 5.7 %fusion.22 = f32[16,32,32,128]{3,2,0,1:T(8,128)} fusion(bf16[16,32,32,256]{3,2,1,0:T(8,128)(2,1)S(1)} %bitcast.135, bf16[32,128,256]{2,1,0:T(8,128)(2,1)S(1)} %all-to-all-done.1), kind=kOutput, calls=%fused_computation.41 | convolution fusion | flops 1073741824 | bytes 18874368 | tf_op jit(solution)/shard_map/borf,olf->borl/dot_general | solution.py:155
  289.1 8.0 %copy.347 = f32[16,32,32,128]{3,2,1,0:T(8,128)} copy(f32[16,32,32,128]{3,2,0,1:T(8,128)} %fusion.22) | data formatting | bytes 16777216 | tf_op jit(solution)/shard_map/borf,olf->borl/transpose | solution.py:155
  297.1 8.9 %reduce-precision_convert_fusion = (bf16[16,1024,128]{2,1,0:T(8,128)(2,1)}, bf16[16,1024,128]{2,1,0:T(8,128)(2,1)}) fusion(f32[16,32,32,128]{3,2,1,0:T(8,128)} %copy.347), kind=kLoop, calls=%fused_computation.12 | loop fusion | flops 8388608 | bytes 16777216 | tf_op jit(solution)/shard_map/convert_element_type | solution.py:32
  306.0 15.6 %fusion.1 = f32[16,128,4,256]{3,1,2,0:T(8,128)} fusion(s32[16,128,4]{1,2,0:T(4,128)S(1)} %copy.329, bf16[16,1024,128]{2,1,0:T(8,128)(2,1)} %get-tuple-element.45, bf16[16,1024,128]{2,1,0:T(8,128)(2,1)} %get-tuple-element.44), kind=kOutput, calls=%fused_computation.2 | convolution fusion | flops 4320133120 | bytes 16809984 | tf_op jit(solution)/shard_map/btkq,bql->btkl/dot_general | solution.py:113
  321.5 4.2 slice_add_fusion
  326.1 8.2 %all_to_all.96 = f32[2,16,64,4,128]{4,2,3,1,0:T(8,128)} all-to-all(f32[2,16,64,4,128]{4,2,3,1,0:T(8,128)S(1)} %bitcast.145), channel_id=1, replica_groups=mesh['dh'=2,'dm'=2,'dn'=4,'lat'=2] {'lat'}, dimensions={0} | all-to-all | bytes 8388608 | tf_op jit(solution)/shard_map/all_to_all | solution.py:61
  334.3 2.8 reduce_sum.143
  338.5 29.4 %all_to_all.97 = f32[4,2,2,64,4,128]{5,4,3,2,1,0:T(4,128)S(1)} all-to-all(f32[4,2,2,64,4,128]{5,4,3,2,1,0:T(4,128)S(1)} %bitcast.150), channel_id=1, replica_groups=mesh['dh'=2,'dm'=2,'dn'=4,'lat'=2] {'dn'}, dimensions={0} | all-to-all | bytes 4194304 | tf_op jit(solution)/shard_map/all_to_all | solution.py:64
  368.5 9.3 %all_to_all.98 = f32[2,2,64,4,128]{4,3,2,1,0:T(4,128)S(1)} all-to-all(f32[2,2,64,4,128]{4,3,2,1,0:T(4,128)S(1)} %copy.352), channel_id=1, replica_groups=mesh['dh'=2,'dm'=2,'dn'=4,'lat'=2] {'dm'}, dimensions={0} | all-to-all | bytes 1048576 | tf_op jit(solution)/shard_map/all_to_all | solution.py:65
  378.0 10.7 %all_to_all.99 = f32[2,64,4,128]{3,2,1,0:T(4,128)S(1)} all-to-all(f32[2,64,4,128]{3,2,1,0:T(4,128)S(1)} %reduce_sum.145), channel_id=1, replica_groups=mesh['dh'=2,'dm'=2,'dn'=4,'lat'=2] {'dh'}, dimensions={0} | all-to-all | bytes 524288 | tf_op jit(solution)/shard_map/all_to_all | solution.py:66
  390.2 7.9 %all_to_all.100 = bf16[2,64,4,128]{3,1,2,0:T(8,128)(2,1)S(1)} all-to-all(bf16[2,64,4,128]{3,1,2,0:T(8,128)(2,1)S(1)} %broadcast_in_dim.48), channel_id=1, replica_groups=mesh['dh'=2,'dm'=2,'dn'=4,'lat'=2] {'dh'}, dimensions={0} | all-to-all | bytes 262144 | tf_op jit(solution)/shard_map/all_to_all | solution.py:69
  398.2 7.6 %all_to_all.101 = bf16[2,2,64,4,128]{4,2,3,1,0:T(8,128)(2,1)S(1)} all-to-all(bf16[2,2,64,4,128]{4,2,3,1,0:T(8,128)(2,1)S(1)} %broadcast_in_dim.49), channel_id=1, replica_groups=mesh['dh'=2,'dm'=2,'dn'=4,'lat'=2] {'dm'}, dimensions={0} | all-to-all | bytes 524288 | tf_op jit(solution)/shard_map/all_to_all | solution.py:70
  406.0 12.5 %all_to_all.102 = bf16[4,2,2,64,4,128]{5,3,4,1,2,0:T(8,128)(2,1)S(1)} all-to-all(bf16[4,2,2,64,4,128]{5,3,4,1,2,0:T(8,128)(2,1)S(1)} %broadcast_in_dim.50), channel_id=1, replica_groups=mesh['dh'=2,'dm'=2,'dn'=4,'lat'=2] {'dn'}, dimensions={0} | all-to-all | bytes 2097152 | tf_op jit(solution)/shard_map/all_to_all | solution.py:73
  421.1 3.9 all-to-all-start.9
  425.0 8.1 %fusion.56 = f32[32,128,256,1]{2,1,0,3:T(8,128)} fusion(bf16[16,32,32,128]{3,2,1,0:T(8,128)(2,1)} %bitcast.143, bf16[16,32,32,256]{3,2,1,0:T(8,128)(2,1)} %bitcast.136), kind=kOutput, calls=%fused_computation.125 | convolution fusion | flops 1073741824 | bytes 16777216 | tf_op jit(solution)/shard_map/borl,borf->olf/dot_general | solution.py:164
  436.4 5.7 %bitcast_convert_fusion = bf16[16,1024,128]{2,1,0:T(8,128)(2,1)S(1)} fusion(bf16[16,128,4,128]{3,1,2,0:T(8,128)(2,1)S(1)} %bitcast.162, s32[16,128,4]{1,2,0:T(4,128)S(1)} %copy.329), kind=kOutput, calls=%fused_computation.23 | convolution fusion | flops 2157969408 | bytes 6324224 | tf_op jit(solution)/shard_map/btkq,btkl->bql/dot_general | solution.py:119
  442.2 5.3 %fusion.20 = bf16[32,128,256]{2,1,0:T(8,128)(2,1)S(1)} fusion(f32[32,128,256,1]{2,1,0,3:T(8,128)S(1)} %copy-done.4, bf16[16,32,32,128]{3,2,1,0:T(8,128)(2,1)S(1)} %bitcast.158, bf16[16,32,32,256]{3,2,1,0:T(8,128)(2,1)} %bitcast.138), kind=kOutput, calls=%fused_computation.36 | convolution fusion | flops 1075838976 | bytes 18874368 | tf_op jit(solution)/shard_map/borl,borf->olf/dot_general | solution.py:165
  449.0 6.0 %all-to-all-start.17 = ((bf16[32,129,256]{2,1,0:T(8,128)(2,1)}), bf16[32,129,256]{2,1,0:T(8,128)(2,1)S(1)}, u32[]{:S(2)}, u32[]{:S(2)}) async-start(bf16[32,129,256]{2,1,0:T(8,128)(2,1)} %pad_maximum_fusion), calls=%async_computation.17 | async-start | bytes 4456448 | tf_op jit(solution)/shard_map/all_to_all | solution.py:170
  461.2 45.5 %all-to-all-done.17 = bf16[32,129,256]{2,1,0:T(8,128)(2,1)S(1)} async-done(((bf16[32,129,256]{2,1,0:T(8,128)(2,1)}), bf16[32,129,256]{2,1,0:T(8,128)(2,1)S(1)}, u32[]{:S(2)}, u32[]{:S(2)}) %all-to-all-start.17) | async-done | bytes 2113568 | tf_op jit(solution)/shard_map/all_to_all | solution.py:170
  508.2 2.7 copy.384
  (108 shorter events, 49.1 us)
Async XLA Ops:
  12.7 34.1 %all-to-all-start = ((bf16[16,132,256]{2,1,0:T(8,128)(2,1)}), bf16[16,132,256]{2,1,0:T(8,128)(2,1)S(1)}, u32[]{:S(2)}, u32[]{:S(2)}) async-start(bf16[16,132,256]{2,1,0:T(8,128)(2,1)} %copy.322), calls=%async_computation | async-start | bytes 2228224 | tf_op jit(solution)/shard_map/all_to_all | solution.py:91
  23.2 30.0 %copy-start.10 = (f32[128]{0:T(128)S(1)}, f32[128]{0:T(128)}, u32[]{:S(2)}) copy-start(f32[128]{0:T(128)} %param.10) | copy-start | bytes 1540
  46.7 1.1 copy-start.5
  47.8 53.8 %all-to-all-start.1 = ((bf16[32,128,256]{2,1,0:T(8,128)(2,1)}), bf16[32,128,256]{2,1,0:T(8,128)(2,1)S(1)}, u32[]{:S(2)}, u32[]{:S(2)}) async-start(bf16[32,128,256]{2,1,0:T(8,128)(2,1)} %bitcast.148), calls=%async_computation.1 | async-start | bytes 4194304 | tf_op jit(solution)/shard_map/all_to_all | solution.py:101
  65.3 2.0 copy-start.1
  156.5 45.5 %copy-start.9 = (s32[128,4]{0,1:T(4,128)S(1)}, s32[128,4]{0,1:T(4,128)}, u32[]{:S(2)}) copy-start(s32[128,4]{0,1:T(4,128)} %param.8) | copy-start | bytes 6148
  198.5 10.7 %all-to-all-start.5 = ((f32[2,64,4,128]{3,2,1,0:T(4,128)}), f32[2,64,4,128]{3,2,1,0:T(4,128)S(1)}, u32[]{:S(2)}, u32[]{:S(2)}) async-start(f32[2,64,4,128]{3,2,1,0:T(4,128)} %reduce_sum.139), calls=%async_computation.5 | async-start | bytes 524288 | tf_op jit(solution)/shard_map/all_to_all | solution.py:66
  201.9 46.5 %all-gather.3.cloned.1.call-start = ((), (), s32[]{:S(2)}) async-start(), calls=%async_computation.18 | async-start | bytes 3145728 | tf_op jit(solution)/shard_map/all_gather | solution.py:77
  241.0 193.6 %all-gather.5.cloned.1.call-start = ((), (), s32[]{:S(2)}) async-start(), calls=%async_computation.19 | async-start | bytes 3145728 | tf_op jit(solution)/shard_map/all_gather | solution.py:77
  256.5 2.0 copy-start.3
  264.1 8.2 %copy-start.2 = (bf16[16,128,1024]{1,2,0:T(8,128)(2,1)S(1)}, bf16[16,128,1024]{1,2,0:T(8,128)(2,1)}, u32[]{:S(2)}) copy-start(bf16[16,128,1024]{1,2,0:T(8,128)(2,1)} %copy-done.1) | copy-start | bytes 12582916
  272.3 7.1 %copy-start.6 = (bf16[16,132,256]{2,1,0:T(8,128)(2,1)S(1)}, bf16[16,132,256]{2,1,0:T(8,128)(2,1)}, u32[]{:S(2)}) copy-start(bf16[16,132,256]{2,1,0:T(8,128)(2,1)} %copy-done.5) | copy-start | bytes 3244036
  283.4 5.7 %copy-start = (bf16[16,1024,256]{2,1,0:T(8,128)(2,1)}, bf16[16,1024,256]{2,1,0:T(8,128)(2,1)S(1)}, u32[]{:S(2)}) copy-start(bf16[16,1024,256]{2,1,0:T(8,128)(2,1)S(1)} %convolution_convert_fusion) | copy-start | bytes 25165828
  390.2 29.5 %copy-start.8 = (s32[128,4]{0,1:T(4,128)S(1)}, s32[128,4]{0,1:T(4,128)}, u32[]{:S(2)}) copy-start(s32[128,4]{0,1:T(4,128)} %param.7) | copy-start | bytes 6148
  390.2 29.8 %copy-start.7 = (bf16[16,128,256]{2,1,0:T(8,128)(2,1)S(1)}, bf16[16,128,256]{2,1,0:T(8,128)(2,1)}, u32[]{:S(2)}) copy-start(bf16[16,128,256]{2,1,0:T(8,128)(2,1)} %get-tuple-element.48) | copy-start | bytes 3145732
  421.1 27.9 %all-to-all-start.9 = ((bf16[16,130,256]{2,1,0:T(8,128)(2,1)}), bf16[16,130,256]{2,1,0:T(8,128)(2,1)S(1)}, u32[]{:S(2)}, u32[]{:S(2)}) async-start(bf16[16,130,256]{2,1,0:T(8,128)(2,1)} %pad_maximum_fusion.2), calls=%async_computation.9 | async-start | bytes 2228224 | tf_op jit(solution)/shard_map/all_to_all | solution.py:149
  436.4 5.8 %copy-start.4 = (f32[32,128,256,1]{2,1,0,3:T(8,128)S(1)}, f32[32,128,256,1]{2,1,0,3:T(8,128)}, u32[]{:S(2)}) copy-start(f32[32,128,256,1]{2,1,0,3:T(8,128)} %fusion.56) | copy-start | bytes 12582916
  449.0 57.7 %all-to-all-start.17 = ((bf16[32,129,256]{2,1,0:T(8,128)(2,1)}), bf16[32,129,256]{2,1,0:T(8,128)(2,1)S(1)}, u32[]{:S(2)}, u32[]{:S(2)}) async-start(bf16[32,129,256]{2,1,0:T(8,128)(2,1)} %pad_maximum_fusion), calls=%async_computation.17 | async-start | bytes 4456448 | tf_op jit(solution)/shard_map/all_to_all | solution.py:170
Sparse Core Ops, SparseCore 0:
  241.1 7.2 all-gather.2
  419.8 7.2 all-gather.4

commit v8 on v6

--- a/solution.py
+++ b/solution.py
@@ -66,7 +66,9 @@
             jnp.broadcast_to(y[None], (dl_count,) + y.shape), "dl", 0, 0, tiled=True
         ).swapaxes(0, 1)
         y = y.reshape((dp_count,) + x.shape)
-        y = lax.all_gather(y, "lat", axis=1, tiled=False)
+        y = lax.all_to_all(
+            jnp.broadcast_to(y[None], (lat_count,) + y.shape), "lat", 0, 0, tiled=True
+        ).swapaxes(0, 1)
         return y.reshape((tokens,) + x.shape[1:])
 
     id_vals = tok_rows * own_count * 2

time: 499 us -> 490 us (0.982)
  blocking collectives: 138 us -> 106 us
  waiting for transfers between devices: 109 us -> 133 us
  between operations: 14.8 us -> 1.42 us
  starting transfers between devices: 26.8 us -> 37.8 us
    all_to_all x2, blocking collectives: 31.7 us -> 10.8 us  [ag_tokens(): lax.all_to_all(jnp.broadcast_to(y[None], (lat_count,) + y.shape), 'lat',...]
    all_to_all x0 -> x3, waiting for transfers between devices: none -> 17.6 us  [the longest x2 12.4 us: ag_tokens(): lax.all_to_all(jnp.broadcast_to(y[None], (dl_count,) + y.shape), 'dl', 0,...]
    all_to_all x1, waiting for transfers between devices: 0.01 us -> 13.1 us  [local(): recon_got = lax.all_to_all(recon_send, DP, 0, 0, tiled=True)]
    all_to_all x0 -> x3, starting transfers between devices: none -> 11.2 us  [the longest x2 7.82 us: ag_tokens(): lax.all_to_all(jnp.broadcast_to(y[None], (dl_count,) + y.shape), 'dl', 0,...]
    all_to_all x2 -> x1, blocking collectives: 16.7 us -> 8.33 us  [ag_tokens(): lax.all_to_all(jnp.broadcast_to(x[None], (dh_count,) + x.shape), 'dh', 0,...]
    all_gather x2 -> x0, waiting for transfers between devices: 6.62 us -> none  [ag_tokens(): y = lax.all_gather(y, 'lat', axis=1, tiled=False)]
    unnamed x32 -> x40, local copies, waits for them, and re-layouts: 16.5 us -> 16.5 us
  transfers between devices with their start and end apart: 7 -> 8, of which waited for: 5 -> 8; matrix products, arithmetic and copies ran while one was open for 11% -> 11% of each run, Pallas kernels for 0% -> 0%
where the time goes in v8:
time: 490 us; the launch traced here: 485 us
  waiting for transfers between devices  133 us (27%)
  blocking collectives  106 us (22%)
  matrix products  94.3 us (19%)
  local copies, waits for them, and re-layouts  61.9 us (13%)
  other arithmetic  50.5 us (10%)
  starting transfers between devices  37.8 us (8%)
    all_to_all x2, blocking collectives, rs_tokens(): y = jnp.sum(lax.all_to_all(y, 'dl', 0, 0, tiled=True), axis=0)  59.6 us
    all_to_all x1, waiting for transfers between devices, local(): lax.all_to_all(jnp.concatenate([gw.astype(BF16), genc], axis=1), ALL, 0,...  45.5 us
    dot_general x2, matrix products, slots_to_pairs(): out = jnp.einsum('btkq,bql->btkl', sel, both, preferred_element_type=F32)  31.1 us
    all_to_all x1, waiting for transfers between devices, local(): w_fs = lax.all_to_all(w_send, ALL, 0, 0, tiled=True)  27.9 us
    all_to_all x1, waiting for transfers between devices, local(): acts_got = lax.all_to_all(acts_send, DP, 0, 0, tiled=True)  21 us
    all_to_all x2, blocking collectives, rs_tokens(): y = jnp.sum(lax.all_to_all(y, 'lat', 0, 0, tiled=True), axis=0)  17.1 us
    unnamed x40, local copies, waits for them, and re-layouts  16.5 us
    convert_element_type x4, other arithmetic, split_hi_lo(): return (hi.astype(BF16), (x - hi).astype(BF16))  14.3 us
  transfers between devices with their start and end apart: 8, of which 8 were waited for; matrix products, arithmetic and copies ran while one was open for 11% of the time, Pallas kernels for 0%

profile of v8, /device:TPU:0, one launch (start us, length us, event | category | flops | bytes accessed | tf_op | source)
XLA Modules:
  0.0 484.9 jit_solution(3891319579730127624)
XLA Ops:
  6.2 8.3 %all-to-all-start = ((bf16[16,132,256]{2,1,0:T(8,128)(2,1)}), bf16[16,132,256]{2,1,0:T(8,128)(2,1)S(1)}, u32[]{:S(2)}, u32[]{:S(2)}) async-start(bf16[16,132,256]{2,1,0:T(8,128)(2,1)} %copy.267), calls=%async_computation | async-start | bytes 2228224 | tf_op jit(solution)/shard_map/all_to_all | solution.py:85
  19.2 21.0 %all-to-all-done = bf16[16,132,256]{2,1,0:T(8,128)(2,1)S(1)} async-done(((bf16[16,132,256]{2,1,0:T(8,128)(2,1)}), bf16[16,132,256]{2,1,0:T(8,128)(2,1)S(1)}, u32[]{:S(2)}, u32[]{:S(2)}) %all-to-all-start) | async-done | bytes 1081376 | tf_op jit(solution)/shard_map/all_to_all | solution.py:85
  41.3 5.1 %all-to-all-start.1 = ((bf16[32,128,256]{2,1,0:T(8,128)(2,1)}), bf16[32,128,256]{2,1,0:T(8,128)(2,1)S(1)}, u32[]{:S(2)}, u32[]{:S(2)}) async-start(bf16[32,128,256]{2,1,0:T(8,128)(2,1)} %bitcast.148), calls=%async_computation.1 | async-start | bytes 4194304 | tf_op jit(solution)/shard_map/all_to_all | solution.py:95
  53.8 4.6 fusion.5
  60.4 6.8 %convolution_convert_fusion.1 = bf16[16,1024,256]{2,1,0:T(8,128)(2,1)} fusion(bf16[16,128,1024]{1,2,0:T(8,128)(2,1)S(1)} %fusion.5, bf16[16,132,256]{2,1,0:T(8,128)(2,1)} %copy-done.5), kind=kOutput, calls=%fused_computation.32 | convolution fusion | flops 1077936128 | bytes 13631488 | tf_op jit(solution)/shard_map/btq,btf->bqf/dot_general | solution.py:100
  67.2 27.9 %all-to-all-done.1 = bf16[32,128,256]{2,1,0:T(8,128)(2,1)S(1)} async-done(((bf16[32,128,256]{2,1,0:T(8,128)(2,1)}), bf16[32,128,256]{2,1,0:T(8,128)(2,1)S(1)}, u32[]{:S(2)}, u32[]{:S(2)}) %all-to-all-start.1) | async-done | bytes 2097184 | tf_op jit(solution)/shard_map/all_to_all | solution.py:95
  95.1 9.0 %add_bitcast_fusion = f32[16,32,32,128]{3,2,0,1:T(8,128)} fusion(f32[32,128]{1,0:T(8,128)S(1)} %broadcast_select_fusion, bf16[16,32,32,256]{3,2,1,0:T(8,128)(2,1)} %bitcast.137, bf16[32,128,256]{2,1,0:T(8,128)(2,1)S(1)} %all-to-all-done.1), kind=kOutput, calls=%fused_computation.30 | convolution fusion | flops 1075838976 | bytes 18890752 | tf_op jit(solution)/shard_map/borf,olf->borl/dot_general | solution.py:117
  104.1 5.0 %copy.277 = f32[16,32,32,128]{3,2,1,0:T(8,128)S(1)} copy(f32[16,32,32,128]{3,2,0,1:T(8,128)} %add_bitcast_fusion) | data formatting | bytes 16777216 | tf_op jit(solution)/shard_map/add | solution.py:121
  109.1 5.4 %reduce-precision_convert_fusion.1 = (bf16[16,1024,128]{2,1,0:T(8,128)(2,1)}, bf16[16,1024,128]{2,1,0:T(8,128)(2,1)}) fusion(f32[16,32,32,128]{3,2,1,0:T(8,128)S(1)} %copy.277), kind=kLoop, calls=%fused_computation.14 | loop fusion | flops 8388608 | bytes 16777216 | tf_op jit(solution)/shard_map/convert_element_type | solution.py:32
  114.4 15.6 %fusion.3 = f32[16,128,4,256]{3,1,2,0:T(8,128)} fusion(s32[16,128,4]{1,2,0:T(4,128)S(1)} %copy.274, bf16[16,1024,128]{2,1,0:T(8,128)(2,1)} %get-tuple-element.43, bf16[16,1024,128]{2,1,0:T(8,128)(2,1)} %get-tuple-element.42), kind=kOutput, calls=%fused_computation.4 | convolution fusion | flops 4320133120 | bytes 16809984 | tf_op jit(solution)/shard_map/btkq,bql->btkl/dot_general | solution.py:107
  130.0 4.2 slice_add_fusion.1
  134.6 8.6 %all_to_all.80 = f32[2,16,64,4,128]{4,2,3,1,0:T(8,128)} all-to-all(f32[2,16,64,4,128]{4,2,3,1,0:T(8,128)S(1)} %bitcast.144), channel_id=1, replica_groups=mesh['dh'=2,'dl'=8,'lat'=2] {'lat'}, dimensions={0} | all-to-all | bytes 8388608 | tf_op jit(solution)/shard_map/all_to_all | solution.py:58
  143.1 4.1 reduce_sum.119
  147.2 3.0 copy.355
  150.3 30.0 %all_to_all.81 = f32[8,2,64,4,128]{4,3,2,1,0:T(4,128)} all-to-all(f32[8,2,64,4,128]{4,3,2,1,0:T(4,128)S(1)} %bitcast.150), channel_id=1, replica_groups=mesh['dh'=2,'dl'=8,'lat'=2] {'dl'}, dimensions={0} | all-to-all | bytes 4194304 | tf_op jit(solution)/shard_map/all_to_all | solution.py:60
  180.3 2.7 reduce_sum.120
  183.0 3.4 all-to-all-start.4
  186.6 7.8 %all-to-all-done.4 = f32[2,64,4,128]{3,2,1,0:T(4,128)S(1)} async-done(((f32[2,64,4,128]{3,2,1,0:T(4,128)}), f32[2,64,4,128]{3,2,1,0:T(4,128)S(1)}, u32[]{:S(2)}, u32[]{:S(2)}) %all-to-all-start.4) | async-done | bytes 262176 | tf_op jit(solution)/shard_map/all_to_all | solution.py:61
  195.9 8.3 %all_to_all.82 = bf16[2,64,4,128]{3,1,2,0:T(8,128)(2,1)S(1)} all-to-all(bf16[2,64,4,128]{3,1,2,0:T(8,128)(2,1)S(1)} %broadcast_in_dim.48), channel_id=1, replica_groups=mesh['dh'=2,'dl'=8,'lat'=2] {'dh'}, dimensions={0} | all-to-all | bytes 262144 | tf_op jit(solution)/shard_map/all_to_all | solution.py:64
  205.4 4.3 all-to-all-start.6
  210.5 11.3 %all-to-all-done.6 = bf16[8,2,64,4,128]{4,2,3,1,0:T(8,128)(2,1)} async-done(((bf16[8,2,64,4,128]{4,2,3,1,0:T(8,128)(2,1)}), bf16[8,2,64,4,128]{4,2,3,1,0:T(8,128)(2,1)}, u32[]{:S(2)}, u32[]{:S(2)}) %all-to-all-start.6) | async-done | bytes 1048608 | tf_op jit(solution)/shard_map/all_to_all | solution.py:65
  223.8 5.4 %all_to_all.83 = bf16[2,16,64,4,128]{4,2,3,1,0:T(8,128)(2,1)S(1)} all-to-all(bf16[2,16,64,4,128]{4,2,3,1,0:T(8,128)(2,1)S(1)} %broadcast_in_dim.51), channel_id=1, replica_groups=mesh['dh'=2,'dl'=8,'lat'=2] {'lat'}, dimensions={0} | all-to-all | bytes 4194304 | tf_op jit(solution)/shard_map/all_to_all | solution.py:69
  229.4 5.9 %bitcast_convert_fusion.1 = bf16[16,1024,128]{2,1,0:T(8,128)(2,1)S(1)} fusion(bf16[16,128,4,128]{3,1,2,0:T(8,128)(2,1)S(1)} %bitcast.165, s32[16,128,4]{1,2,0:T(4,128)S(1)} %copy.274), kind=kOutput, calls=%fused_computation.24 | convolution fusion | flops 2157969408 | bytes 6324224 | tf_op jit(solution)/shard_map/btkq,btkl->bql/dot_general | solution.py:113
  237.4 5.6 %convert_bitcast_fusion = bf16[16,32,32,256]{3,2,0,1:T(8,128)(2,1)} fusion(bf16[16,32,32,128]{3,2,1,0:T(8,128)(2,1)S(1)} %bitcast.142, bf16[32,128,256]{2,1,0:T(8,128)(2,1)S(1)} %all-to-all-done.1), kind=kOutput, calls=%fused_computation.29 | convolution fusion | flops 1077936128 | bytes 14680064 | tf_op jit(solution)/shard_map/borl,olf->borf/dot_general | solution.py:132
  242.9 8.2 %copy.286 = bf16[16,32,32,256]{3,2,1,0:T(8,128)(2,1)} copy(bf16[16,32,32,256]{3,2,0,1:T(8,128)(2,1)} %convert_bitcast_fusion) | data formatting | bytes 16777216 | tf_op jit(solution)/shard_map/convert_element_type | solution.py:133
  251.1 7.1 %add_convert_fusion = (bf16[16,128,256]{2,1,0:T(8,128)(2,1)}, f32[256]{0:T(256)S(1)}, f32[16,128,256]{2,1,0:T(8,128)}) fusion(f32[256]{0:T(256)S(1)} %dynamic_slice.10, bf16[16,132,256]{2,1,0:T(8,128)(2,1)} %copy-done.5, bf16[16,128,1024]{1,2,0:T(8,128)(2,1)S(1)} %copy-done.2, bf16[16,1024,256]{2,1,0:T(8,128)(2,1)} %bitcast.139), kind=kOutput, calls=%fused_computation.50 | convolution fusion | flops 1076363008 | bytes 16779264 | tf_op jit(solution)/shard_map/btq,bqf->btf/dot_general | solution.py:134
  258.3 4.0 convolution_convert_fusion
  262.3 5.7 %fusion.22 = f32[16,32,32,128]{3,2,0,1:T(8,128)} fusion(bf16[16,32,32,256]{3,2,1,0:T(8,128)(2,1)S(1)} %bitcast.135, bf16[32,128,256]{2,1,0:T(8,128)(2,1)S(1)} %all-to-all-done.1), kind=kOutput, calls=%fused_computation.41 | convolution fusion | flops 1073741824 | bytes 18874368 | tf_op jit(solution)/shard_map/borf,olf->borl/dot_general | solution.py:149
  268.0 8.0 %copy.290 = f32[16,32,32,128]{3,2,1,0:T(8,128)} copy(f32[16,32,32,128]{3,2,0,1:T(8,128)} %fusion.22) | data formatting | bytes 16777216 | tf_op jit(solution)/shard_map/borf,olf->borl/transpose | solution.py:149
  276.0 8.9 %reduce-precision_convert_fusion = (bf16[16,1024,128]{2,1,0:T(8,128)(2,1)}, bf16[16,1024,128]{2,1,0:T(8,128)(2,1)}) fusion(f32[16,32,32,128]{3,2,1,0:T(8,128)} %copy.290), kind=kLoop, calls=%fused_computation.12 | loop fusion | flops 8388608 | bytes 16777216 | tf_op jit(solution)/shard_map/convert_element_type | solution.py:32
  284.9 15.6 %fusion.1 = f32[16,128,4,256]{3,1,2,0:T(8,128)} fusion(s32[16,128,4]{1,2,0:T(4,128)S(1)} %copy.274, bf16[16,1024,128]{2,1,0:T(8,128)(2,1)} %get-tuple-element.41, bf16[16,1024,128]{2,1,0:T(8,128)(2,1)} %get-tuple-element.40), kind=kOutput, calls=%fused_computation.2 | convolution fusion | flops 4320133120 | bytes 16809984 | tf_op jit(solution)/shard_map/btkq,bql->btkl/dot_general | solution.py:107
  300.5 4.2 slice_add_fusion
  305.0 8.5 %all_to_all.84 = f32[2,16,64,4,128]{4,2,3,1,0:T(8,128)} all-to-all(f32[2,16,64,4,128]{4,2,3,1,0:T(8,128)S(1)} %bitcast.145), channel_id=1, replica_groups=mesh['dh'=2,'dl'=8,'lat'=2] {'lat'}, dimensions={0} | all-to-all | bytes 8388608 | tf_op jit(solution)/shard_map/all_to_all | solution.py:58
  313.6 2.8 reduce_sum.124
  317.8 29.6 %all_to_all.85 = f32[8,2,64,4,128]{4,3,2,1,0:T(4,128)S(1)} all-to-all(f32[8,2,64,4,128]{4,3,2,1,0:T(4,128)S(1)} %bitcast.152), channel_id=1, replica_groups=mesh['dh'=2,'dl'=8,'lat'=2] {'dl'}, dimensions={0} | all-to-all | bytes 4194304 | tf_op jit(solution)/shard_map/all_to_all | solution.py:60
  347.8 10.2 %all_to_all.86 = f32[2,64,4,128]{3,2,1,0:T(4,128)S(1)} all-to-all(f32[2,64,4,128]{3,2,1,0:T(4,128)S(1)} %reduce_sum.125), channel_id=1, replica_groups=mesh['dh'=2,'dl'=8,'lat'=2] {'dh'}, dimensions={0} | all-to-all | bytes 524288 | tf_op jit(solution)/shard_map/all_to_all | solution.py:61
  360.9 3.4 all-to-all-start.12
  364.4 5.2 %all-to-all-done.12 = bf16[2,64,4,128]{3,1,2,0:T(8,128)(2,1)S(1)} async-done(((bf16[2,64,4,128]{3,1,2,0:T(8,128)(2,1)}), bf16[2,64,4,128]{3,1,2,0:T(8,128)(2,1)S(1)}, u32[]{:S(2)}, u32[]{:S(2)}) %all-to-all-start.12) | async-done | bytes 131104 | tf_op jit(solution)/shard_map/all_to_all | solution.py:64
  370.8 3.6 all-to-all-start.13
  375.7 8.1 %fusion.56 = f32[32,128,256,1]{2,1,0,3:T(8,128)} fusion(bf16[16,32,32,128]{3,2,1,0:T(8,128)(2,1)} %bitcast.143, bf16[16,32,32,256]{3,2,1,0:T(8,128)(2,1)} %bitcast.136), kind=kOutput, calls=%fused_computation.125 | convolution fusion | flops 1073741824 | bytes 16777216 | tf_op jit(solution)/shard_map/borl,borf->olf/dot_general | solution.py:158
  387.1 5.4 %all_to_all.87 = bf16[2,16,64,4,128]{4,2,3,1,0:T(8,128)(2,1)S(1)} all-to-all(bf16[2,16,64,4,128]{4,2,3,1,0:T(8,128)(2,1)S(1)} %broadcast_in_dim.56), channel_id=1, replica_groups=mesh['dh'=2,'dl'=8,'lat'=2] {'lat'}, dimensions={0} | all-to-all | bytes 4194304 | tf_op jit(solution)/shard_map/all_to_all | solution.py:69
  392.5 4.4 all-to-all-start.8
  397.1 5.7 %bitcast_convert_fusion = bf16[16,1024,128]{2,1,0:T(8,128)(2,1)S(1)} fusion(bf16[16,128,4,128]{3,1,2,0:T(8,128)(2,1)S(1)} %bitcast.164, s32[16,128,4]{1,2,0:T(4,128)S(1)} %copy-done.9), kind=kOutput, calls=%fused_computation.23 | convolution fusion | flops 2157969408 | bytes 6324224 | tf_op jit(solution)/shard_map/btkq,btkl->bql/dot_general | solution.py:113
  402.9 5.3 %fusion.20 = bf16[32,128,256]{2,1,0:T(8,128)(2,1)S(1)} fusion(f32[32,128,256,1]{2,1,0,3:T(8,128)S(1)} %copy-done.4, bf16[16,32,32,128]{3,2,1,0:T(8,128)(2,1)S(1)} %bitcast.160, bf16[16,32,32,256]{3,2,1,0:T(8,128)(2,1)} %bitcast.138), kind=kOutput, calls=%fused_computation.36 | convolution fusion | flops 1075838976 | bytes 18874368 | tf_op jit(solution)/shard_map/borl,borf->olf/dot_general | solution.py:159
  409.7 13.1 %all-to-all-done.8 = bf16[16,130,256]{2,1,0:T(8,128)(2,1)S(1)} async-done(((bf16[16,130,256]{2,1,0:T(8,128)(2,1)}), bf16[16,130,256]{2,1,0:T(8,128)(2,1)S(1)}, u32[]{:S(2)}, u32[]{:S(2)}) %all-to-all-start.8) | async-done | bytes 1064992 | tf_op jit(solution)/shard_map/all_to_all | solution.py:143
  422.8 5.4 %all-to-all-start.15 = ((bf16[32,129,256]{2,1,0:T(8,128)(2,1)}), bf16[32,129,256]{2,1,0:T(8,128)(2,1)S(1)}, u32[]{:S(2)}, u32[]{:S(2)}) async-start(bf16[32,129,256]{2,1,0:T(8,128)(2,1)} %pad_maximum_fusion), calls=%async_computation.15 | async-start | bytes 4456448 | tf_op jit(solution)/shard_map/all_to_all | solution.py:164
  434.4 45.5 %all-to-all-done.15 = bf16[32,129,256]{2,1,0:T(8,128)(2,1)S(1)} async-done(((bf16[32,129,256]{2,1,0:T(8,128)(2,1)}), bf16[32,129,256]{2,1,0:T(8,128)(2,1)S(1)}, u32[]{:S(2)}, u32[]{:S(2)}) %all-to-all-start.15) | async-done | bytes 2113568 | tf_op jit(solution)/shard_map/all_to_all | solution.py:164
  481.3 2.7 copy.325
  (105 shorter events, 49.6 us)
Async XLA Ops:
  6.2 34.1 %all-to-all-start = ((bf16[16,132,256]{2,1,0:T(8,128)(2,1)}), bf16[16,132,256]{2,1,0:T(8,128)(2,1)S(1)}, u32[]{:S(2)}, u32[]{:S(2)}) async-start(bf16[16,132,256]{2,1,0:T(8,128)(2,1)} %copy.267), calls=%async_computation | async-start | bytes 2228224 | tf_op jit(solution)/shard_map/all_to_all | solution.py:85
  16.7 29.7 %copy-start.14 = (f32[128]{0:T(128)S(1)}, f32[128]{0:T(128)}, u32[]{:S(2)}) copy-start(f32[128]{0:T(128)} %param.10) | copy-start | bytes 1540
  40.2 1.1 copy-start.5
  41.3 53.8 %all-to-all-start.1 = ((bf16[32,128,256]{2,1,0:T(8,128)(2,1)}), bf16[32,128,256]{2,1,0:T(8,128)(2,1)S(1)}, u32[]{:S(2)}, u32[]{:S(2)}) async-start(bf16[32,128,256]{2,1,0:T(8,128)(2,1)} %bitcast.148), calls=%async_computation.1 | async-start | bytes 4194304 | tf_op jit(solution)/shard_map/all_to_all | solution.py:95
  53.8 231.1 %copy-start.8 = (s32[16,128,4]{1,2,0:T(4,128)}, s32[16,128,4]{1,2,0:T(4,128)S(1)}, u32[]{:S(2)}) copy-start(s32[16,128,4]{1,2,0:T(4,128)S(1)} %copy.274) | copy-start | bytes 98308
  58.5 2.0 copy-start.1
  150.2 36.2 %copy-start.13 = (s32[128,4]{0,1:T(4,128)S(1)}, s32[128,4]{0,1:T(4,128)}, u32[]{:S(2)}) copy-start(s32[128,4]{0,1:T(4,128)} %param.8) | copy-start | bytes 6148
  183.0 11.3 %all-to-all-start.4 = ((f32[2,64,4,128]{3,2,1,0:T(4,128)}), f32[2,64,4,128]{3,2,1,0:T(4,128)S(1)}, u32[]{:S(2)}, u32[]{:S(2)}) async-start(f32[2,64,4,128]{3,2,1,0:T(4,128)} %reduce_sum.120), calls=%async_computation.4 | async-start | bytes 524288 | tf_op jit(solution)/shard_map/all_to_all | solution.py:61
  186.5 23.3 %copy-start.11 = (s32[128]{0:T(128)}, s32[128]{0:T(128)S(1)}, u32[]{:S(2)}) copy-start(s32[128]{0:T(128)S(1)} %get-tuple-element.55) | copy-start | bytes 1540
  186.5 37.3 %copy-start.12 = (s32[128]{0:T(128)}, s32[128]{0:T(128)S(1)}, u32[]{:S(2)}) copy-start(s32[128]{0:T(128)S(1)} %get-tuple-element.56) | copy-start | bytes 1540
  205.4 16.4 %all-to-all-start.6 = ((bf16[8,2,64,4,128]{4,2,3,1,0:T(8,128)(2,1)}), bf16[8,2,64,4,128]{4,2,3,1,0:T(8,128)(2,1)}, u32[]{:S(2)}, u32[]{:S(2)}) async-start(bf16[8,2,64,4,128]{4,2,3,1,0:T(8,128)(2,1)} %broadcast_in_dim.49), calls=%async_computation.6 | async-start | bytes 2097152 | tf_op jit(solution)/shard_map/all_to_all | solution.py:65
  235.3 2.0 copy-start.3
  242.9 8.2 %copy-start.2 = (bf16[16,128,1024]{1,2,0:T(8,128)(2,1)S(1)}, bf16[16,128,1024]{1,2,0:T(8,128)(2,1)}, u32[]{:S(2)}) copy-start(bf16[16,128,1024]{1,2,0:T(8,128)(2,1)} %copy-done.1) | copy-start | bytes 12582916
  251.1 7.1 %copy-start.6 = (bf16[16,132,256]{2,1,0:T(8,128)(2,1)S(1)}, bf16[16,132,256]{2,1,0:T(8,128)(2,1)}, u32[]{:S(2)}) copy-start(bf16[16,132,256]{2,1,0:T(8,128)(2,1)} %copy-done.5) | copy-start | bytes 3244036
  262.2 5.7 %copy-start = (bf16[16,1024,256]{2,1,0:T(8,128)(2,1)}, bf16[16,1024,256]{2,1,0:T(8,128)(2,1)S(1)}, u32[]{:S(2)}) copy-start(bf16[16,1024,256]{2,1,0:T(8,128)(2,1)S(1)} %convolution_convert_fusion) | copy-start | bytes 25165828
  317.8 46.5 %copy-start.10 = (s32[128,4]{0,1:T(4,128)S(1)}, s32[128,4]{0,1:T(4,128)}, u32[]{:S(2)}) copy-start(s32[128,4]{0,1:T(4,128)} %param.7) | copy-start | bytes 6148
  347.4 27.2 %copy-start.7 = (bf16[16,128,256]{2,1,0:T(8,128)(2,1)S(1)}, bf16[16,128,256]{2,1,0:T(8,128)(2,1)}, u32[]{:S(2)}) copy-start(bf16[16,128,256]{2,1,0:T(8,128)(2,1)} %get-tuple-element.44) | copy-start | bytes 3145732
  360.9 8.7 %all-to-all-start.12 = ((bf16[2,64,4,128]{3,1,2,0:T(8,128)(2,1)}), bf16[2,64,4,128]{3,1,2,0:T(8,128)(2,1)S(1)}, u32[]{:S(2)}, u32[]{:S(2)}) async-start(bf16[2,64,4,128]{3,1,2,0:T(8,128)(2,1)} %broadcast_in_dim.53), calls=%async_computation.12 | async-start | bytes 262144 | tf_op jit(solution)/shard_map/all_to_all | solution.py:64
  370.8 15.5 %all-to-all-start.13 = ((bf16[8,2,64,4,128]{4,2,3,1,0:T(8,128)(2,1)}), bf16[8,2,64,4,128]{4,2,3,1,0:T(8,128)(2,1)S(1)}, u32[]{:S(2)}, u32[]{:S(2)}) async-start(bf16[8,2,64,4,128]{4,2,3,1,0:T(8,128)(2,1)} %broadcast_in_dim.54), calls=%async_computation.13 | async-start | bytes 2097152 | tf_op jit(solution)/shard_map/all_to_all | solution.py:65
  392.5 4.6 copy-start.9
  392.5 30.2 %all-to-all-start.8 = ((bf16[16,130,256]{2,1,0:T(8,128)(2,1)}), bf16[16,130,256]{2,1,0:T(8,128)(2,1)S(1)}, u32[]{:S(2)}, u32[]{:S(2)}) async-start(bf16[16,130,256]{2,1,0:T(8,128)(2,1)} %pad_maximum_fusion.2), calls=%async_computation.8 | async-start | bytes 2228224 | tf_op jit(solution)/shard_map/all_to_all | solution.py:143
  397.1 5.8 %copy-start.4 = (f32[32,128,256,1]{2,1,0,3:T(8,128)S(1)}, f32[32,128,256,1]{2,1,0,3:T(8,128)}, u32[]{:S(2)}) copy-start(f32[32,128,256,1]{2,1,0,3:T(8,128)} %fusion.56) | copy-start | bytes 12582916
  422.8 57.1 %all-to-all-start.15 = ((bf16[32,129,256]{2,1,0:T(8,128)(2,1)}), bf16[32,129,256]{2,1,0:T(8,128)(2,1)S(1)}, u32[]{:S(2)}, u32[]{:S(2)}) async-start(bf16[32,129,256]{2,1,0:T(8,128)(2,1)} %pad_maximum_fusion), calls=%async_computation.15 | async-start | bytes 4456448 | tf_op jit(solution)/shard_map/all_to_all | solution.py:164

commit v9 on v8

--- a/solution.py
+++ b/solution.py
@@ -92,7 +92,17 @@
         .transpose(2, 1, 0, 3)
         .reshape(owner_total, lat_own, fs)
     )
-    w_fs = lax.all_to_all(w_send, ALL, 0, 0, tiled=True)
+    bias_vals = 2 * lat_own
+    bias_rows = -(-bias_vals // fs)
+    bias_code = jnp.concatenate(split_hi_lo(enc_bias), axis=0)
+    bias_code = jnp.pad(bias_code, (0, bias_rows * fs - bias_vals)).reshape(bias_rows, fs)
+    w_send = jnp.concatenate(
+        [w_send, jnp.broadcast_to(bias_code[None], (owner_total, bias_rows, fs))], axis=1
+    )
+    w_got = lax.all_to_all(w_send, ALL, 0, 0, tiled=True)
+    w_fs = w_got[:, :lat_own]
+    bias_got = w_got[:, lat_own:].reshape(owner_total, bias_rows * fs)[:, :bias_vals].astype(F32)
+    enc_all = bias_got[:, :lat_own] + bias_got[:, lat_own:]
 
     sel, place = slot_tables(ids_all, owner_total, tok_rows, slot_cap)
 
@@ -115,15 +125,15 @@
 
     acts_slots = rows_to_slots(acts_fs)
     pre_part = jnp.einsum("borf,olf->borl", acts_slots, w_fs, preferred_element_type=F32)
-    own_bias = jnp.where(
-        (jnp.arange(owner_total) == me)[:, None], enc_bias[None, :], 0.0
-    )
-    pre_part = pre_part + own_bias[None, :, None, :]
-    pre = rs_tokens(slots_to_pairs(pre_part))
 
     start = lat_idx * mine_rows
     my_ids = lax.dynamic_slice_in_dim(owner_ids, start, mine_rows, 0)
     my_codes = lax.dynamic_slice_in_dim(block_codes, start, mine_rows, 0)
+    own_hit = (
+        my_ids[:, :, None] == jnp.arange(owner_total, dtype=jnp.int32)[None, None, :]
+    ).astype(F32)
+    pair_bias = jnp.sum(own_hit[:, :, :, None] * enc_all[None, None, :, :], axis=2)
+    pre = rs_tokens(slots_to_pairs(pre_part)) + pair_bias
     lat_block = jnp.arange(lat_own, dtype=jnp.int32) // block_width
     gate = ((my_codes[:, :, None] // (2**lat_block)[None, None, :]) % 2).astype(F32)
     codes = (jnp.maximum(pre, 0.0) * gate).astype(BF16)
@@ -149,9 +159,6 @@
     gc_part = jnp.einsum("borf,olf->borl", gerr_slots, w_fs, preferred_element_type=F32)
     gcodes = rs_tokens(slots_to_pairs(gc_part))
     gpre = gcodes * gate * (pre > 0.0).astype(F32)
-    own_hit = (
-        my_ids[:, :, None] == jnp.arange(owner_total, dtype=jnp.int32)[None, None, :]
-    ).astype(F32)
     genc_part = jnp.sum(own_hit[:, :, :, None] * gpre[:, :, None, :], axis=(0, 1))
 
     gpre_slots = pairs_to_slots(ag_tokens(gpre.astype(BF16)))

time: 490 us -> 502 us (1.024)
  waiting for transfers between devices: 133 us -> 158 us
  blocking collectives: 106 us -> 84.8 us
    all_to_all x2 -> x1, blocking collectives: 59.6 us -> 29.6 us  [rs_tokens(): y = jnp.sum(lax.all_to_all(y, 'dl', 0, 0, tiled=True), axis=0)]
    all_to_all x2, waiting for transfers between devices: 33.1 us -> 56.7 us  [the longest x1 30.8 us: local(): w_got = lax.all_to_all(w_send, ALL, 0, 0, tiled=True)]
    all_to_all x1 -> x2, blocking collectives: 8.33 us -> 16.1 us  [ag_tokens(): lax.all_to_all(jnp.broadcast_to(x[None], (dh_count,) + x.shape), 'dh', 0,...]
    unnamed x40 -> x47, local copies, waits for them, and re-layouts: 16.5 us -> 16.4 us
    convert_element_type x4 -> x5, other arithmetic: 14.3 us -> 14.3 us  [split_hi_lo(): return (hi.astype(BF16), (x - hi).astype(BF16))]
where the time goes in v9:
time: 502 us; the launch traced here: 497 us
  waiting for transfers between devices  158 us (31%)
  matrix products  95.6 us (19%)
  blocking collectives  84.8 us (17%)
  local copies, waits for them, and re-layouts  61.6 us (12%)
  other arithmetic  54.4 us (11%)
  starting transfers between devices  40.7 us (8%)
    all_to_all x1, waiting for transfers between devices, local(): lax.all_to_all(jnp.concatenate([gw.astype(BF16), genc], axis=1), ALL, 0,...  45.5 us
    dot_general x2, matrix products, slots_to_pairs(): out = jnp.einsum('btkq,bql->btkl', sel, both, preferred_element_type=F32)  31.4 us
    all_to_all x1, waiting for transfers between devices, local(): w_got = lax.all_to_all(w_send, ALL, 0, 0, tiled=True)  30.8 us
    all_to_all x1, blocking collectives, rs_tokens(): y = jnp.sum(lax.all_to_all(y, 'dl', 0, 0, tiled=True), axis=0)  29.6 us
    all_to_all x1, waiting for transfers between devices, rs_tokens(): y = jnp.sum(lax.all_to_all(y, 'dl', 0, 0, tiled=True), axis=0)  25.9 us
    all_to_all x1, waiting for transfers between devices, local(): acts_got = lax.all_to_all(acts_send, DP, 0, 0, tiled=True)  20.7 us
    all_to_all x2, blocking collectives, rs_tokens(): y = jnp.sum(lax.all_to_all(y, 'lat', 0, 0, tiled=True), axis=0)  17.1 us
    unnamed x47, local copies, waits for them, and re-layouts  16.4 us
  transfers between devices with their start and end apart: 8, of which 8 were waited for; matrix products, arithmetic and copies ran while one was open for 11% of the time, Pallas kernels for 0%

profile of v9, /device:TPU:0, one launch (start us, length us, event | category | flops | bytes accessed | tf_op | source)
XLA Modules:
  0.0 496.8 jit_solution(4865913315087021040)
XLA Ops:
  6.2 8.3 %all-to-all-start = ((bf16[16,132,256]{2,1,0:T(8,128)(2,1)}), bf16[16,132,256]{2,1,0:T(8,128)(2,1)S(1)}, u32[]{:S(2)}, u32[]{:S(2)}) async-start(bf16[16,132,256]{2,1,0:T(8,128)(2,1)} %copy.270), calls=%async_computation | async-start | bytes 2228224 | tf_op jit(solution)/shard_map/all_to_all | solution.py:85
  19.5 20.7 %all-to-all-done = bf16[16,132,256]{2,1,0:T(8,128)(2,1)S(1)} async-done(((bf16[16,132,256]{2,1,0:T(8,128)(2,1)}), bf16[16,132,256]{2,1,0:T(8,128)(2,1)S(1)}, u32[]{:S(2)}, u32[]{:S(2)}) %all-to-all-start) | async-done | bytes 1081376 | tf_op jit(solution)/shard_map/all_to_all | solution.py:85
  41.2 5.1 %all-to-all-start.1 = ((bf16[32,129,256]{2,1,0:T(8,128)(2,1)}), bf16[32,129,256]{2,1,0:T(8,128)(2,1)S(1)}, u32[]{:S(2)}, u32[]{:S(2)}) async-start(bf16[32,129,256]{2,1,0:T(8,128)(2,1)} %pad_maximum_fusion), calls=%async_computation.1 | async-start | bytes 4456448 | tf_op jit(solution)/shard_map/all_to_all | solution.py:102
  53.7 4.6 fusion.5
  60.3 6.8 %convolution_convert_fusion.1 = bf16[16,1024,256]{2,1,0:T(8,128)(2,1)} fusion(bf16[16,128,1024]{1,2,0:T(8,128)(2,1)S(1)} %fusion.5, bf16[16,132,256]{2,1,0:T(8,128)(2,1)} %copy-done.5), kind=kOutput, calls=%fused_computation.31 | convolution fusion | flops 1077936128 | bytes 13631488 | tf_op jit(solution)/shard_map/btq,btf->bqf/dot_general | solution.py:110
  67.0 30.8 %all-to-all-done.1 = bf16[32,129,256]{2,1,0:T(8,128)(2,1)S(1)} async-done(((bf16[32,129,256]{2,1,0:T(8,128)(2,1)}), bf16[32,129,256]{2,1,0:T(8,128)(2,1)S(1)}, u32[]{:S(2)}, u32[]{:S(2)}) %all-to-all-start.1) | async-done | bytes 2113568 | tf_op jit(solution)/shard_map/all_to_all | solution.py:102
  97.9 9.8 %fusion.22 = f32[16,32,32,128]{3,2,0,1:T(8,128)} fusion(bf16[16,32,32,256]{3,2,1,0:T(8,128)(2,1)} %bitcast.138, bf16[32,129,256]{2,1,0:T(8,128)(2,1)S(1)} %all-to-all-done.1), kind=kOutput, calls=%fused_computation.41 | convolution fusion | flops 1073741824 | bytes 18874368 | tf_op jit(solution)/shard_map/borf,olf->borl/dot_general | solution.py:127
  107.6 4.8 copy.280
  112.4 5.6 %reduce-precision_convert_fusion.1 = (bf16[16,1024,128]{2,1,0:T(8,128)(2,1)}, bf16[16,1024,128]{2,1,0:T(8,128)(2,1)}) fusion(f32[16,32,32,128]{3,2,1,0:T(8,128)S(1)} %copy.280), kind=kLoop, calls=%fused_computation.14 | loop fusion | flops 8388608 | bytes 16777216 | tf_op jit(solution)/shard_map/convert_element_type | solution.py:32
  118.0 15.6 %fusion.3 = f32[16,128,4,256]{3,1,2,0:T(8,128)} fusion(s32[16,128,4]{1,2,0:T(4,128)S(1)} %copy.277, bf16[16,1024,128]{2,1,0:T(8,128)(2,1)} %get-tuple-element.43, bf16[16,1024,128]{2,1,0:T(8,128)(2,1)} %get-tuple-element.42), kind=kOutput, calls=%fused_computation.4 | convolution fusion | flops 4320133120 | bytes 16809984 | tf_op jit(solution)/shard_map/btkq,bql->btkl/dot_general | solution.py:117
  133.6 4.2 slice_add_fusion.1
  138.1 8.6 %all_to_all.80 = f32[2,16,64,4,128]{4,2,3,1,0:T(8,128)} all-to-all(f32[2,16,64,4,128]{4,2,3,1,0:T(8,128)S(1)} %bitcast.143), channel_id=1, replica_groups=mesh['dh'=2,'dl'=8,'lat'=2] {'lat'}, dimensions={0} | all-to-all | bytes 8388608 | tf_op jit(solution)/shard_map/all_to_all | solution.py:58
  146.7 4.1 reduce_sum.128
  150.8 4.3 copy.370
  155.2 4.4 all-to-all-start.3
  160.0 25.9 %all-to-all-done.3 = f32[8,2,64,4,128]{4,3,2,1,0:T(4,128)} async-done(((f32[8,2,64,4,128]{4,3,2,1,0:T(4,128)}), f32[8,2,64,4,128]{4,3,2,1,0:T(4,128)}, u32[]{:S(2)}, u32[]{:S(2)}) %all-to-all-start.3) | async-done | bytes 2097184 | tf_op jit(solution)/shard_map/all_to_all | solution.py:60
  185.9 2.7 reduce_sum.129
  188.6 3.4 all-to-all-start.4
  193.6 7.2 %all-to-all-done.4 = f32[2,64,4,128]{3,2,1,0:T(4,128)S(1)} async-done(((f32[2,64,4,128]{3,2,1,0:T(4,128)}), f32[2,64,4,128]{3,2,1,0:T(4,128)S(1)}, u32[]{:S(2)}, u32[]{:S(2)}) %all-to-all-start.4) | async-done | bytes 262176 | tf_op jit(solution)/shard_map/all_to_all | solution.py:61
  202.4 7.7 %all_to_all.81 = bf16[2,64,4,128]{3,1,2,0:T(8,128)(2,1)S(1)} all-to-all(bf16[2,64,4,128]{3,1,2,0:T(8,128)(2,1)S(1)} %broadcast_in_dim.28), channel_id=1, replica_groups=mesh['dh'=2,'dl'=8,'lat'=2] {'dh'}, dimensions={0} | all-to-all | bytes 262144 | tf_op jit(solution)/shard_map/all_to_all | solution.py:64
  211.3 6.4 %all-to-all-start.6 = ((bf16[8,2,64,4,128]{4,2,3,1,0:T(8,128)(2,1)}), bf16[8,2,64,4,128]{4,2,3,1,0:T(8,128)(2,1)}, u32[]{:S(2)}, u32[]{:S(2)}) async-start(bf16[8,2,64,4,128]{4,2,3,1,0:T(8,128)(2,1)} %broadcast_in_dim.29), calls=%async_computation.6 | async-start | bytes 2097152 | tf_op jit(solution)/shard_map/all_to_all | solution.py:65
  219.1 13.6 %all-to-all-done.6 = bf16[8,2,64,4,128]{4,2,3,1,0:T(8,128)(2,1)} async-done(((bf16[8,2,64,4,128]{4,2,3,1,0:T(8,128)(2,1)}), bf16[8,2,64,4,128]{4,2,3,1,0:T(8,128)(2,1)}, u32[]{:S(2)}, u32[]{:S(2)}) %all-to-all-start.6) | async-done | bytes 1048608 | tf_op jit(solution)/shard_map/all_to_all | solution.py:65
  234.7 5.4 %all_to_all.82 = bf16[2,16,64,4,128]{4,2,3,1,0:T(8,128)(2,1)S(1)} all-to-all(bf16[2,16,64,4,128]{4,2,3,1,0:T(8,128)(2,1)S(1)} %broadcast_in_dim.31), channel_id=1, replica_groups=mesh['dh'=2,'dl'=8,'lat'=2] {'lat'}, dimensions={0} | all-to-all | bytes 4194304 | tf_op jit(solution)/shard_map/all_to_all | solution.py:69
  240.3 5.9 %bitcast_convert_fusion.1 = bf16[16,1024,128]{2,1,0:T(8,128)(2,1)S(1)} fusion(bf16[16,128,4,128]{3,1,2,0:T(8,128)(2,1)S(1)} %bitcast.166, s32[16,128,4]{1,2,0:T(4,128)S(1)} %copy.277), kind=kOutput, calls=%fused_computation.24 | convolution fusion | flops 2157969408 | bytes 6324224 | tf_op jit(solution)/shard_map/btkq,btkl->bql/dot_general | solution.py:123
  248.3 5.6 %convert_bitcast_fusion = bf16[16,32,32,256]{3,2,0,1:T(8,128)(2,1)} fusion(bf16[16,32,32,128]{3,2,1,0:T(8,128)(2,1)S(1)} %bitcast.159, bf16[32,129,256]{2,1,0:T(8,128)(2,1)S(1)} %all-to-all-done.1), kind=kOutput, calls=%fused_computation.29 | convolution fusion | flops 1077936128 | bytes 14680064 | tf_op jit(solution)/shard_map/borl,olf->borf/dot_general | solution.py:142
  253.9 8.2 %copy.291 = bf16[16,32,32,256]{3,2,1,0:T(8,128)(2,1)} copy(bf16[16,32,32,256]{3,2,0,1:T(8,128)(2,1)} %convert_bitcast_fusion) | data formatting | bytes 16777216 | tf_op jit(solution)/shard_map/convert_element_type | solution.py:143
  262.0 5.9 %add_convert_fusion = (bf16[16,128,256]{2,1,0:T(8,128)(2,1)}, f32[256]{0:T(256)S(1)}, f32[16,128,256]{2,1,0:T(8,128)S(1)}) fusion(f32[256]{0:T(256)S(1)} %copy-done.10, bf16[16,132,256]{2,1,0:T(8,128)(2,1)S(1)} %copy-done.6, bf16[16,128,1024]{1,2,0:T(8,128)(2,1)S(1)} %copy-done.2, bf16[16,1024,256]{2,1,0:T(8,128)(2,1)} %bitcast.140), kind=kOutput, calls=%fused_computation.50 | convolution fusion | flops 1076363008 | bytes 16779264 | tf_op jit(solution)/shard_map/btq,bqf->btf/dot_general | solution.py:144
  268.0 2.4 convolution_convert_fusion
  270.4 8.7 %fusion.25 = f32[16,32,32,128]{3,2,0,1:T(8,128)} fusion(bf16[16,32,32,256]{3,2,1,0:T(8,128)(2,1)S(1)} %bitcast.136, bf16[32,129,256]{2,1,0:T(8,128)(2,1)} %copy-done.3), kind=kOutput, calls=%fused_computation.42 | convolution fusion | flops 1073741824 | bytes 18874368 | tf_op jit(solution)/shard_map/borf,olf->borl/dot_general | solution.py:159
  279.1 8.0 %copy.295 = f32[16,32,32,128]{3,2,1,0:T(8,128)} copy(f32[16,32,32,128]{3,2,0,1:T(8,128)} %fusion.25) | data formatting | bytes 16777216 | tf_op jit(solution)/shard_map/borf,olf->borl/transpose | solution.py:159
  287.1 8.7 %reduce-precision_convert_fusion = (bf16[16,1024,128]{2,1,0:T(8,128)(2,1)}, bf16[16,1024,128]{2,1,0:T(8,128)(2,1)}) fusion(f32[16,32,32,128]{3,2,1,0:T(8,128)} %copy.295), kind=kLoop, calls=%fused_computation.12 | loop fusion | flops 8388608 | bytes 16777216 | tf_op jit(solution)/shard_map/convert_element_type | solution.py:32
  295.8 15.8 %fusion.1 = f32[16,128,4,256]{3,1,2,0:T(8,128)} fusion(s32[16,128,4]{1,2,0:T(4,128)S(1)} %copy.277, bf16[16,1024,128]{2,1,0:T(8,128)(2,1)} %get-tuple-element.41, bf16[16,1024,128]{2,1,0:T(8,128)(2,1)} %get-tuple-element.40), kind=kOutput, calls=%fused_computation.2 | convolution fusion | flops 4320133120 | bytes 16809984 | tf_op jit(solution)/shard_map/btkq,bql->btkl/dot_general | solution.py:117
  311.6 4.2 slice_add_fusion
  316.2 8.5 %all_to_all.83 = f32[2,16,64,4,128]{4,2,3,1,0:T(8,128)} all-to-all(f32[2,16,64,4,128]{4,2,3,1,0:T(8,128)S(1)} %bitcast.144), channel_id=1, replica_groups=mesh['dh'=2,'dl'=8,'lat'=2] {'lat'}, dimensions={0} | all-to-all | bytes 8388608 | tf_op jit(solution)/shard_map/all_to_all | solution.py:58
  324.7 2.8 reduce_sum.134
  329.0 29.6 %all_to_all.84 = f32[8,2,64,4,128]{4,3,2,1,0:T(4,128)S(1)} all-to-all(f32[8,2,64,4,128]{4,3,2,1,0:T(4,128)S(1)} %bitcast.151), channel_id=1, replica_groups=mesh['dh'=2,'dl'=8,'lat'=2] {'dl'}, dimensions={0} | all-to-all | bytes 4194304 | tf_op jit(solution)/shard_map/all_to_all | solution.py:60
  359.7 11.2 %all_to_all.85 = f32[2,64,4,128]{3,2,1,0:T(4,128)S(1)} all-to-all(f32[2,64,4,128]{3,2,1,0:T(4,128)} %reduce_sum.135), channel_id=1, replica_groups=mesh['dh'=2,'dl'=8,'lat'=2] {'dh'}, dimensions={0} | all-to-all | bytes 524288 | tf_op jit(solution)/shard_map/all_to_all | solution.py:61
  373.4 8.3 %all_to_all.86 = bf16[2,64,4,128]{3,1,2,0:T(8,128)(2,1)S(1)} all-to-all(bf16[2,64,4,128]{3,1,2,0:T(8,128)(2,1)S(1)} %broadcast_in_dim.33), channel_id=1, replica_groups=mesh['dh'=2,'dl'=8,'lat'=2] {'dh'}, dimensions={0} | all-to-all | bytes 262144 | tf_op jit(solution)/shard_map/all_to_all | solution.py:64
  382.9 3.6 all-to-all-start.13
  387.6 8.1 %fusion.55 = f32[32,128,256,1]{2,1,0,3:T(8,128)} fusion(bf16[16,32,32,128]{3,2,1,0:T(8,128)(2,1)} %bitcast.160, bf16[16,32,32,256]{3,2,1,0:T(8,128)(2,1)} %bitcast.137), kind=kOutput, calls=%fused_computation.131 | convolution fusion | flops 1073741824 | bytes 16777216 | tf_op jit(solution)/shard_map/borl,borf->olf/dot_general | solution.py:165
  399.3 5.4 %all_to_all.87 = bf16[2,16,64,4,128]{4,2,3,1,0:T(8,128)(2,1)S(1)} all-to-all(bf16[2,16,64,4,128]{4,2,3,1,0:T(8,128)(2,1)S(1)} %broadcast_in_dim.36), channel_id=1, replica_groups=mesh['dh'=2,'dl'=8,'lat'=2] {'lat'}, dimensions={0} | all-to-all | bytes 4194304 | tf_op jit(solution)/shard_map/all_to_all | solution.py:69
  404.7 4.0 all-to-all-start.8
  408.9 5.7 %bitcast_convert_fusion = bf16[16,1024,128]{2,1,0:T(8,128)(2,1)S(1)} fusion(bf16[16,128,4,128]{3,1,2,0:T(8,128)(2,1)S(1)} %bitcast.165, s32[16,128,4]{1,2,0:T(4,128)S(1)} %copy.277), kind=kOutput, calls=%fused_computation.23 | convolution fusion | flops 2157969408 | bytes 6324224 | tf_op jit(solution)/shard_map/btkq,btkl->bql/dot_general | solution.py:123
  414.7 5.3 %fusion.20 = bf16[32,128,256]{2,1,0:T(8,128)(2,1)S(1)} fusion(f32[32,128,256,1]{2,1,0,3:T(8,128)S(1)} %copy-done.4, bf16[16,32,32,128]{3,2,1,0:T(8,128)(2,1)S(1)} %bitcast.161, bf16[16,32,32,256]{3,2,1,0:T(8,128)(2,1)} %bitcast.139), kind=kOutput, calls=%fused_computation.35 | convolution fusion | flops 1075838976 | bytes 18874368 | tf_op jit(solution)/shard_map/borl,borf->olf/dot_general | solution.py:166
  421.5 13.1 %all-to-all-done.8 = bf16[16,130,256]{2,1,0:T(8,128)(2,1)S(1)} async-done(((bf16[16,130,256]{2,1,0:T(8,128)(2,1)}), bf16[16,130,256]{2,1,0:T(8,128)(2,1)S(1)}, u32[]{:S(2)}, u32[]{:S(2)}) %all-to-all-start.8) | async-done | bytes 1064992 | tf_op jit(solution)/shard_map/all_to_all | solution.py:153
  434.6 5.5 %all-to-all-start.15 = ((bf16[32,129,256]{2,1,0:T(8,128)(2,1)}), bf16[32,129,256]{2,1,0:T(8,128)(2,1)S(1)}, u32[]{:S(2)}, u32[]{:S(2)}) async-start(bf16[32,129,256]{2,1,0:T(8,128)(2,1)} %pad_maximum_fusion.1), calls=%async_computation.15 | async-start | bytes 4456448 | tf_op jit(solution)/shard_map/all_to_all | solution.py:171
  446.4 45.5 %all-to-all-done.15 = bf16[32,129,256]{2,1,0:T(8,128)(2,1)S(1)} async-done(((bf16[32,129,256]{2,1,0:T(8,128)(2,1)}), bf16[32,129,256]{2,1,0:T(8,128)(2,1)S(1)}, u32[]{:S(2)}, u32[]{:S(2)}) %all-to-all-start.15) | async-done | bytes 2113568 | tf_op jit(solution)/shard_map/all_to_all | solution.py:171
  493.3 2.7 copy.330
  (117 shorter events, 52.3 us)
Async XLA Ops:
  6.2 34.1 %all-to-all-start = ((bf16[16,132,256]{2,1,0:T(8,128)(2,1)}), bf16[16,132,256]{2,1,0:T(8,128)(2,1)S(1)}, u32[]{:S(2)}, u32[]{:S(2)}) async-start(bf16[16,132,256]{2,1,0:T(8,128)(2,1)} %copy.270), calls=%async_computation | async-start | bytes 2228224 | tf_op jit(solution)/shard_map/all_to_all | solution.py:85
  14.5 3.4 copy-start.17
  40.2 1.0 copy-start.5
  41.2 56.6 %all-to-all-start.1 = ((bf16[32,129,256]{2,1,0:T(8,128)(2,1)}), bf16[32,129,256]{2,1,0:T(8,128)(2,1)S(1)}, u32[]{:S(2)}, u32[]{:S(2)}) async-start(bf16[32,129,256]{2,1,0:T(8,128)(2,1)} %pad_maximum_fusion), calls=%async_computation.1 | async-start | bytes 4456448 | tf_op jit(solution)/shard_map/all_to_all | solution.py:102
  58.3 1.9 copy-start.1
  97.9 148.4 %copy-start.3 = (bf16[32,129,256]{2,1,0:T(8,128)(2,1)}, bf16[32,129,256]{2,1,0:T(8,128)(2,1)S(1)}, u32[]{:S(2)}) copy-start(bf16[32,129,256]{2,1,0:T(8,128)(2,1)S(1)} %all-to-all-done.1) | copy-start | bytes 6340612
  150.8 8.7 %copy-start.11 = (s32[128,4]{0,1:T(4,128)S(1)}, s32[128,4]{0,1:T(4,128)}, u32[]{:S(2)}) copy-start(s32[128,4]{0,1:T(4,128)} %param.7) | copy-start | bytes 6148
  150.8 8.9 %copy-start.16 = (s32[128,4]{0,1:T(4,128)S(1)}, s32[128,4]{0,1:T(4,128)}, u32[]{:S(2)}) copy-start(s32[128,4]{0,1:T(4,128)} %param.8) | copy-start | bytes 6148
  155.2 30.8 %all-to-all-start.3 = ((f32[8,2,64,4,128]{4,3,2,1,0:T(4,128)}), f32[8,2,64,4,128]{4,3,2,1,0:T(4,128)}, u32[]{:S(2)}, u32[]{:S(2)}) async-start(f32[8,2,64,4,128]{4,3,2,1,0:T(4,128)} %bitcast.147), calls=%async_computation.3 | async-start | bytes 4194304 | tf_op jit(solution)/shard_map/all_to_all | solution.py:60
  159.7 74.3 %copy-start.12 = (s32[128]{0:T(128)}, s32[128]{0:T(128)S(1)}, u32[]{:S(2)}) copy-start(s32[128]{0:T(128)S(1)} %get-tuple-element.57) | copy-start | bytes 1540
  159.8 74.3 %copy-start.14 = (s32[128]{0:T(128)}, s32[128]{0:T(128)S(1)}, u32[]{:S(2)}) copy-start(s32[128]{0:T(128)S(1)} %get-tuple-element.58) | copy-start | bytes 1540
  188.6 12.2 %all-to-all-start.4 = ((f32[2,64,4,128]{3,2,1,0:T(4,128)}), f32[2,64,4,128]{3,2,1,0:T(4,128)S(1)}, u32[]{:S(2)}, u32[]{:S(2)}) async-start(f32[2,64,4,128]{3,2,1,0:T(4,128)} %reduce_sum.129), calls=%async_computation.4 | async-start | bytes 524288 | tf_op jit(solution)/shard_map/all_to_all | solution.py:61
  200.9 33.8 %copy-start.9 = (f32[64,4,128]{2,1,0:T(4,128)}, f32[64,4,128]{2,1,0:T(4,128)S(1)}, u32[]{:S(2)}) copy-start(f32[64,4,128]{2,1,0:T(4,128)S(1)} %reduce_sum.130) | copy-start | bytes 393220
  211.3 21.4 %all-to-all-start.6 = ((bf16[8,2,64,4,128]{4,2,3,1,0:T(8,128)(2,1)}), bf16[8,2,64,4,128]{4,2,3,1,0:T(8,128)(2,1)}, u32[]{:S(2)}, u32[]{:S(2)}) async-start(bf16[8,2,64,4,128]{4,2,3,1,0:T(8,128)(2,1)} %broadcast_in_dim.29), calls=%async_computation.6 | async-start | bytes 2097152 | tf_op jit(solution)/shard_map/all_to_all | solution.py:65
  246.2 2.0 copy-start.8
  253.8 8.2 %copy-start.2 = (bf16[16,128,1024]{1,2,0:T(8,128)(2,1)S(1)}, bf16[16,128,1024]{1,2,0:T(8,128)(2,1)}, u32[]{:S(2)}) copy-start(bf16[16,128,1024]{1,2,0:T(8,128)(2,1)} %copy-done.1) | copy-start | bytes 12582916
  253.8 8.2 %copy-start.6 = (bf16[16,132,256]{2,1,0:T(8,128)(2,1)S(1)}, bf16[16,132,256]{2,1,0:T(8,128)(2,1)}, u32[]{:S(2)}) copy-start(bf16[16,132,256]{2,1,0:T(8,128)(2,1)} %copy-done.5) | copy-start | bytes 3244036
  253.9 8.2 %copy-start.10 = (f32[256]{0:T(256)S(1)}, f32[256]{0:T(256)}, u32[]{:S(2)}) copy-start(f32[256]{0:T(256)} %dynamic_slice.11) | copy-start | bytes 3076
  270.4 8.8 %copy-start = (bf16[16,1024,256]{2,1,0:T(8,128)(2,1)}, bf16[16,1024,256]{2,1,0:T(8,128)(2,1)S(1)}, u32[]{:S(2)}) copy-start(bf16[16,1024,256]{2,1,0:T(8,128)(2,1)S(1)} %convolution_convert_fusion) | copy-start | bytes 25165828
  328.9 42.0 %copy-start.13 = (s32[128]{0:T(128)S(1)}, s32[128]{0:T(128)}, u32[]{:S(2)}) copy-start(s32[128]{0:T(128)} %copy-done.12) | copy-start | bytes 1540
  328.9 42.0 %copy-start.15 = (s32[128]{0:T(128)S(1)}, s32[128]{0:T(128)}, u32[]{:S(2)}) copy-start(s32[128]{0:T(128)} %copy-done.14) | copy-start | bytes 1540
  358.5 28.0 %copy-start.7 = (bf16[16,128,256]{2,1,0:T(8,128)(2,1)S(1)}, bf16[16,128,256]{2,1,0:T(8,128)(2,1)}, u32[]{:S(2)}) copy-start(bf16[16,128,256]{2,1,0:T(8,128)(2,1)} %get-tuple-element.44) | copy-start | bytes 3145732
  382.9 15.6 %all-to-all-start.13 = ((bf16[8,2,64,4,128]{4,2,3,1,0:T(8,128)(2,1)}), bf16[8,2,64,4,128]{4,2,3,1,0:T(8,128)(2,1)S(1)}, u32[]{:S(2)}, u32[]{:S(2)}) async-start(bf16[8,2,64,4,128]{4,2,3,1,0:T(8,128)(2,1)} %broadcast_in_dim.34), calls=%async_computation.13 | async-start | bytes 2097152 | tf_op jit(solution)/shard_map/all_to_all | solution.py:65
  404.7 29.9 %all-to-all-start.8 = ((bf16[16,130,256]{2,1,0:T(8,128)(2,1)}), bf16[16,130,256]{2,1,0:T(8,128)(2,1)S(1)}, u32[]{:S(2)}, u32[]{:S(2)}) async-start(bf16[16,130,256]{2,1,0:T(8,128)(2,1)} %pad_maximum_fusion.3), calls=%async_computation.8 | async-start | bytes 2228224 | tf_op jit(solution)/shard_map/all_to_all | solution.py:153
  408.9 5.8 %copy-start.4 = (f32[32,128,256,1]{2,1,0,3:T(8,128)S(1)}, f32[32,128,256,1]{2,1,0,3:T(8,128)}, u32[]{:S(2)}) copy-start(f32[32,128,256,1]{2,1,0,3:T(8,128)} %fusion.55) | copy-start | bytes 12582916
  434.6 57.3 %all-to-all-start.15 = ((bf16[32,129,256]{2,1,0:T(8,128)(2,1)}), bf16[32,129,256]{2,1,0:T(8,128)(2,1)S(1)}, u32[]{:S(2)}, u32[]{:S(2)}) async-start(bf16[32,129,256]{2,1,0:T(8,128)(2,1)} %pad_maximum_fusion.1), calls=%async_computation.15 | async-start | bytes 4456448 | tf_op jit(solution)/shard_map/all_to_all | solution.py:171

commit v10 on v8

--- a/solution.py
+++ b/solution.py
@@ -115,11 +115,8 @@
 
     acts_slots = rows_to_slots(acts_fs)
     pre_part = jnp.einsum("borf,olf->borl", acts_slots, w_fs, preferred_element_type=F32)
-    own_bias = jnp.where(
-        (jnp.arange(owner_total) == me)[:, None], enc_bias[None, :], 0.0
-    )
-    pre_part = pre_part + own_bias[None, :, None, :]
-    pre = rs_tokens(slots_to_pairs(pre_part))
+    own_bias = jnp.where((ids_all == me)[:, :, None], enc_bias[None, None, :], 0.0)
+    pre = rs_tokens(slots_to_pairs(pre_part) + own_bias)
 
     start = lat_idx * mine_rows
     my_ids = lax.dynamic_slice_in_dim(owner_ids, start, mine_rows, 0)

time: 490 us -> 490 us (level)
    transpose x0 -> x1, local copies, waits for them, and re-layouts: none -> 5 us  [local(): jnp.einsum('borf,olf->borl', acts_slots, w_fs, preferred_element_type=F32)]
    add x1 -> x0, local copies, waits for them, and re-layouts: 5 us -> none  [local(): pre_part = pre_part + own_bias[None, :, None, :]]
where the time goes in v10:
time: 490 us; the launch traced here: 486 us
  waiting for transfers between devices  133 us (27%)
  blocking collectives  106 us (22%)
  matrix products  94.3 us (19%)
  local copies, waits for them, and re-layouts  61.7 us (13%)
  other arithmetic  52 us (11%)
  starting transfers between devices  37.8 us (8%)
    all_to_all x2, blocking collectives, rs_tokens(): y = jnp.sum(lax.all_to_all(y, 'dl', 0, 0, tiled=True), axis=0)  59.6 us
    all_to_all x1, waiting for transfers between devices, local(): lax.all_to_all(jnp.concatenate([gw.astype(BF16), genc], axis=1), ALL, 0,...  45.5 us
    dot_general x2, matrix products, slots_to_pairs(): out = jnp.einsum('btkq,bql->btkl', sel, both, preferred_element_type=F32)  31.1 us
    all_to_all x1, waiting for transfers between devices, local(): w_fs = lax.all_to_all(w_send, ALL, 0, 0, tiled=True)  27.8 us
    all_to_all x1, waiting for transfers between devices, local(): acts_got = lax.all_to_all(acts_send, DP, 0, 0, tiled=True)  21 us
    all_to_all x2, blocking collectives, rs_tokens(): y = jnp.sum(lax.all_to_all(y, 'lat', 0, 0, tiled=True), axis=0)  16.7 us
    unnamed x40, local copies, waits for them, and re-layouts  16.4 us
    convert_element_type x4, other arithmetic, split_hi_lo(): return (hi.astype(BF16), (x - hi).astype(BF16))  14.3 us
  transfers between devices with their start and end apart: 8, of which 8 were waited for; matrix products, arithmetic and copies ran while one was open for 11% of the time, Pallas kernels for 0%

profile of v10, /device:TPU:0, one launch (start us, length us, event | category | flops | bytes accessed | tf_op | source)
XLA Modules:
  0.0 485.7 jit_solution(9032080853754908319)
XLA Ops:
  6.2 8.3 %all-to-all-start = ((bf16[16,132,256]{2,1,0:T(8,128)(2,1)}), bf16[16,132,256]{2,1,0:T(8,128)(2,1)S(1)}, u32[]{:S(2)}, u32[]{:S(2)}) async-start(bf16[16,132,256]{2,1,0:T(8,128)(2,1)} %copy.281), calls=%async_computation | async-start | bytes 2228224 | tf_op jit(solution)/shard_map/all_to_all | solution.py:85
  19.2 21.0 %all-to-all-done = bf16[16,132,256]{2,1,0:T(8,128)(2,1)S(1)} async-done(((bf16[16,132,256]{2,1,0:T(8,128)(2,1)}), bf16[16,132,256]{2,1,0:T(8,128)(2,1)S(1)}, u32[]{:S(2)}, u32[]{:S(2)}) %all-to-all-start) | async-done | bytes 1081376 | tf_op jit(solution)/shard_map/all_to_all | solution.py:85
  41.3 5.1 %all-to-all-start.1 = ((bf16[32,128,256]{2,1,0:T(8,128)(2,1)}), bf16[32,128,256]{2,1,0:T(8,128)(2,1)S(1)}, u32[]{:S(2)}, u32[]{:S(2)}) async-start(bf16[32,128,256]{2,1,0:T(8,128)(2,1)} %bitcast.150), calls=%async_computation.1 | async-start | bytes 4194304 | tf_op jit(solution)/shard_map/all_to_all | solution.py:95
  53.9 4.6 fusion.5
  60.5 6.8 %convolution_convert_fusion.1 = bf16[16,1024,256]{2,1,0:T(8,128)(2,1)} fusion(bf16[16,128,1024]{1,2,0:T(8,128)(2,1)S(1)} %fusion.5, bf16[16,132,256]{2,1,0:T(8,128)(2,1)} %copy-done.5), kind=kOutput, calls=%fused_computation.31 | convolution fusion | flops 1077936128 | bytes 13631488 | tf_op jit(solution)/shard_map/btq,btf->bqf/dot_general | solution.py:100
  67.3 27.8 %all-to-all-done.1 = bf16[32,128,256]{2,1,0:T(8,128)(2,1)S(1)} async-done(((bf16[32,128,256]{2,1,0:T(8,128)(2,1)}), bf16[32,128,256]{2,1,0:T(8,128)(2,1)S(1)}, u32[]{:S(2)}, u32[]{:S(2)}) %all-to-all-start.1) | async-done | bytes 2097184 | tf_op jit(solution)/shard_map/all_to_all | solution.py:95
  95.1 9.0 %fusion.23 = f32[16,32,32,128]{3,2,0,1:T(8,128)} fusion(bf16[16,32,32,256]{3,2,1,0:T(8,128)(2,1)} %bitcast.140, bf16[32,128,256]{2,1,0:T(8,128)(2,1)S(1)} %all-to-all-done.1), kind=kOutput, calls=%fused_computation.41 | convolution fusion | flops 1073741824 | bytes 18874368 | tf_op jit(solution)/shard_map/borf,olf->borl/dot_general | solution.py:117
  104.1 5.0 %copy.291 = f32[16,32,32,128]{3,2,1,0:T(8,128)S(1)} copy(f32[16,32,32,128]{3,2,0,1:T(8,128)} %fusion.23) | data formatting | bytes 16777216 | tf_op jit(solution)/shard_map/borf,olf->borl/transpose | solution.py:117
  109.1 5.4 %reduce-precision_convert_fusion.1 = (bf16[16,1024,128]{2,1,0:T(8,128)(2,1)}, bf16[16,1024,128]{2,1,0:T(8,128)(2,1)}) fusion(f32[16,32,32,128]{3,2,1,0:T(8,128)S(1)} %copy.291), kind=kLoop, calls=%fused_computation.14 | loop fusion | flops 8388608 | bytes 16777216 | tf_op jit(solution)/shard_map/convert_element_type | solution.py:32
  114.4 15.6 %fusion.3 = f32[16,128,4,256]{3,1,2,0:T(8,128)} fusion(s32[16,128,4]{1,2,0:T(4,128)S(1)} %copy.288, bf16[16,1024,128]{2,1,0:T(8,128)(2,1)} %get-tuple-element.43, bf16[16,1024,128]{2,1,0:T(8,128)(2,1)} %get-tuple-element.42), kind=kOutput, calls=%fused_computation.4 | convolution fusion | flops 4320133120 | bytes 16809984 | tf_op jit(solution)/shard_map/btkq,bql->btkl/dot_general | solution.py:107
  130.0 4.2 slice_add_fusion.1
  135.8 8.2 %all_to_all.80 = f32[2,16,64,4,128]{4,2,3,1,0:T(8,128)} all-to-all(f32[2,16,64,4,128]{4,2,3,1,0:T(8,128)S(1)} %fusion.22), channel_id=1, replica_groups=mesh['dh'=2,'dl'=8,'lat'=2] {'lat'}, dimensions={0} | all-to-all | bytes 8388608 | tf_op jit(solution)/shard_map/all_to_all | solution.py:58
  144.0 4.1 reduce_sum.119
  148.1 3.0 copy.371
  151.1 30.0 %all_to_all.81 = f32[8,2,64,4,128]{4,3,2,1,0:T(4,128)} all-to-all(f32[8,2,64,4,128]{4,3,2,1,0:T(4,128)S(1)} %bitcast.152), channel_id=1, replica_groups=mesh['dh'=2,'dl'=8,'lat'=2] {'dl'}, dimensions={0} | all-to-all | bytes 4194304 | tf_op jit(solution)/shard_map/all_to_all | solution.py:60
  181.2 2.7 reduce_sum.120
  183.8 3.4 all-to-all-start.4
  187.4 7.8 %all-to-all-done.4 = f32[2,64,4,128]{3,2,1,0:T(4,128)S(1)} async-done(((f32[2,64,4,128]{3,2,1,0:T(4,128)}), f32[2,64,4,128]{3,2,1,0:T(4,128)S(1)}, u32[]{:S(2)}, u32[]{:S(2)}) %all-to-all-start.4) | async-done | bytes 262176 | tf_op jit(solution)/shard_map/all_to_all | solution.py:61
  196.8 8.3 %all_to_all.82 = bf16[2,64,4,128]{3,1,2,0:T(8,128)(2,1)S(1)} all-to-all(bf16[2,64,4,128]{3,1,2,0:T(8,128)(2,1)S(1)} %broadcast_in_dim.48), channel_id=1, replica_groups=mesh['dh'=2,'dl'=8,'lat'=2] {'dh'}, dimensions={0} | all-to-all | bytes 262144 | tf_op jit(solution)/shard_map/all_to_all | solution.py:64
  206.3 4.3 all-to-all-start.6
  211.4 11.3 %all-to-all-done.6 = bf16[8,2,64,4,128]{4,2,3,1,0:T(8,128)(2,1)} async-done(((bf16[8,2,64,4,128]{4,2,3,1,0:T(8,128)(2,1)}), bf16[8,2,64,4,128]{4,2,3,1,0:T(8,128)(2,1)}, u32[]{:S(2)}, u32[]{:S(2)}) %all-to-all-start.6) | async-done | bytes 1048608 | tf_op jit(solution)/shard_map/all_to_all | solution.py:65
  224.7 5.4 %all_to_all.83 = bf16[2,16,64,4,128]{4,2,3,1,0:T(8,128)(2,1)S(1)} all-to-all(bf16[2,16,64,4,128]{4,2,3,1,0:T(8,128)(2,1)S(1)} %broadcast_in_dim.51), channel_id=1, replica_groups=mesh['dh'=2,'dl'=8,'lat'=2] {'lat'}, dimensions={0} | all-to-all | bytes 4194304 | tf_op jit(solution)/shard_map/all_to_all | solution.py:69
  230.3 5.9 %bitcast_convert_fusion.1 = bf16[16,1024,128]{2,1,0:T(8,128)(2,1)S(1)} fusion(bf16[16,128,4,128]{3,1,2,0:T(8,128)(2,1)S(1)} %bitcast.167, s32[16,128,4]{1,2,0:T(4,128)S(1)} %copy.288), kind=kOutput, calls=%fused_computation.24 | convolution fusion | flops 2157969408 | bytes 6324224 | tf_op jit(solution)/shard_map/btkq,btkl->bql/dot_general | solution.py:113
  238.2 5.6 %convert_bitcast_fusion = bf16[16,32,32,256]{3,2,0,1:T(8,128)(2,1)} fusion(bf16[16,32,32,128]{3,2,1,0:T(8,128)(2,1)S(1)} %bitcast.145, bf16[32,128,256]{2,1,0:T(8,128)(2,1)S(1)} %all-to-all-done.1), kind=kOutput, calls=%fused_computation.29 | convolution fusion | flops 1077936128 | bytes 14680064 | tf_op jit(solution)/shard_map/borl,olf->borf/dot_general | solution.py:129
  243.8 8.2 %copy.301 = bf16[16,32,32,256]{3,2,1,0:T(8,128)(2,1)} copy(bf16[16,32,32,256]{3,2,0,1:T(8,128)(2,1)} %convert_bitcast_fusion) | data formatting | bytes 16777216 | tf_op jit(solution)/shard_map/convert_element_type | solution.py:130
  252.0 7.1 %add_convert_fusion = (bf16[16,128,256]{2,1,0:T(8,128)(2,1)}, f32[256]{0:T(256)S(1)}, f32[16,128,256]{2,1,0:T(8,128)}) fusion(f32[256]{0:T(256)S(1)} %dynamic_slice.10, bf16[16,132,256]{2,1,0:T(8,128)(2,1)} %copy-done.5, bf16[16,128,1024]{1,2,0:T(8,128)(2,1)S(1)} %copy-done.2, bf16[16,1024,256]{2,1,0:T(8,128)(2,1)} %bitcast.142), kind=kOutput, calls=%fused_computation.51 | convolution fusion | flops 1076363008 | bytes 16779264 | tf_op jit(solution)/shard_map/btq,bqf->btf/dot_general | solution.py:131
  259.1 4.0 convolution_convert_fusion
  263.1 5.7 %fusion.26 = f32[16,32,32,128]{3,2,0,1:T(8,128)} fusion(bf16[16,32,32,256]{3,2,1,0:T(8,128)(2,1)S(1)} %bitcast.138, bf16[32,128,256]{2,1,0:T(8,128)(2,1)S(1)} %all-to-all-done.1), kind=kOutput, calls=%fused_computation.42 | convolution fusion | flops 1073741824 | bytes 18874368 | tf_op jit(solution)/shard_map/borf,olf->borl/dot_general | solution.py:146
  268.8 8.0 %copy.305 = f32[16,32,32,128]{3,2,1,0:T(8,128)} copy(f32[16,32,32,128]{3,2,0,1:T(8,128)} %fusion.26) | data formatting | bytes 16777216 | tf_op jit(solution)/shard_map/borf,olf->borl/transpose | solution.py:146
  276.9 8.9 %reduce-precision_convert_fusion = (bf16[16,1024,128]{2,1,0:T(8,128)(2,1)}, bf16[16,1024,128]{2,1,0:T(8,128)(2,1)}) fusion(f32[16,32,32,128]{3,2,1,0:T(8,128)} %copy.305), kind=kLoop, calls=%fused_computation.12 | loop fusion | flops 8388608 | bytes 16777216 | tf_op jit(solution)/shard_map/convert_element_type | solution.py:32
  285.8 15.6 %fusion.1 = f32[16,128,4,256]{3,1,2,0:T(8,128)} fusion(s32[16,128,4]{1,2,0:T(4,128)S(1)} %copy.288, bf16[16,1024,128]{2,1,0:T(8,128)(2,1)} %get-tuple-element.41, bf16[16,1024,128]{2,1,0:T(8,128)(2,1)} %get-tuple-element.40), kind=kOutput, calls=%fused_computation.2 | convolution fusion | flops 4320133120 | bytes 16809984 | tf_op jit(solution)/shard_map/btkq,bql->btkl/dot_general | solution.py:107
  301.4 4.2 slice_add_fusion
  305.9 8.5 %all_to_all.84 = f32[2,16,64,4,128]{4,2,3,1,0:T(8,128)} all-to-all(f32[2,16,64,4,128]{4,2,3,1,0:T(8,128)S(1)} %bitcast.147), channel_id=1, replica_groups=mesh['dh'=2,'dl'=8,'lat'=2] {'lat'}, dimensions={0} | all-to-all | bytes 8388608 | tf_op jit(solution)/shard_map/all_to_all | solution.py:58
  314.4 2.8 reduce_sum.124
  318.7 29.6 %all_to_all.85 = f32[8,2,64,4,128]{4,3,2,1,0:T(4,128)S(1)} all-to-all(f32[8,2,64,4,128]{4,3,2,1,0:T(4,128)S(1)} %bitcast.154), channel_id=1, replica_groups=mesh['dh'=2,'dl'=8,'lat'=2] {'dl'}, dimensions={0} | all-to-all | bytes 4194304 | tf_op jit(solution)/shard_map/all_to_all | solution.py:60
  348.7 10.2 %all_to_all.86 = f32[2,64,4,128]{3,2,1,0:T(4,128)S(1)} all-to-all(f32[2,64,4,128]{3,2,1,0:T(4,128)S(1)} %reduce_sum.125), channel_id=1, replica_groups=mesh['dh'=2,'dl'=8,'lat'=2] {'dh'}, dimensions={0} | all-to-all | bytes 524288 | tf_op jit(solution)/shard_map/all_to_all | solution.py:61
  361.7 3.4 all-to-all-start.12
  365.3 5.2 %all-to-all-done.12 = bf16[2,64,4,128]{3,1,2,0:T(8,128)(2,1)S(1)} async-done(((bf16[2,64,4,128]{3,1,2,0:T(8,128)(2,1)}), bf16[2,64,4,128]{3,1,2,0:T(8,128)(2,1)S(1)}, u32[]{:S(2)}, u32[]{:S(2)}) %all-to-all-start.12) | async-done | bytes 131104 | tf_op jit(solution)/shard_map/all_to_all | solution.py:64
  371.7 3.6 all-to-all-start.13
  376.5 8.1 %fusion.58 = f32[32,128,256,1]{2,1,0,3:T(8,128)} fusion(bf16[16,32,32,128]{3,2,1,0:T(8,128)(2,1)} %bitcast.146, bf16[16,32,32,256]{3,2,1,0:T(8,128)(2,1)} %bitcast.139), kind=kOutput, calls=%fused_computation.125 | convolution fusion | flops 1073741824 | bytes 16777216 | tf_op jit(solution)/shard_map/borl,borf->olf/dot_general | solution.py:155
  388.0 5.4 %all_to_all.87 = bf16[2,16,64,4,128]{4,2,3,1,0:T(8,128)(2,1)S(1)} all-to-all(bf16[2,16,64,4,128]{4,2,3,1,0:T(8,128)(2,1)S(1)} %broadcast_in_dim.56), channel_id=1, replica_groups=mesh['dh'=2,'dl'=8,'lat'=2] {'lat'}, dimensions={0} | all-to-all | bytes 4194304 | tf_op jit(solution)/shard_map/all_to_all | solution.py:69
  393.4 4.4 all-to-all-start.8
  398.0 5.7 %bitcast_convert_fusion = bf16[16,1024,128]{2,1,0:T(8,128)(2,1)S(1)} fusion(bf16[16,128,4,128]{3,1,2,0:T(8,128)(2,1)S(1)} %bitcast.166, s32[16,128,4]{1,2,0:T(4,128)S(1)} %copy-done.9), kind=kOutput, calls=%fused_computation.23 | convolution fusion | flops 2157969408 | bytes 6324224 | tf_op jit(solution)/shard_map/btkq,btkl->bql/dot_general | solution.py:113
  403.7 5.3 %fusion.20 = bf16[32,128,256]{2,1,0:T(8,128)(2,1)S(1)} fusion(f32[32,128,256,1]{2,1,0,3:T(8,128)S(1)} %copy-done.4, bf16[16,32,32,128]{3,2,1,0:T(8,128)(2,1)S(1)} %bitcast.162, bf16[16,32,32,256]{3,2,1,0:T(8,128)(2,1)} %bitcast.141), kind=kOutput, calls=%fused_computation.35 | convolution fusion | flops 1075838976 | bytes 18874368 | tf_op jit(solution)/shard_map/borl,borf->olf/dot_general | solution.py:156
  410.6 13.1 %all-to-all-done.8 = bf16[16,130,256]{2,1,0:T(8,128)(2,1)S(1)} async-done(((bf16[16,130,256]{2,1,0:T(8,128)(2,1)}), bf16[16,130,256]{2,1,0:T(8,128)(2,1)S(1)}, u32[]{:S(2)}, u32[]{:S(2)}) %all-to-all-start.8) | async-done | bytes 1064992 | tf_op jit(solution)/shard_map/all_to_all | solution.py:140
  423.6 5.4 %all-to-all-start.15 = ((bf16[32,129,256]{2,1,0:T(8,128)(2,1)}), bf16[32,129,256]{2,1,0:T(8,128)(2,1)S(1)}, u32[]{:S(2)}, u32[]{:S(2)}) async-start(bf16[32,129,256]{2,1,0:T(8,128)(2,1)} %pad_maximum_fusion), calls=%async_computation.15 | async-start | bytes 4456448 | tf_op jit(solution)/shard_map/all_to_all | solution.py:161
  435.3 45.5 %all-to-all-done.15 = bf16[32,129,256]{2,1,0:T(8,128)(2,1)S(1)} async-done(((bf16[32,129,256]{2,1,0:T(8,128)(2,1)}), bf16[32,129,256]{2,1,0:T(8,128)(2,1)S(1)}, u32[]{:S(2)}, u32[]{:S(2)}) %all-to-all-start.15) | async-done | bytes 2113568 | tf_op jit(solution)/shard_map/all_to_all | solution.py:161
  482.2 2.7 copy.340
  (106 shorter events, 50.9 us)
Async XLA Ops:
  6.2 34.1 %all-to-all-start = ((bf16[16,132,256]{2,1,0:T(8,128)(2,1)}), bf16[16,132,256]{2,1,0:T(8,128)(2,1)S(1)}, u32[]{:S(2)}, u32[]{:S(2)}) async-start(bf16[16,132,256]{2,1,0:T(8,128)(2,1)} %copy.281), calls=%async_computation | async-start | bytes 2228224 | tf_op jit(solution)/shard_map/all_to_all | solution.py:85
  40.2 1.1 copy-start.5
  41.3 53.8 %all-to-all-start.1 = ((bf16[32,128,256]{2,1,0:T(8,128)(2,1)}), bf16[32,128,256]{2,1,0:T(8,128)(2,1)S(1)}, u32[]{:S(2)}, u32[]{:S(2)}) async-start(bf16[32,128,256]{2,1,0:T(8,128)(2,1)} %bitcast.150), calls=%async_computation.1 | async-start | bytes 4194304 | tf_op jit(solution)/shard_map/all_to_all | solution.py:95
  53.9 231.9 %copy-start.8 = (s32[16,128,4]{1,2,0:T(4,128)}, s32[16,128,4]{1,2,0:T(4,128)S(1)}, u32[]{:S(2)}) copy-start(s32[16,128,4]{1,2,0:T(4,128)S(1)} %copy.288) | copy-start | bytes 98308
  58.5 2.0 copy-start.1
  130.0 4.2 copy-start.14
  151.1 36.2 %copy-start.13 = (s32[128,4]{0,1:T(4,128)S(1)}, s32[128,4]{0,1:T(4,128)}, u32[]{:S(2)}) copy-start(s32[128,4]{0,1:T(4,128)} %param.8) | copy-start | bytes 6148
  183.8 11.3 %all-to-all-start.4 = ((f32[2,64,4,128]{3,2,1,0:T(4,128)}), f32[2,64,4,128]{3,2,1,0:T(4,128)S(1)}, u32[]{:S(2)}, u32[]{:S(2)}) async-start(f32[2,64,4,128]{3,2,1,0:T(4,128)} %reduce_sum.120), calls=%async_computation.4 | async-start | bytes 524288 | tf_op jit(solution)/shard_map/all_to_all | solution.py:61
  187.3 23.3 %copy-start.11 = (s32[128]{0:T(128)}, s32[128]{0:T(128)S(1)}, u32[]{:S(2)}) copy-start(s32[128]{0:T(128)S(1)} %get-tuple-element.55) | copy-start | bytes 1540
  187.3 37.3 %copy-start.12 = (s32[128]{0:T(128)}, s32[128]{0:T(128)S(1)}, u32[]{:S(2)}) copy-start(s32[128]{0:T(128)S(1)} %get-tuple-element.56) | copy-start | bytes 1540
  206.3 16.4 %all-to-all-start.6 = ((bf16[8,2,64,4,128]{4,2,3,1,0:T(8,128)(2,1)}), bf16[8,2,64,4,128]{4,2,3,1,0:T(8,128)(2,1)}, u32[]{:S(2)}, u32[]{:S(2)}) async-start(bf16[8,2,64,4,128]{4,2,3,1,0:T(8,128)(2,1)} %broadcast_in_dim.49), calls=%async_computation.6 | async-start | bytes 2097152 | tf_op jit(solution)/shard_map/all_to_all | solution.py:65
  236.2 2.0 copy-start.3
  243.8 8.2 %copy-start.2 = (bf16[16,128,1024]{1,2,0:T(8,128)(2,1)S(1)}, bf16[16,128,1024]{1,2,0:T(8,128)(2,1)}, u32[]{:S(2)}) copy-start(bf16[16,128,1024]{1,2,0:T(8,128)(2,1)} %copy-done.1) | copy-start | bytes 12582916
  252.0 7.1 %copy-start.6 = (bf16[16,132,256]{2,1,0:T(8,128)(2,1)S(1)}, bf16[16,132,256]{2,1,0:T(8,128)(2,1)}, u32[]{:S(2)}) copy-start(bf16[16,132,256]{2,1,0:T(8,128)(2,1)} %copy-done.5) | copy-start | bytes 3244036
  263.1 5.7 %copy-start = (bf16[16,1024,256]{2,1,0:T(8,128)(2,1)}, bf16[16,1024,256]{2,1,0:T(8,128)(2,1)S(1)}, u32[]{:S(2)}) copy-start(bf16[16,1024,256]{2,1,0:T(8,128)(2,1)S(1)} %convolution_convert_fusion) | copy-start | bytes 25165828
  318.7 46.5 %copy-start.10 = (s32[128,4]{0,1:T(4,128)S(1)}, s32[128,4]{0,1:T(4,128)}, u32[]{:S(2)}) copy-start(s32[128,4]{0,1:T(4,128)} %param.7) | copy-start | bytes 6148
  348.2 27.2 %copy-start.7 = (bf16[16,128,256]{2,1,0:T(8,128)(2,1)S(1)}, bf16[16,128,256]{2,1,0:T(8,128)(2,1)}, u32[]{:S(2)}) copy-start(bf16[16,128,256]{2,1,0:T(8,128)(2,1)} %get-tuple-element.44) | copy-start | bytes 3145732
  361.7 8.7 %all-to-all-start.12 = ((bf16[2,64,4,128]{3,1,2,0:T(8,128)(2,1)}), bf16[2,64,4,128]{3,1,2,0:T(8,128)(2,1)S(1)}, u32[]{:S(2)}, u32[]{:S(2)}) async-start(bf16[2,64,4,128]{3,1,2,0:T(8,128)(2,1)} %broadcast_in_dim.53), calls=%async_computation.12 | async-start | bytes 262144 | tf_op jit(solution)/shard_map/all_to_all | solution.py:64
  371.7 15.5 %all-to-all-start.13 = ((bf16[8,2,64,4,128]{4,2,3,1,0:T(8,128)(2,1)}), bf16[8,2,64,4,128]{4,2,3,1,0:T(8,128)(2,1)S(1)}, u32[]{:S(2)}, u32[]{:S(2)}) async-start(bf16[8,2,64,4,128]{4,2,3,1,0:T(8,128)(2,1)} %broadcast_in_dim.54), calls=%async_computation.13 | async-start | bytes 2097152 | tf_op jit(solution)/shard_map/all_to_all | solution.py:65
  393.4 4.6 copy-start.9
  393.4 30.2 %all-to-all-start.8 = ((bf16[16,130,256]{2,1,0:T(8,128)(2,1)}), bf16[16,130,256]{2,1,0:T(8,128)(2,1)S(1)}, u32[]{:S(2)}, u32[]{:S(2)}) async-start(bf16[16,130,256]{2,1,0:T(8,128)(2,1)} %pad_maximum_fusion.2), calls=%async_computation.8 | async-start | bytes 2228224 | tf_op jit(solution)/shard_map/all_to_all | solution.py:140
  398.0 5.8 %copy-start.4 = (f32[32,128,256,1]{2,1,0,3:T(8,128)S(1)}, f32[32,128,256,1]{2,1,0,3:T(8,128)}, u32[]{:S(2)}) copy-start(f32[32,128,256,1]{2,1,0,3:T(8,128)} %fusion.58) | copy-start | bytes 12582916
  423.6 57.1 %all-to-all-start.15 = ((bf16[32,129,256]{2,1,0:T(8,128)(2,1)}), bf16[32,129,256]{2,1,0:T(8,128)(2,1)S(1)}, u32[]{:S(2)}, u32[]{:S(2)}) async-start(bf16[32,129,256]{2,1,0:T(8,128)(2,1)} %pad_maximum_fusion), calls=%async_computation.15 | async-start | bytes 4456448 | tf_op jit(solution)/shard_map/all_to_all | solution.py:161
